TPU v7x, 256 devices: a whole 4x4x8 slice. The times are simulated.
256 devices in a mesh: pipe: 4 (over x), expert: 64 (over z, y, core).
Axes of the slice: x: 4, y: 4, z: 8, core: 2. Of those that a mesh axis runs over, the one named last changes fastest.
Arguments:
- saved_inputs: bfloat16 [4, 3, 4096, 2048], P('pipe', None, 'expert'), may hold values from -6 to 6
- routes: int32 [4, 3, 4096, 4], P('pipe', None, 'expert'), may hold values from 0 to 63, as said below
- gates: float32 [4, 3, 4096, 4], P('pipe', None, 'expert'), may hold values from 0.1 to 0.6
- w_in: bfloat16 [4, 64, 2048, 768], P('pipe', 'expert'), may hold values from -0.125 to 0.125
- w_out: bfloat16 [4, 64, 768, 2048], P('pipe', 'expert'), may hold values from -0.21875 to 0.21875
- cotangent: bfloat16 [3, 4096, 2048], P(None, 'expert', 'pipe'), may hold values from -6 to 6
Outputs:
- grad_in: bfloat16 [3, 4096, 2048], P(None, 'expert', 'pipe')
- grad_w_in: bfloat16 [4, 64, 2048, 768], P('pipe', 'expert')
- grad_w_out: bfloat16 [4, 64, 768, 2048], P('pipe', 'expert')
Inputs may be any that keep to these rules, and one draw needn't show every extreme that they name: `routes`: each token names 4 different experts. Among the 64 tokens of one device's micro-batch (aligned blocks of the token dimension) no expert is named by more than 4 tokens. In every micro-batch of every section some expert is named by exactly 4 tokens in every such block.
All inputs are finite; a program needn't handle non-finite values.
Results may differ from a plain program's by a relative error of at most 0.02.
Values may be sent and summed in bfloat16 or wider, within the bound.
No kernel may reach another device: no remote copies, remote signals or barrier semaphores. Data moves between devices by JAX's collectives and lax.ppermute only.
A program may use at most 128 MiB of HBM per device.

v0:
```python
import jax
import jax.numpy as jnp
from jax import lax
from jax.sharding import PartitionSpec as P


def shifted(value, axis, steps):
    count = lax.axis_size(axis)
    first, last = (max(0, -steps), min(count, count - steps))
    return lax.ppermute(value, axis, [(source, source + steps) for source in range(first, last)])


def silu_slope(preactivation):
    logistic = jax.nn.sigmoid(preactivation)
    return logistic * (1.0 + preactivation * (1.0 - logistic))


def placement_tables(routes_micro, expert_count, capacity):
    flat_routes = routes_micro.reshape(-1)
    expert_ids = jnp.arange(expert_count, dtype=jnp.int32)
    one_hot = (flat_routes[:, None] == expert_ids[None, :]).astype(jnp.int32)
    ranks = jnp.sum((jnp.cumsum(one_hot, axis=0) - 1) * one_hot, axis=1)
    slots = flat_routes * capacity + ranks
    slot_ids = jnp.arange(expert_count * capacity, dtype=jnp.int32)
    route_table = (slot_ids[:, None] == slots[None, :]).astype(jnp.bfloat16)
    slot_grid = slots.reshape(routes_micro.shape[0], routes_micro.shape[1])
    token_table = jnp.zeros((expert_count * capacity, routes_micro.shape[0]), jnp.float32)
    for route_no in range(routes_micro.shape[1]):
        token_table = token_table + (slot_ids[:, None] == slot_grid[:, route_no][None, :]).astype(
            jnp.float32
        )
    return (route_table, token_table.astype(jnp.bfloat16))


def on_device(saved_inputs, routes, gates, w_in, w_out, cotangent):
    section_count = lax.axis_size("pipe")
    owners = lax.axis_size("expert")
    section_id = lax.axis_index("pipe")
    micro_count = saved_inputs.shape[1]
    tokens_dev = saved_inputs.shape[2]
    model_width = saved_inputs.shape[3]
    route_count = routes.shape[3]
    local_count = w_in.shape[1]
    expert_count = local_count * owners
    capacity = max(2, tokens_dev * route_count * 6 // (5 * expert_count))
    tick_count = section_count + micro_count - 1
    first_tick = section_count - 1 - section_id
    first_weights = w_in[0, 0]
    second_weights = w_out[0, 0]
    inputs_dev = saved_inputs[0]
    upstream = lax.all_gather(cotangent, "pipe", axis=2, tiled=True)
    pairs = [
        placement_tables(routes[0, micro_no], expert_count, capacity)
        for micro_no in range(micro_count)
    ]
    tables = jnp.stack([pair[0] for pair in pairs])
    token_route_tables = jnp.stack([pair[1] for pair in pairs])
    incoming = jnp.zeros((tokens_dev, model_width), jnp.bfloat16)
    kept_inputs, kept_grads, kept_pre, kept_hidden, kept_out = ([], [], [], [], [])
    for tick_no in range(tick_count):
        micro_id = jnp.clip(tick_no - first_tick, 0, micro_count - 1)
        grad_now = jnp.where(section_id == section_count - 1, upstream[micro_id], incoming)
        gate_now = gates[0, micro_id]
        gate_scaled_rows = (gate_now[:, :, None] * grad_now.astype(jnp.float32)[:, None, :]).astype(
            jnp.bfloat16
        )
        gate_scaled_rows = gate_scaled_rows.reshape(tokens_dev * route_count, model_width)
        gradient_slot_buffer = jnp.dot(
            tables[micro_id], gate_scaled_rows, preferred_element_type=jnp.float32
        ).astype(jnp.bfloat16)
        input_slots = jnp.dot(
            token_route_tables[micro_id], inputs_dev[micro_id], preferred_element_type=jnp.float32
        ).astype(jnp.bfloat16)
        input_recv, grad_recv = (
            lax.all_to_all(input_slots, "expert", split_axis=0, concat_axis=0, tiled=True),
            lax.all_to_all(gradient_slot_buffer, "expert", split_axis=0, concat_axis=0, tiled=True),
        )
        kept_inputs.append(input_recv)
        preactivation = jnp.dot(input_recv, first_weights, preferred_element_type=jnp.float32)
        hidden_grad = lax.dot_general(
            grad_recv, second_weights, (((1,), (1,)), ((), ())), preferred_element_type=jnp.float32
        )
        pre_grad = (hidden_grad * silu_slope(preactivation)).astype(jnp.bfloat16)
        hidden = jax.nn.silu(preactivation).astype(jnp.bfloat16)
        row_grads = lax.dot_general(
            pre_grad, first_weights, (((1,), (1,)), ((), ())), preferred_element_type=jnp.float32
        ).astype(jnp.bfloat16)
        returned = lax.all_to_all(row_grads, "expert", split_axis=0, concat_axis=0, tiled=True)
        summed = lax.dot_general(
            token_route_tables[micro_id],
            returned,
            (((0,), (0,)), ((), ())),
            preferred_element_type=jnp.float32,
        )
        grad_out = (grad_now.astype(jnp.float32) + summed).astype(jnp.bfloat16)
        kept_grads.append(grad_recv)
        kept_pre.append(pre_grad)
        kept_hidden.append(hidden)
        kept_out.append(grad_out)
        if tick_no + 1 < tick_count:
            incoming = shifted(grad_out, "pipe", -1)

    def valid_part(kept):
        return lax.dynamic_slice_in_dim(jnp.stack(kept), first_tick, micro_count, 0)

    gradient_ready_flags = valid_part(kept_grads)
    preactivation_ready = valid_part(kept_pre)
    hidden_ready_flags = valid_part(kept_hidden)
    input_ready_flags = valid_part(kept_inputs)
    first_grad = jnp.einsum(
        "qpz,qpy->zy", input_ready_flags, preactivation_ready, preferred_element_type=jnp.float32
    ).astype(jnp.bfloat16)
    second_grad = jnp.einsum(
        "cgk,cgs->ks", hidden_ready_flags, gradient_ready_flags, preferred_element_type=jnp.float32
    ).astype(jnp.bfloat16)
    final_rows = valid_part(kept_out)
    final_term = jnp.where(section_id == 0, final_rows.astype(jnp.float32), 0.0)
    grad_in = lax.psum_scatter(
        final_term.astype(jnp.bfloat16), "pipe", scatter_dimension=2, tiled=True
    )
    return (grad_in, first_grad[None, None], second_grad[None, None])


def solution(mesh):
    return jax.shard_map(
        on_device,
        mesh=mesh,
        in_specs=(
            P("pipe", None, "expert", None),
            P("pipe", None, "expert", None),
            P("pipe", None, "expert", None),
            P("pipe", "expert", None, None),
            P("pipe", "expert", None, None),
            P(None, "expert", "pipe"),
        ),
        out_specs=(
            P(None, "expert", "pipe"),
            P("pipe", "expert", None, None),
            P("pipe", "expert", None, None),
        ),
        check_vma=False,
    )
```

profile of v0, /device:TPU:8, one launch (start us, length us, event | category | flops | bytes accessed | tf_op | source)
XLA Modules:
  0.0 788.6 jit_solution(8374065733947151300)
XLA Ops:
  20.3 12.3 %all-to-all-start.1 = ((bf16[64,4,2048]{2,1,0:T(4,128)(2,1)}), bf16[64,4,2048]{2,1,0:T(4,128)(2,1)}, u32[]{:S(2)}, u32[]{:S(2)}) async-start(bf16[64,4,2048]{2,1,0:T(4,128)(2,1)} %all_to_all.147), calls=%async_computation.1 | async-start | bytes 2097152 | tf_op jit(solution)/shard_map/all_to_all | solution.py:75
  32.6 13.9 %all_gather.3 = bf16[3,64,2048]{2,1,0:T(8,128)(2,1)S(1)} all-gather(bf16[3,64,512]{2,1,0:T(8,128)(2,1)S(1)} %copy-done.12), channel_id=1, replica_groups=mesh['pipe'=4,'expert'=64] {'pipe'}, dimensions={2}, use_global_device_ids=true | all-gather | bytes 983040 | tf_op jit(solution)/shard_map/all_gather | solution.py:51
  61.3 9.7 %all-to-all-start = ((bf16[64,4,2048]{2,1,0:T(4,128)(2,1)}), bf16[64,4,2048]{2,1,0:T(4,128)(2,1)}, u32[]{:S(2)}, u32[]{:S(2)}) async-start(bf16[64,4,2048]{2,1,0:T(4,128)(2,1)} %all_to_all.144), calls=%async_computation | async-start | bytes 2097152 | tf_op jit(solution)/shard_map/all_to_all | solution.py:76
  76.3 23.3 %all-to-all-done = bf16[64,4,2048]{2,1,0:T(4,128)(2,1)} async-done(((bf16[64,4,2048]{2,1,0:T(4,128)(2,1)}), bf16[64,4,2048]{2,1,0:T(4,128)(2,1)}, u32[]{:S(2)}, u32[]{:S(2)}) %all-to-all-start) | async-done | bytes 1048608 | tf_op jit(solution)/shard_map/all_to_all | solution.py:76
  110.3 5.9 all-to-all-start.2
  120.8 24.1 %all-to-all-done.2 = bf16[64,4,2048]{2,1,0:T(4,128)(2,1)} async-done(((bf16[64,4,2048]{2,1,0:T(4,128)(2,1)}), bf16[64,4,2048]{2,1,0:T(4,128)(2,1)}, u32[]{:S(2)}, u32[]{:S(2)}) %all-to-all-start.2) | async-done | bytes 1048608 | tf_op jit(solution)/shard_map/all_to_all | solution.py:88
  144.9 5.9 all-to-all-start.4
  157.3 8.5 %collective-permute-done = bf16[64,2048]{1,0:T(8,128)(2,1)} collective-permute-done((bf16[64,2048]{1,0:T(8,128)(2,1)}, bf16[64,2048]{1,0:T(8,128)(2,1)}, u32[]{:S(2)}, u32[]{:S(2)}) %collective-permute-start) | collective-permute-done | bytes 262176 | tf_op jit(solution)/shard_map/ppermute | solution.py:10
  179.4 8.0 %all-to-all-start.3 = ((bf16[64,4,2048]{2,1,0:T(4,128)(2,1)}), bf16[64,4,2048]{2,1,0:T(4,128)(2,1)}, u32[]{:S(2)}, u32[]{:S(2)}) async-start(bf16[64,4,2048]{2,1,0:T(4,128)(2,1)} %all_to_all.153), calls=%async_computation.3 | async-start | bytes 2097152 | tf_op jit(solution)/shard_map/all_to_all | solution.py:76
  192.9 23.3 %all-to-all-done.3 = bf16[64,4,2048]{2,1,0:T(4,128)(2,1)} async-done(((bf16[64,4,2048]{2,1,0:T(4,128)(2,1)}), bf16[64,4,2048]{2,1,0:T(4,128)(2,1)}, u32[]{:S(2)}, u32[]{:S(2)}) %all-to-all-start.3) | async-done | bytes 1048608 | tf_op jit(solution)/shard_map/all_to_all | solution.py:76
  226.8 5.9 all-to-all-start.5
  237.3 24.1 %all-to-all-done.5 = bf16[64,4,2048]{2,1,0:T(4,128)(2,1)} async-done(((bf16[64,4,2048]{2,1,0:T(4,128)(2,1)}), bf16[64,4,2048]{2,1,0:T(4,128)(2,1)}, u32[]{:S(2)}, u32[]{:S(2)}) %all-to-all-start.5) | async-done | bytes 1048608 | tf_op jit(solution)/shard_map/all_to_all | solution.py:88
  261.4 5.9 all-to-all-start.7
  273.9 8.5 %collective-permute-done.1 = bf16[64,2048]{1,0:T(8,128)(2,1)} collective-permute-done((bf16[64,2048]{1,0:T(8,128)(2,1)}, bf16[64,2048]{1,0:T(8,128)(2,1)}, u32[]{:S(2)}, u32[]{:S(2)}) %collective-permute-start.1) | collective-permute-done | bytes 262176 | tf_op jit(solution)/shard_map/ppermute | solution.py:10
  295.9 8.7 %all-to-all-start.6 = ((bf16[64,4,2048]{2,1,0:T(4,128)(2,1)}), bf16[64,4,2048]{2,1,0:T(4,128)(2,1)}, u32[]{:S(2)}, u32[]{:S(2)}) async-start(bf16[64,4,2048]{2,1,0:T(4,128)(2,1)} %all_to_all.162), calls=%async_computation.6 | async-start | bytes 2097152 | tf_op jit(solution)/shard_map/all_to_all | solution.py:76
  310.0 23.1 %all-to-all-done.6 = bf16[64,4,2048]{2,1,0:T(4,128)(2,1)} async-done(((bf16[64,4,2048]{2,1,0:T(4,128)(2,1)}), bf16[64,4,2048]{2,1,0:T(4,128)(2,1)}, u32[]{:S(2)}, u32[]{:S(2)}) %all-to-all-start.6) | async-done | bytes 1048608 | tf_op jit(solution)/shard_map/all_to_all | solution.py:76
  343.8 5.9 all-to-all-start.8
  354.4 24.0 %all-to-all-done.8 = bf16[64,4,2048]{2,1,0:T(4,128)(2,1)} async-done(((bf16[64,4,2048]{2,1,0:T(4,128)(2,1)}), bf16[64,4,2048]{2,1,0:T(4,128)(2,1)}, u32[]{:S(2)}, u32[]{:S(2)}) %all-to-all-start.8) | async-done | bytes 1048608 | tf_op jit(solution)/shard_map/all_to_all | solution.py:88
  390.9 8.5 %collective-permute-done.2 = bf16[64,2048]{1,0:T(8,128)(2,1)} collective-permute-done((bf16[64,2048]{1,0:T(8,128)(2,1)}, bf16[64,2048]{1,0:T(8,128)(2,1)}, u32[]{:S(2)}, u32[]{:S(2)}) %collective-permute-start.2) | collective-permute-done | bytes 262176 | tf_op jit(solution)/shard_map/ppermute | solution.py:10
  412.9 8.2 %all-to-all-start.9 = ((bf16[64,4,2048]{2,1,0:T(4,128)(2,1)}), bf16[64,4,2048]{2,1,0:T(4,128)(2,1)}, u32[]{:S(2)}, u32[]{:S(2)}) async-start(bf16[64,4,2048]{2,1,0:T(4,128)(2,1)} %all_to_all.171), calls=%async_computation.9 | async-start | bytes 2097152 | tf_op jit(solution)/shard_map/all_to_all | solution.py:76
  426.5 23.3 %all-to-all-done.9 = bf16[64,4,2048]{2,1,0:T(4,128)(2,1)} async-done(((bf16[64,4,2048]{2,1,0:T(4,128)(2,1)}), bf16[64,4,2048]{2,1,0:T(4,128)(2,1)}, u32[]{:S(2)}, u32[]{:S(2)}) %all-to-all-start.9) | async-done | bytes 1048608 | tf_op jit(solution)/shard_map/all_to_all | solution.py:76
  471.1 24.0 %all-to-all-done.11 = bf16[64,4,2048]{2,1,0:T(4,128)(2,1)} async-done(((bf16[64,4,2048]{2,1,0:T(4,128)(2,1)}), bf16[64,4,2048]{2,1,0:T(4,128)(2,1)}, u32[]{:S(2)}, u32[]{:S(2)}) %all-to-all-start.11) | async-done | bytes 1048608 | tf_op jit(solution)/shard_map/all_to_all | solution.py:88
  507.6 8.5 %collective-permute-done.3 = bf16[64,2048]{1,0:T(8,128)(2,1)} collective-permute-done((bf16[64,2048]{1,0:T(8,128)(2,1)}, bf16[64,2048]{1,0:T(8,128)(2,1)}, u32[]{:S(2)}, u32[]{:S(2)}) %collective-permute-start.3) | collective-permute-done | bytes 262176 | tf_op jit(solution)/shard_map/ppermute | solution.py:10
  529.6 8.3 %all-to-all-start.12 = ((bf16[64,4,2048]{2,1,0:T(4,128)(2,1)}), bf16[64,4,2048]{2,1,0:T(4,128)(2,1)}, u32[]{:S(2)}, u32[]{:S(2)}) async-start(bf16[64,4,2048]{2,1,0:T(4,128)(2,1)} %all_to_all.180), calls=%async_computation.12 | async-start | bytes 2097152 | tf_op jit(solution)/shard_map/all_to_all | solution.py:76
  543.4 23.3 %all-to-all-done.12 = bf16[64,4,2048]{2,1,0:T(4,128)(2,1)} async-done(((bf16[64,4,2048]{2,1,0:T(4,128)(2,1)}), bf16[64,4,2048]{2,1,0:T(4,128)(2,1)}, u32[]{:S(2)}, u32[]{:S(2)}) %all-to-all-start.12) | async-done | bytes 1048608 | tf_op jit(solution)/shard_map/all_to_all | solution.py:76
  577.3 5.9 all-to-all-start.14
  587.8 24.0 %all-to-all-done.14 = bf16[64,4,2048]{2,1,0:T(4,128)(2,1)} async-done(((bf16[64,4,2048]{2,1,0:T(4,128)(2,1)}), bf16[64,4,2048]{2,1,0:T(4,128)(2,1)}, u32[]{:S(2)}, u32[]{:S(2)}) %all-to-all-start.14) | async-done | bytes 1048608 | tf_op jit(solution)/shard_map/all_to_all | solution.py:88
  624.6 8.3 %collective-permute-done.4 = bf16[64,2048]{1,0:T(8,128)(2,1)} collective-permute-done((bf16[64,2048]{1,0:T(8,128)(2,1)}, bf16[64,2048]{1,0:T(8,128)(2,1)}, u32[]{:S(2)}, u32[]{:S(2)}) %collective-permute-start.4) | collective-permute-done | bytes 262176 | tf_op jit(solution)/shard_map/ppermute | solution.py:10
  646.4 8.1 %all-to-all-start.15 = ((bf16[64,4,2048]{2,1,0:T(4,128)(2,1)}), bf16[64,4,2048]{2,1,0:T(4,128)(2,1)}, u32[]{:S(2)}, u32[]{:S(2)}) async-start(bf16[64,4,2048]{2,1,0:T(4,128)(2,1)} %all_to_all.189), calls=%async_computation.15 | async-start | bytes 2097152 | tf_op jit(solution)/shard_map/all_to_all | solution.py:76
  660.0 23.3 %all-to-all-done.15 = bf16[64,4,2048]{2,1,0:T(4,128)(2,1)} async-done(((bf16[64,4,2048]{2,1,0:T(4,128)(2,1)}), bf16[64,4,2048]{2,1,0:T(4,128)(2,1)}, u32[]{:S(2)}, u32[]{:S(2)}) %all-to-all-start.15) | async-done | bytes 1048608 | tf_op jit(solution)/shard_map/all_to_all | solution.py:76
  768.4 6.8 fusion.41
  775.1 6.2 fusion.38
  (242 shorter events, 345.9 us)
Async XLA Ops:
  7.2 66.0 %copy-start = (bf16[1,1,2048,768]{3,2,1,0:T(8,128)(2,1)S(1)}, bf16[1,1,2048,768]{3,2,1,0:T(8,128)(2,1)}, u32[]{:S(2)}) copy-start(bf16[1,1,2048,768]{3,2,1,0:T(8,128)(2,1)} %param.9) | copy-start | bytes 9437188
  14.7 17.9 %copy-start.12 = (bf16[3,64,512]{2,1,0:T(8,128)(2,1)S(1)}, bf16[3,64,512]{2,1,0:T(8,128)(2,1)}, u32[]{:S(2)}) copy-start(bf16[3,64,512]{2,1,0:T(8,128)(2,1)} %param.11) | copy-start | bytes 589828
  18.0 30.2 %copy-start.13 = (f32[1,3,64,4]{2,3,1,0:T(4,128)S(1)}, f32[1,3,64,4]{2,3,1,0:T(4,128)}, u32[]{:S(2)}) copy-start(f32[1,3,64,4]{2,3,1,0:T(4,128)} %param.8) | copy-start | bytes 9220
  20.3 41.0 %all-to-all-start.1 = ((bf16[64,4,2048]{2,1,0:T(4,128)(2,1)}), bf16[64,4,2048]{2,1,0:T(4,128)(2,1)}, u32[]{:S(2)}, u32[]{:S(2)}) async-start(bf16[64,4,2048]{2,1,0:T(4,128)(2,1)} %all_to_all.147), calls=%async_computation.1 | async-start | bytes 2097152 | tf_op jit(solution)/shard_map/all_to_all | solution.py:75
  61.3 38.4 %all-to-all-start = ((bf16[64,4,2048]{2,1,0:T(4,128)(2,1)}), bf16[64,4,2048]{2,1,0:T(4,128)(2,1)}, u32[]{:S(2)}, u32[]{:S(2)}) async-start(bf16[64,4,2048]{2,1,0:T(4,128)(2,1)} %all_to_all.144), calls=%async_computation | async-start | bytes 2097152 | tf_op jit(solution)/shard_map/all_to_all | solution.py:76
  110.3 34.6 %all-to-all-start.2 = ((bf16[64,4,2048]{2,1,0:T(4,128)(2,1)}), bf16[64,4,2048]{2,1,0:T(4,128)(2,1)}, u32[]{:S(2)}, u32[]{:S(2)}) async-start(bf16[64,4,2048]{2,1,0:T(4,128)(2,1)} %all_to_all.150), calls=%async_computation.2 | async-start | bytes 2097152 | tf_op jit(solution)/shard_map/all_to_all | solution.py:88
  120.8 35.8 %copy-start.22 = (f32[64,4]{0,1:T(4,128)S(1)}, f32[64,4]{0,1:T(4,128)}, u32[]{:S(2)}) copy-start(f32[64,4]{0,1:T(4,128)} %get-tuple-element.18) | copy-start | bytes 3076
  144.9 34.6 %all-to-all-start.4 = ((bf16[64,4,2048]{2,1,0:T(4,128)(2,1)}), bf16[64,4,2048]{2,1,0:T(4,128)(2,1)}, u32[]{:S(2)}, u32[]{:S(2)}) async-start(bf16[64,4,2048]{2,1,0:T(4,128)(2,1)} %all_to_all.156), calls=%async_computation.4 | async-start | bytes 2097152 | tf_op jit(solution)/shard_map/all_to_all | solution.py:75
  155.3 10.5 %collective-permute-start = (bf16[64,2048]{1,0:T(8,128)(2,1)}, bf16[64,2048]{1,0:T(8,128)(2,1)}, u32[]{:S(2)}, u32[]{:S(2)}) collective-permute-start(bf16[64,2048]{1,0:T(8,128)(2,1)} %get-tuple-element.25), channel_id=1, source_target_pairs={{64,0},{128,64},{192,128},{65,1},{129,65},{193,129},{66,2},{130,66... | collective-permute-start | bytes 786440 | tf_op jit(solution)/shard_map/ppermute | solution.py:10
  179.4 36.7 %all-to-all-start.3 = ((bf16[64,4,2048]{2,1,0:T(4,128)(2,1)}), bf16[64,4,2048]{2,1,0:T(4,128)(2,1)}, u32[]{:S(2)}, u32[]{:S(2)}) async-start(bf16[64,4,2048]{2,1,0:T(4,128)(2,1)} %all_to_all.153), calls=%async_computation.3 | async-start | bytes 2097152 | tf_op jit(solution)/shard_map/all_to_all | solution.py:76
  226.8 34.6 %all-to-all-start.5 = ((bf16[64,4,2048]{2,1,0:T(4,128)(2,1)}), bf16[64,4,2048]{2,1,0:T(4,128)(2,1)}, u32[]{:S(2)}, u32[]{:S(2)}) async-start(bf16[64,4,2048]{2,1,0:T(4,128)(2,1)} %all_to_all.159), calls=%async_computation.5 | async-start | bytes 2097152 | tf_op jit(solution)/shard_map/all_to_all | solution.py:88
  237.3 35.9 %copy-start.21 = (f32[64,4]{0,1:T(4,128)S(1)}, f32[64,4]{0,1:T(4,128)}, u32[]{:S(2)}) copy-start(f32[64,4]{0,1:T(4,128)} %get-tuple-element.17) | copy-start | bytes 3076
  261.4 34.6 %all-to-all-start.7 = ((bf16[64,4,2048]{2,1,0:T(4,128)(2,1)}), bf16[64,4,2048]{2,1,0:T(4,128)(2,1)}, u32[]{:S(2)}, u32[]{:S(2)}) async-start(bf16[64,4,2048]{2,1,0:T(4,128)(2,1)} %all_to_all.165), calls=%async_computation.7 | async-start | bytes 2097152 | tf_op jit(solution)/shard_map/all_to_all | solution.py:75
  271.9 10.5 %collective-permute-start.1 = (bf16[64,2048]{1,0:T(8,128)(2,1)}, bf16[64,2048]{1,0:T(8,128)(2,1)}, u32[]{:S(2)}, u32[]{:S(2)}) collective-permute-start(bf16[64,2048]{1,0:T(8,128)(2,1)} %get-tuple-element.27), channel_id=1, source_target_pairs={{64,0},{128,64},{192,128},{65,1},{129,65},{193,129},{66,2},{130,66... | collective-permute-start | bytes 786440 | tf_op jit(solution)/shard_map/ppermute | solution.py:10
  295.9 37.2 %all-to-all-start.6 = ((bf16[64,4,2048]{2,1,0:T(4,128)(2,1)}), bf16[64,4,2048]{2,1,0:T(4,128)(2,1)}, u32[]{:S(2)}, u32[]{:S(2)}) async-start(bf16[64,4,2048]{2,1,0:T(4,128)(2,1)} %all_to_all.162), calls=%async_computation.6 | async-start | bytes 2097152 | tf_op jit(solution)/shard_map/all_to_all | solution.py:76
  343.8 34.6 %all-to-all-start.8 = ((bf16[64,4,2048]{2,1,0:T(4,128)(2,1)}), bf16[64,4,2048]{2,1,0:T(4,128)(2,1)}, u32[]{:S(2)}, u32[]{:S(2)}) async-start(bf16[64,4,2048]{2,1,0:T(4,128)(2,1)} %all_to_all.168), calls=%async_computation.8 | async-start | bytes 2097152 | tf_op jit(solution)/shard_map/all_to_all | solution.py:88
  354.4 35.9 %copy-start.20 = (f32[64,4]{0,1:T(4,128)S(1)}, f32[64,4]{0,1:T(4,128)}, u32[]{:S(2)}) copy-start(f32[64,4]{0,1:T(4,128)} %get-tuple-element.16) | copy-start | bytes 3076
  378.4 34.6 %all-to-all-start.10 = ((bf16[64,4,2048]{2,1,0:T(4,128)(2,1)}), bf16[64,4,2048]{2,1,0:T(4,128)(2,1)}, u32[]{:S(2)}, u32[]{:S(2)}) async-start(bf16[64,4,2048]{2,1,0:T(4,128)(2,1)} %all_to_all.174), calls=%async_computation.10 | async-start | bytes 2097152 | tf_op jit(solution)/shard_map/all_to_all | solution.py:75
  388.9 10.5 %collective-permute-start.2 = (bf16[64,2048]{1,0:T(8,128)(2,1)}, bf16[64,2048]{1,0:T(8,128)(2,1)}, u32[]{:S(2)}, u32[]{:S(2)}) collective-permute-start(bf16[64,2048]{1,0:T(8,128)(2,1)} %get-tuple-element.29), channel_id=1, source_target_pairs={{64,0},{128,64},{192,128},{65,1},{129,65},{193,129},{66,2},{130,66... | collective-permute-start | bytes 786440 | tf_op jit(solution)/shard_map/ppermute | solution.py:10
  412.9 36.9 %all-to-all-start.9 = ((bf16[64,4,2048]{2,1,0:T(4,128)(2,1)}), bf16[64,4,2048]{2,1,0:T(4,128)(2,1)}, u32[]{:S(2)}, u32[]{:S(2)}) async-start(bf16[64,4,2048]{2,1,0:T(4,128)(2,1)} %all_to_all.171), calls=%async_computation.9 | async-start | bytes 2097152 | tf_op jit(solution)/shard_map/all_to_all | solution.py:76
  460.5 34.5 %all-to-all-start.11 = ((bf16[64,4,2048]{2,1,0:T(4,128)(2,1)}), bf16[64,4,2048]{2,1,0:T(4,128)(2,1)}, u32[]{:S(2)}, u32[]{:S(2)}) async-start(bf16[64,4,2048]{2,1,0:T(4,128)(2,1)} %all_to_all.177), calls=%async_computation.11 | async-start | bytes 2097152 | tf_op jit(solution)/shard_map/all_to_all | solution.py:88
  471.1 35.9 %copy-start.19 = (f32[64,4]{0,1:T(4,128)S(1)}, f32[64,4]{0,1:T(4,128)}, u32[]{:S(2)}) copy-start(f32[64,4]{0,1:T(4,128)} %get-tuple-element.20) | copy-start | bytes 3076
  495.1 34.6 %all-to-all-start.13 = ((bf16[64,4,2048]{2,1,0:T(4,128)(2,1)}), bf16[64,4,2048]{2,1,0:T(4,128)(2,1)}, u32[]{:S(2)}, u32[]{:S(2)}) async-start(bf16[64,4,2048]{2,1,0:T(4,128)(2,1)} %all_to_all.183), calls=%async_computation.13 | async-start | bytes 2097152 | tf_op jit(solution)/shard_map/all_to_all | solution.py:75
  505.6 10.5 %collective-permute-start.3 = (bf16[64,2048]{1,0:T(8,128)(2,1)}, bf16[64,2048]{1,0:T(8,128)(2,1)}, u32[]{:S(2)}, u32[]{:S(2)}) collective-permute-start(bf16[64,2048]{1,0:T(8,128)(2,1)} %get-tuple-element.31), channel_id=1, source_target_pairs={{64,0},{128,64},{192,128},{65,1},{129,65},{193,129},{66,2},{130,66... | collective-permute-start | bytes 786440 | tf_op jit(solution)/shard_map/ppermute | solution.py:10
  529.6 37.0 %all-to-all-start.12 = ((bf16[64,4,2048]{2,1,0:T(4,128)(2,1)}), bf16[64,4,2048]{2,1,0:T(4,128)(2,1)}, u32[]{:S(2)}, u32[]{:S(2)}) async-start(bf16[64,4,2048]{2,1,0:T(4,128)(2,1)} %all_to_all.180), calls=%async_computation.12 | async-start | bytes 2097152 | tf_op jit(solution)/shard_map/all_to_all | solution.py:76
  577.3 34.6 %all-to-all-start.14 = ((bf16[64,4,2048]{2,1,0:T(4,128)(2,1)}), bf16[64,4,2048]{2,1,0:T(4,128)(2,1)}, u32[]{:S(2)}, u32[]{:S(2)}) async-start(bf16[64,4,2048]{2,1,0:T(4,128)(2,1)} %all_to_all.186), calls=%async_computation.14 | async-start | bytes 2097152 | tf_op jit(solution)/shard_map/all_to_all | solution.py:88
  587.8 36.0 %copy-start.18 = (f32[64,4]{0,1:T(4,128)S(1)}, f32[64,4]{0,1:T(4,128)}, u32[]{:S(2)}) copy-start(f32[64,4]{0,1:T(4,128)} %get-tuple-element.15) | copy-start | bytes 3076
  611.9 34.6 %all-to-all-start.16 = ((bf16[64,4,2048]{2,1,0:T(4,128)(2,1)}), bf16[64,4,2048]{2,1,0:T(4,128)(2,1)}, u32[]{:S(2)}, u32[]{:S(2)}) async-start(bf16[64,4,2048]{2,1,0:T(4,128)(2,1)} %all_to_all.192), calls=%async_computation.16 | async-start | bytes 2097152 | tf_op jit(solution)/shard_map/all_to_all | solution.py:75
  622.4 10.5 %collective-permute-start.4 = (bf16[64,2048]{1,0:T(8,128)(2,1)}, bf16[64,2048]{1,0:T(8,128)(2,1)}, u32[]{:S(2)}, u32[]{:S(2)}) collective-permute-start(bf16[64,2048]{1,0:T(8,128)(2,1)} %get-tuple-element.33), channel_id=1, source_target_pairs={{64,0},{128,64},{192,128},{65,1},{129,65},{193,129},{66,2},{130,66... | collective-permute-start | bytes 786440 | tf_op jit(solution)/shard_map/ppermute | solution.py:10
  646.4 36.8 %all-to-all-start.15 = ((bf16[64,4,2048]{2,1,0:T(4,128)(2,1)}), bf16[64,4,2048]{2,1,0:T(4,128)(2,1)}, u32[]{:S(2)}, u32[]{:S(2)}) async-start(bf16[64,4,2048]{2,1,0:T(4,128)(2,1)} %all_to_all.189), calls=%async_computation.15 | async-start | bytes 2097152 | tf_op jit(solution)/shard_map/all_to_all | solution.py:76
  694.0 51.9 %all-to-all-start.17 = ((bf16[64,4,2048]{2,1,0:T(4,128)(2,1)}), bf16[64,4,2048]{2,1,0:T(4,128)(2,1)}, u32[]{:S(2)}, u32[]{:S(2)}) async-start(bf16[64,4,2048]{2,1,0:T(4,128)(2,1)} %all_to_all.195), calls=%async_computation.17 | async-start | bytes 2097152 | tf_op jit(solution)/shard_map/all_to_all | solution.py:88
  699.9 81.5 %reduce-scatter.2.cloned.1.call-start = ((), (), s32[]{:S(2)}) async-start(), calls=%async_computation.19 | async-start | bytes 983040 | tf_op jit(solution)/shard_map/reduce_scatter | solution.py:118
  (16 other events, 40.3 us)
Sparse Core Ops, SparseCore 0:
  752.8 25.1 reduce-scatter.1
where the time goes:
time: 803 us; the launch traced here: 789 us
  waiting for transfers between devices  315 us (39%)
  local copies, waits for them, and re-layouts  168 us (21%)
  starting transfers between devices  135 us (17%)
  matrix products  115 us (14%)
  other arithmetic  27.1 us (3%)
  between operations  15.1 us (2%)
  blocking collectives  13.9 us (2%)
    all_to_all x6, waiting for transfers between devices, on_device(): lax.all_to_all(gradient_slot_buffer, 'expert', split_axis=0, concat_axis=...  140 us
    all_to_all x6, waiting for transfers between devices, on_device(): lax.all_to_all(row_grads, 'expert', split_axis=0, concat_axis=0, tiled=True)  120 us
    all_to_all x6, starting transfers between devices, on_device(): lax.all_to_all(gradient_slot_buffer, 'expert', split_axis=0, concat_axis=...  51.2 us
    another operation x20, local copies, waits for them, and re-layouts, valid_part(): return lax.dynamic_slice_in_dim(jnp.stack(kept), first_tick, micro_count, 0)  43 us
    ppermute x5, waiting for transfers between devices, shifted(): lax.ppermute(value, axis, [(source, source + steps) for source in range(f...  42.4 us
    all_to_all x6, starting transfers between devices, on_device(): lax.all_to_all(input_slots, 'expert', split_axis=0, concat_axis=0, tiled=...  41.6 us
    all_to_all x6, starting transfers between devices, on_device(): lax.all_to_all(row_grads, 'expert', split_axis=0, concat_axis=0, tiled=True)  35.2 us
    all_to_all x12, local copies, waits for them, and re-layouts, on_device(): lax.all_to_all(row_grads, 'expert', split_axis=0, concat_axis=0, tiled=True)  26.6 us
  transfers between devices with their start and end apart: 24, of which 22 were waited for; matrix products, arithmetic and copies ran while one was open for 22% of the time, Pallas kernels for 0%

commit v1 on v0

--- a/solution.py
+++ b/solution.py
@@ -32,6 +32,10 @@
     return (route_table, token_table.astype(jnp.bfloat16))
 
 
+def exchange(rows):
+    return lax.all_to_all(rows, "expert", split_axis=0, concat_axis=0, tiled=True)
+
+
 def on_device(saved_inputs, routes, gates, w_in, w_out, cotangent):
     section_count = lax.axis_size("pipe")
     owners = lax.axis_size("expert")
@@ -55,10 +59,29 @@
     ]
     tables = jnp.stack([pair[0] for pair in pairs])
     token_route_tables = jnp.stack([pair[1] for pair in pairs])
+
+    recv_inputs, slopes, hiddens = [], [], []
+    for micro_no in range(micro_count):
+        input_slots = jnp.dot(
+            token_route_tables[micro_no], inputs_dev[micro_no], preferred_element_type=jnp.float32
+        ).astype(jnp.bfloat16)
+        input_recv = exchange(input_slots)
+        preactivation = jnp.dot(input_recv, first_weights, preferred_element_type=jnp.float32)
+        recv_inputs.append(input_recv)
+        slopes.append(silu_slope(preactivation))
+        hiddens.append(jax.nn.silu(preactivation).astype(jnp.bfloat16))
+    recv_inputs = jnp.stack(recv_inputs)
+    slopes = jnp.stack(slopes)
+    hiddens = jnp.stack(hiddens)
+
     incoming = jnp.zeros((tokens_dev, model_width), jnp.bfloat16)
-    kept_inputs, kept_grads, kept_pre, kept_hidden, kept_out = ([], [], [], [], [])
+    first_acc = jnp.zeros((model_width, first_weights.shape[1]), jnp.float32)
+    second_acc = jnp.zeros((second_weights.shape[0], model_width), jnp.float32)
+    final_rows = []
     for tick_no in range(tick_count):
-        micro_id = jnp.clip(tick_no - first_tick, 0, micro_count - 1)
+        offset = tick_no - first_tick
+        valid = (offset >= 0) & (offset < micro_count)
+        micro_id = jnp.clip(offset, 0, micro_count - 1)
         grad_now = jnp.where(section_id == section_count - 1, upstream[micro_id], incoming)
         gate_now = gates[0, micro_id]
         gate_scaled_rows = (gate_now[:, :, None] * grad_now.astype(jnp.float32)[:, None, :]).astype(
@@ -68,24 +91,15 @@
         gradient_slot_buffer = jnp.dot(
             tables[micro_id], gate_scaled_rows, preferred_element_type=jnp.float32
         ).astype(jnp.bfloat16)
-        input_slots = jnp.dot(
-            token_route_tables[micro_id], inputs_dev[micro_id], preferred_element_type=jnp.float32
-        ).astype(jnp.bfloat16)
-        input_recv, grad_recv = (
-            lax.all_to_all(input_slots, "expert", split_axis=0, concat_axis=0, tiled=True),
-            lax.all_to_all(gradient_slot_buffer, "expert", split_axis=0, concat_axis=0, tiled=True),
-        )
-        kept_inputs.append(input_recv)
-        preactivation = jnp.dot(input_recv, first_weights, preferred_element_type=jnp.float32)
+        grad_recv = exchange(gradient_slot_buffer)
         hidden_grad = lax.dot_general(
             grad_recv, second_weights, (((1,), (1,)), ((), ())), preferred_element_type=jnp.float32
         )
-        pre_grad = (hidden_grad * silu_slope(preactivation)).astype(jnp.bfloat16)
-        hidden = jax.nn.silu(preactivation).astype(jnp.bfloat16)
+        pre_grad = (hidden_grad * slopes[micro_id]).astype(jnp.bfloat16)
         row_grads = lax.dot_general(
             pre_grad, first_weights, (((1,), (1,)), ((), ())), preferred_element_type=jnp.float32
         ).astype(jnp.bfloat16)
-        returned = lax.all_to_all(row_grads, "expert", split_axis=0, concat_axis=0, tiled=True)
+        returned = exchange(row_grads)
         summed = lax.dot_general(
             token_route_tables[micro_id],
             returned,
@@ -93,31 +107,24 @@
             preferred_element_type=jnp.float32,
         )
         grad_out = (grad_now.astype(jnp.float32) + summed).astype(jnp.bfloat16)
-        kept_grads.append(grad_recv)
-        kept_pre.append(pre_grad)
-        kept_hidden.append(hidden)
-        kept_out.append(grad_out)
+        first_term = lax.dot_general(
+            recv_inputs[micro_id], pre_grad, (((0,), (0,)), ((), ())), preferred_element_type=jnp.float32
+        )
+        second_term = lax.dot_general(
+            hiddens[micro_id], grad_recv, (((0,), (0,)), ((), ())), preferred_element_type=jnp.float32
+        )
+        first_acc = first_acc + jnp.where(valid, first_term, 0.0)
+        second_acc = second_acc + jnp.where(valid, second_term, 0.0)
+        if tick_no >= tick_count - micro_count:
+            final_rows.append(grad_out)
         if tick_no + 1 < tick_count:
             incoming = shifted(grad_out, "pipe", -1)
 
-    def valid_part(kept):
-        return lax.dynamic_slice_in_dim(jnp.stack(kept), first_tick, micro_count, 0)
-
-    gradient_ready_flags = valid_part(kept_grads)
-    preactivation_ready = valid_part(kept_pre)
-    hidden_ready_flags = valid_part(kept_hidden)
-    input_ready_flags = valid_part(kept_inputs)
-    first_grad = jnp.einsum(
-        "qpz,qpy->zy", input_ready_flags, preactivation_ready, preferred_element_type=jnp.float32
-    ).astype(jnp.bfloat16)
-    second_grad = jnp.einsum(
-        "cgk,cgs->ks", hidden_ready_flags, gradient_ready_flags, preferred_element_type=jnp.float32
-    ).astype(jnp.bfloat16)
-    final_rows = valid_part(kept_out)
-    final_term = jnp.where(section_id == 0, final_rows.astype(jnp.float32), 0.0)
-    grad_in = lax.psum_scatter(
-        final_term.astype(jnp.bfloat16), "pipe", scatter_dimension=2, tiled=True
-    )
+    final_rows = jnp.stack(final_rows)
+    final_term = jnp.where(section_id == 0, final_rows, jnp.zeros_like(final_rows))
+    grad_in = lax.psum_scatter(final_term, "pipe", scatter_dimension=2, tiled=True)
+    first_grad = first_acc.astype(jnp.bfloat16)
+    second_grad = second_acc.astype(jnp.bfloat16)
     return (grad_in, first_grad[None, None], second_grad[None, None])
 
 

time: 803 us -> 777 us (0.968)
  blocking collectives: 13.9 us -> 259 us
  waiting for transfers between devices: 315 us -> 163 us
  starting transfers between devices: 135 us -> 63.9 us
  local copies, waits for them, and re-layouts: 168 us -> 109 us
  matrix products: 115 us -> 131 us
    all_to_all x0 -> x7, blocking collectives: none -> 245 us  [exchange(): lax.all_to_all(rows, 'expert', split_axis=0, concat_axis=0, tiled=True)]
    all_to_all x18 -> x8, waiting for transfers between devices: 272 us -> 119 us  [exchange(): lax.all_to_all(rows, 'expert', split_axis=0, concat_axis=0, tiled=True)]
    all_to_all x18 -> x8, starting transfers between devices: 128 us -> 57.1 us  [exchange(): lax.all_to_all(rows, 'expert', split_axis=0, concat_axis=0, tiled=True)]
    dot_general x8 -> x15, matrix products: 27.2 us -> 63.1 us  [the longest x6 34.7 us: on_device(): lax.dot_general(recv_inputs[micro_id], pre_grad, (((0,), (0,)), ((), ()))...]
    another operation x25 -> x9, local copies, waits for them, and re-layouts: 43.3 us -> 7.96 us  [the longest x4 7.58 us: on_device(): recv_inputs = jnp.stack(recv_inputs)]
    all_to_all x36 -> x30, local copies, waits for them, and re-layouts: 79.6 us -> 65.8 us  [exchange(): lax.all_to_all(rows, 'expert', split_axis=0, concat_axis=0, tiled=True)]
    dot_general x6 -> x3, matrix products: 19.3 us -> 6.39 us  [on_device(): jnp.dot(input_recv, first_weights, preferred_element_type=jnp.float32)]
    reduce_scatter x1, waiting for transfers between devices: 0.01 us -> 12.5 us  [on_device(): lax.psum_scatter(final_term, 'pipe', scatter_dimension=2, tiled=True)]
  transfers between devices with their start and end apart: 24 -> 14, of which waited for: 22 -> 14; matrix products, arithmetic and copies ran while one was open for 22% -> 13% of each run, Pallas kernels for 0% -> 0%
where the time goes in v1:
time: 777 us; the launch traced here: 767 us
  blocking collectives  259 us (33%)
  waiting for transfers between devices  163 us (21%)
  matrix products  131 us (17%)
  local copies, waits for them, and re-layouts  109 us (14%)
  starting transfers between devices  63.9 us (8%)
  other arithmetic  26.3 us (3%)
  between operations  15.4 us (2%)
    all_to_all x7, blocking collectives, exchange(): lax.all_to_all(rows, 'expert', split_axis=0, concat_axis=0, tiled=True)  245 us
    all_to_all x8, waiting for transfers between devices, exchange(): lax.all_to_all(rows, 'expert', split_axis=0, concat_axis=0, tiled=True)  119 us
    all_to_all x30, local copies, waits for them, and re-layouts, exchange(): lax.all_to_all(rows, 'expert', split_axis=0, concat_axis=0, tiled=True)  65.8 us
    all_to_all x8, starting transfers between devices, exchange(): lax.all_to_all(rows, 'expert', split_axis=0, concat_axis=0, tiled=True)  57.1 us
    dot_general x6, matrix products, on_device(): lax.dot_general(recv_inputs[micro_id], pre_grad, (((0,), (0,)), ((), ()))...  34.7 us
    ppermute x5, waiting for transfers between devices, shifted(): lax.ppermute(value, axis, [(source, source + steps) for source in range(f...  31.1 us
    dot_general x6, matrix products, on_device(): lax.dot_general(hiddens[micro_id], grad_recv, (((0,), (0,)), ((), ())), p...  21.4 us
    dot_general x6, matrix products, on_device(): lax.dot_general(grad_recv, second_weights, (((1,), (1,)), ((), ())), pref...  20.5 us
  transfers between devices with their start and end apart: 14, of which 14 were waited for; matrix products, arithmetic and copies ran while one was open for 13% of the time, Pallas kernels for 0%

profile of v1, /device:TPU:8, one launch (start us, length us, event | category | flops | bytes accessed | tf_op | source)
XLA Modules:
  0.0 766.8 jit_solution(7152250231966774901)
XLA Ops:
  14.3 12.3 %all-to-all-start.3 = ((bf16[64,4,2048]{2,1,0:T(4,128)(2,1)}), bf16[64,4,2048]{2,1,0:T(4,128)(2,1)}, u32[]{:S(2)}, u32[]{:S(2)}) async-start(bf16[64,4,2048]{2,1,0:T(4,128)(2,1)} %all_to_all.129), calls=%async_computation.3 | async-start | bytes 2097152 | tf_op jit(solution)/shard_map/all_to_all | solution.py:36
  33.4 21.9 %all-to-all-done.3 = bf16[64,4,2048]{2,1,0:T(4,128)(2,1)} async-done(((bf16[64,4,2048]{2,1,0:T(4,128)(2,1)}), bf16[64,4,2048]{2,1,0:T(4,128)(2,1)}, u32[]{:S(2)}, u32[]{:S(2)}) %all-to-all-start.3) | async-done | bytes 1048608 | tf_op jit(solution)/shard_map/all_to_all | solution.py:36
  55.3 5.9 all-to-all-start.2
  67.4 13.8 %all_gather.3 = bf16[3,64,2048]{2,1,0:T(8,128)(2,1)S(1)} all-gather(bf16[3,64,512]{2,1,0:T(8,128)(2,1)S(1)} %copy-done.29), channel_id=1, replica_groups=mesh['pipe'=4,'expert'=64] {'pipe'}, dimensions={2}, use_global_device_ids=true | all-gather | bytes 983040 | tf_op jit(solution)/shard_map/all_gather | solution.py:55
  83.0 6.8 all-to-all-done.2
  89.8 5.9 all-to-all-start.1
  106.0 18.4 %all-to-all-done.1 = bf16[64,4,2048]{2,1,0:T(4,128)(2,1)} async-done(((bf16[64,4,2048]{2,1,0:T(4,128)(2,1)}), bf16[64,4,2048]{2,1,0:T(4,128)(2,1)}, u32[]{:S(2)}, u32[]{:S(2)}) %all-to-all-start.1) | async-done | bytes 1048608 | tf_op jit(solution)/shard_map/all_to_all | solution.py:36
  124.4 6.3 all-to-all-start
  145.1 14.1 %all-to-all-done = bf16[64,4,2048]{2,1,0:T(4,128)(2,1)} async-done(((bf16[64,4,2048]{2,1,0:T(4,128)(2,1)}), bf16[64,4,2048]{2,1,0:T(4,128)(2,1)}, u32[]{:S(2)}, u32[]{:S(2)}) %all-to-all-start) | async-done | bytes 1048608 | tf_op jit(solution)/shard_map/all_to_all | solution.py:36
  169.8 5.9 all-to-all-start.4
  176.0 28.3 %all-to-all-done.4 = bf16[64,4,2048]{2,1,0:T(4,128)(2,1)} async-done(((bf16[64,4,2048]{2,1,0:T(4,128)(2,1)}), bf16[64,4,2048]{2,1,0:T(4,128)(2,1)}, u32[]{:S(2)}, u32[]{:S(2)}) %all-to-all-start.4) | async-done | bytes 1048608 | tf_op jit(solution)/shard_map/all_to_all | solution.py:36
  211.4 6.6 collective-permute-done
  229.1 35.3 %all_to_all.180 = bf16[64,4,2048]{2,1,0:T(4,128)(2,1)} all-to-all(bf16[64,4,2048]{2,1,0:T(4,128)(2,1)} %all_to_all.135), channel_id=1, replica_groups=mesh['pipe'=4,'expert'=64] {'expert'}, dimensions={0} | all-to-all | bytes 2097152 | tf_op jit(solution)/shard_map/all_to_all | solution.py:36
  274.9 35.0 %all_to_all.181 = bf16[64,4,2048]{2,1,0:T(4,128)(2,1)} all-to-all(bf16[64,4,2048]{2,1,0:T(4,128)(2,1)} %all_to_all.138), channel_id=1, replica_groups=mesh['pipe'=4,'expert'=64] {'expert'}, dimensions={0} | all-to-all | bytes 2097152 | tf_op jit(solution)/shard_map/all_to_all | solution.py:36
  316.4 7.3 collective-permute-done.1
  334.7 35.3 %all_to_all.182 = bf16[64,4,2048]{2,1,0:T(4,128)(2,1)} all-to-all(bf16[64,4,2048]{2,1,0:T(4,128)(2,1)} %all_to_all.141), channel_id=1, replica_groups=mesh['pipe'=4,'expert'=64] {'expert'}, dimensions={0} | all-to-all | bytes 2097152 | tf_op jit(solution)/shard_map/all_to_all | solution.py:36
  380.6 34.5 %all_to_all.183 = bf16[64,4,2048]{2,1,0:T(4,128)(2,1)} all-to-all(bf16[64,4,2048]{2,1,0:T(4,128)(2,1)} %all_to_all.144), channel_id=1, replica_groups=mesh['pipe'=4,'expert'=64] {'expert'}, dimensions={0} | all-to-all | bytes 2097152 | tf_op jit(solution)/shard_map/all_to_all | solution.py:36
  421.7 7.3 collective-permute-done.2
  440.1 35.3 %all_to_all.184 = bf16[64,4,2048]{2,1,0:T(4,128)(2,1)} all-to-all(bf16[64,4,2048]{2,1,0:T(4,128)(2,1)} %all_to_all.147), channel_id=1, replica_groups=mesh['pipe'=4,'expert'=64] {'expert'}, dimensions={0} | all-to-all | bytes 2097152 | tf_op jit(solution)/shard_map/all_to_all | solution.py:36
  485.9 34.5 %all_to_all.185 = bf16[64,4,2048]{2,1,0:T(4,128)(2,1)} all-to-all(bf16[64,4,2048]{2,1,0:T(4,128)(2,1)} %all_to_all.150), channel_id=1, replica_groups=mesh['pipe'=4,'expert'=64] {'expert'}, dimensions={0} | all-to-all | bytes 2097152 | tf_op jit(solution)/shard_map/all_to_all | solution.py:36
  527.0 7.3 collective-permute-done.3
  545.4 35.3 %all_to_all.186 = bf16[64,4,2048]{2,1,0:T(4,128)(2,1)} all-to-all(bf16[64,4,2048]{2,1,0:T(4,128)(2,1)} %all_to_all.153), channel_id=1, replica_groups=mesh['pipe'=4,'expert'=64] {'expert'}, dimensions={0} | all-to-all | bytes 2097152 | tf_op jit(solution)/shard_map/all_to_all | solution.py:36
  591.3 5.9 all-to-all-start.12
  614.5 11.3 %all-to-all-done.12 = bf16[64,4,2048]{2,1,0:T(4,128)(2,1)} async-done(((bf16[64,4,2048]{2,1,0:T(4,128)(2,1)}), bf16[64,4,2048]{2,1,0:T(4,128)(2,1)}, u32[]{:S(2)}, u32[]{:S(2)}) %all-to-all-start.12) | async-done | bytes 1048608 | tf_op jit(solution)/shard_map/all_to_all | solution.py:36
  649.1 7.0 all-to-all-start.13
  656.1 5.1 fusion.100
  695.1 8.0 %all-to-all-start.14 = ((bf16[64,4,2048]{2,1,0:T(4,128)(2,1)}), bf16[64,4,2048]{2,1,0:T(4,128)(2,1)}, u32[]{:S(2)}, u32[]{:S(2)}) async-start(bf16[64,4,2048]{2,1,0:T(4,128)(2,1)} %all_to_all.162), calls=%async_computation.14 | async-start | bytes 2097152 | tf_op jit(solution)/shard_map/all_to_all | solution.py:36
  703.5 5.2 fusion.94
  710.0 5.8 fusion.31
  715.8 16.0 %all-to-all-done.14 = bf16[64,4,2048]{2,1,0:T(4,128)(2,1)} async-done(((bf16[64,4,2048]{2,1,0:T(4,128)(2,1)}), bf16[64,4,2048]{2,1,0:T(4,128)(2,1)}, u32[]{:S(2)}, u32[]{:S(2)}) %all-to-all-start.14) | async-done | bytes 1048608 | tf_op jit(solution)/shard_map/all_to_all | solution.py:36
  737.7 9.3 %fusion.30 = bf16[1,1,2048,768]{3,2,1,0:T(8,128)(2,1)} fusion(bf16[256,768]{1,0:T(8,128)(2,1)} %copy-done.21, pred[]{:T(512)S(6)} %and.24, f32[2048,768]{1,0:T(8,128)} %fusion.94, pred[]{:T(512)S(6)} %and.23, f32[2048,768]{1,0:T(8,128)} %fusion.96, pred[]{:T(512)S(6)} %and.22, f32[2048,768]{1,0:T(8,128)} %fusion.98, pred[]{:T(512)S(6)} %and.21, ...), kind=kOutput, calls=%fused_computation.32 | convolution fusion | flops 824180736 | bytes 36044808 | tf_op jit(solution)/shard_map/dot_general | solution.py:110
  747.0 12.5 %reduce-scatter.2.cloned.1.call-done = bf16[3,64,512]{2,1,0:T(8,128)(2,1)} async-done(((bf16[3,64,2048]{2,1,0:T(8,128)(2,1)}), bf16[3,64,512]{2,1,0:T(8,128)(2,1)}) %reduce-scatter.2.cloned.1.call-update) | async-done | bytes 196624 | tf_op jit(solution)/shard_map/reduce_scatter | solution.py:125
  (262 shorter events, 252.1 us)
Async XLA Ops:
  7.2 129.9 %copy-start = (bf16[1,1,2048,768]{3,2,1,0:T(8,128)(2,1)S(1)}, bf16[1,1,2048,768]{3,2,1,0:T(8,128)(2,1)}, u32[]{:S(2)}) copy-start(bf16[1,1,2048,768]{3,2,1,0:T(8,128)(2,1)} %param.9) | copy-start | bytes 9437188
  9.7 18.1 %copy-start.32 = (s32[64]{0:T(128)}, s32[64]{0:T(128)S(1)}, u32[]{:S(2)}) copy-start(s32[64]{0:T(128)S(1)} %get-tuple-element.13) | copy-start | bytes 772
  9.7 21.5 %copy-start.34 = (s32[64]{0:T(128)}, s32[64]{0:T(128)S(1)}, u32[]{:S(2)}) copy-start(s32[64]{0:T(128)S(1)} %get-tuple-element.14) | copy-start | bytes 772
  14.3 41.0 %all-to-all-start.3 = ((bf16[64,4,2048]{2,1,0:T(4,128)(2,1)}), bf16[64,4,2048]{2,1,0:T(4,128)(2,1)}, u32[]{:S(2)}, u32[]{:S(2)}) async-start(bf16[64,4,2048]{2,1,0:T(4,128)(2,1)} %all_to_all.129), calls=%async_computation.3 | async-start | bytes 2097152 | tf_op jit(solution)/shard_map/all_to_all | solution.py:36
  33.4 34.0 %copy-start.29 = (bf16[3,64,512]{2,1,0:T(8,128)(2,1)S(1)}, bf16[3,64,512]{2,1,0:T(8,128)(2,1)}, u32[]{:S(2)}) copy-start(bf16[3,64,512]{2,1,0:T(8,128)(2,1)} %param.11) | copy-start | bytes 589828
  55.3 34.6 %all-to-all-start.2 = ((bf16[64,4,2048]{2,1,0:T(4,128)(2,1)}), bf16[64,4,2048]{2,1,0:T(4,128)(2,1)}, u32[]{:S(2)}, u32[]{:S(2)}) async-start(bf16[64,4,2048]{2,1,0:T(4,128)(2,1)} %all_to_all.126), calls=%async_computation.2 | async-start | bytes 2097152 | tf_op jit(solution)/shard_map/all_to_all | solution.py:36
  62.8 27.0 %copy-start.44 = (s32[64]{0:T(128)}, s32[64]{0:T(128)S(1)}, u32[]{:S(2)}) copy-start(s32[64]{0:T(128)S(1)} %get-tuple-element.3) | copy-start | bytes 772
  62.8 27.0 %copy-start.46 = (s32[64]{0:T(128)}, s32[64]{0:T(128)S(1)}, u32[]{:S(2)}) copy-start(s32[64]{0:T(128)S(1)} %get-tuple-element.4) | copy-start | bytes 772
  62.8 27.0 %copy-start.48 = (s32[64]{0:T(128)}, s32[64]{0:T(128)S(1)}, u32[]{:S(2)}) copy-start(s32[64]{0:T(128)S(1)} %get-tuple-element.5) | copy-start | bytes 772
  62.8 27.0 %copy-start.50 = (s32[64]{0:T(128)}, s32[64]{0:T(128)S(1)}, u32[]{:S(2)}) copy-start(s32[64]{0:T(128)S(1)} %get-tuple-element.6) | copy-start | bytes 772
  65.2 30.5 %copy-start.31 = (f32[1,3,64,4]{2,3,1,0:T(4,128)S(1)}, f32[1,3,64,4]{2,3,1,0:T(4,128)}, u32[]{:S(2)}) copy-start(f32[1,3,64,4]{2,3,1,0:T(4,128)} %param.8) | copy-start | bytes 9220
  89.8 34.6 %all-to-all-start.1 = ((bf16[64,4,2048]{2,1,0:T(4,128)(2,1)}), bf16[64,4,2048]{2,1,0:T(4,128)(2,1)}, u32[]{:S(2)}, u32[]{:S(2)}) async-start(bf16[64,4,2048]{2,1,0:T(4,128)(2,1)} %all_to_all.123), calls=%async_computation.1 | async-start | bytes 2097152 | tf_op jit(solution)/shard_map/all_to_all | solution.py:36
  124.4 34.7 %all-to-all-start = ((bf16[64,4,2048]{2,1,0:T(4,128)(2,1)}), bf16[64,4,2048]{2,1,0:T(4,128)(2,1)}, u32[]{:S(2)}, u32[]{:S(2)}) async-start(bf16[64,4,2048]{2,1,0:T(4,128)(2,1)} %all_to_all.120), calls=%async_computation | async-start | bytes 2097152 | tf_op jit(solution)/shard_map/all_to_all | solution.py:36
  167.5 8.2 %copy-start.49 = (s32[64]{0:T(128)S(1)}, s32[64]{0:T(128)}, u32[]{:S(2)}) copy-start(s32[64]{0:T(128)} %copy-done.48) | copy-start | bytes 772
  167.5 8.2 %copy-start.51 = (s32[64]{0:T(128)S(1)}, s32[64]{0:T(128)}, u32[]{:S(2)}) copy-start(s32[64]{0:T(128)} %copy-done.50) | copy-start | bytes 772
  167.5 8.3 %copy-start.37 = (s32[64]{0:T(128)S(1)}, s32[64]{0:T(128)}, u32[]{:S(2)}) copy-start(s32[64]{0:T(128)} %copy-done.36) | copy-start | bytes 772
  167.5 8.3 %copy-start.39 = (s32[64]{0:T(128)S(1)}, s32[64]{0:T(128)}, u32[]{:S(2)}) copy-start(s32[64]{0:T(128)} %copy-done.38) | copy-start | bytes 772
  167.5 8.3 %copy-start.41 = (s32[64]{0:T(128)S(1)}, s32[64]{0:T(128)}, u32[]{:S(2)}) copy-start(s32[64]{0:T(128)} %copy-done.40) | copy-start | bytes 772
  167.5 8.3 %copy-start.43 = (s32[64]{0:T(128)S(1)}, s32[64]{0:T(128)}, u32[]{:S(2)}) copy-start(s32[64]{0:T(128)} %copy-done.42) | copy-start | bytes 772
  167.5 8.4 %copy-start.33 = (s32[64]{0:T(128)S(1)}, s32[64]{0:T(128)}, u32[]{:S(2)}) copy-start(s32[64]{0:T(128)} %copy-done.32) | copy-start | bytes 772
  167.5 8.4 %copy-start.35 = (s32[64]{0:T(128)S(1)}, s32[64]{0:T(128)}, u32[]{:S(2)}) copy-start(s32[64]{0:T(128)} %copy-done.34) | copy-start | bytes 772
  169.8 34.6 %all-to-all-start.4 = ((bf16[64,4,2048]{2,1,0:T(4,128)(2,1)}), bf16[64,4,2048]{2,1,0:T(4,128)(2,1)}, u32[]{:S(2)}, u32[]{:S(2)}) async-start(bf16[64,4,2048]{2,1,0:T(4,128)(2,1)} %all_to_all.132), calls=%async_computation.4 | async-start | bytes 2097152 | tf_op jit(solution)/shard_map/all_to_all | solution.py:36
  208.8 9.3 %collective-permute-start = (bf16[64,2048]{1,0:T(8,128)(2,1)}, bf16[64,2048]{1,0:T(8,128)(2,1)}, u32[]{:S(2)}, u32[]{:S(2)}) collective-permute-start(bf16[64,2048]{1,0:T(8,128)(2,1)} %fusion.50), channel_id=1, source_target_pairs={{64,0},{128,64},{192,128},{65,1},{129,65},{193,129},{66,2},{130,66... | collective-permute-start | bytes 786440 | tf_op jit(solution)/shard_map/ppermute | solution.py:10
  314.4 9.3 %collective-permute-start.1 = (bf16[64,2048]{1,0:T(8,128)(2,1)}, bf16[64,2048]{1,0:T(8,128)(2,1)}, u32[]{:S(2)}, u32[]{:S(2)}) collective-permute-start(bf16[64,2048]{1,0:T(8,128)(2,1)} %fusion.51), channel_id=1, source_target_pairs={{64,0},{128,64},{192,128},{65,1},{129,65},{193,129},{66,2},{130,66... | collective-permute-start | bytes 786440 | tf_op jit(solution)/shard_map/ppermute | solution.py:10
  419.7 9.3 %collective-permute-start.2 = (bf16[64,2048]{1,0:T(8,128)(2,1)}, bf16[64,2048]{1,0:T(8,128)(2,1)}, u32[]{:S(2)}, u32[]{:S(2)}) collective-permute-start(bf16[64,2048]{1,0:T(8,128)(2,1)} %fusion.52), channel_id=1, source_target_pairs={{64,0},{128,64},{192,128},{65,1},{129,65},{193,129},{66,2},{130,66... | collective-permute-start | bytes 786440 | tf_op jit(solution)/shard_map/ppermute | solution.py:10
  525.0 9.3 %collective-permute-start.3 = (bf16[64,2048]{1,0:T(8,128)(2,1)}, bf16[64,2048]{1,0:T(8,128)(2,1)}, u32[]{:S(2)}, u32[]{:S(2)}) collective-permute-start(bf16[64,2048]{1,0:T(8,128)(2,1)} %fusion.53), channel_id=1, source_target_pairs={{64,0},{128,64},{192,128},{65,1},{129,65},{193,129},{66,2},{130,66... | collective-permute-start | bytes 786440 | tf_op jit(solution)/shard_map/ppermute | solution.py:10
  591.3 34.6 %all-to-all-start.12 = ((bf16[64,4,2048]{2,1,0:T(4,128)(2,1)}), bf16[64,4,2048]{2,1,0:T(4,128)(2,1)}, u32[]{:S(2)}, u32[]{:S(2)}) async-start(bf16[64,4,2048]{2,1,0:T(4,128)(2,1)} %all_to_all.156), calls=%async_computation.12 | async-start | bytes 2097152 | tf_op jit(solution)/shard_map/all_to_all | solution.py:36
  629.7 10.9 %copy-start.30 = (f32[64,4]{1,0:T(8,128)S(1)}, f32[64,4]{1,0:T(8,128)}, u32[]{:S(2)}) copy-start(f32[64,4]{1,0:T(8,128)} %copy.32) | copy-start | bytes 3076
  629.7 9.1 %collective-permute-start.4 = (bf16[64,2048]{1,0:T(8,128)(2,1)S(1)}, bf16[64,2048]{1,0:T(8,128)(2,1)S(1)}, u32[]{:S(2)}, u32[]{:S(2)}) collective-permute-start(bf16[64,2048]{1,0:T(8,128)(2,1)S(1)} %fusion.54), channel_id=1, source_target_pairs={{64,0},{128,64},{192,128},{65,1},{129,65},{193,129},{66,2},{130,66... | collective-permute-start | bytes 786440 | tf_op jit(solution)/shard_map/ppermute | solution.py:10
  649.1 35.5 %all-to-all-start.13 = ((bf16[64,4,2048]{2,1,0:T(4,128)(2,1)}), bf16[64,4,2048]{2,1,0:T(4,128)(2,1)}, u32[]{:S(2)}, u32[]{:S(2)}) async-start(bf16[64,4,2048]{2,1,0:T(4,128)(2,1)} %all_to_all.159), calls=%async_computation.13 | async-start | bytes 2097152 | tf_op jit(solution)/shard_map/all_to_all | solution.py:36
  695.1 36.7 %all-to-all-start.14 = ((bf16[64,4,2048]{2,1,0:T(4,128)(2,1)}), bf16[64,4,2048]{2,1,0:T(4,128)(2,1)}, u32[]{:S(2)}, u32[]{:S(2)}) async-start(bf16[64,4,2048]{2,1,0:T(4,128)(2,1)} %all_to_all.162), calls=%async_computation.14 | async-start | bytes 2097152 | tf_op jit(solution)/shard_map/all_to_all | solution.py:36
  703.2 56.3 %reduce-scatter.2.cloned.1.call-start = ((), (), s32[]{:S(2)}) async-start(), calls=%async_computation.16 | async-start | bytes 983040 | tf_op jit(solution)/shard_map/reduce_scatter | solution.py:125
  (34 other events, 97.8 us)
Sparse Core Ops, SparseCore 0:
  737.8 21.6 reduce-scatter.1

commit v2 on v1

v2 whole, which is shorter than its diff:
```python
import jax
import jax.numpy as jnp
from jax import lax
from jax.sharding import PartitionSpec as P


def shifted(value, axis, steps):
    count = lax.axis_size(axis)
    first, last = (max(0, -steps), min(count, count - steps))
    return lax.ppermute(value, axis, [(source, source + steps) for source in range(first, last)])


def silu_slope(preactivation):
    logistic = jax.nn.sigmoid(preactivation)
    return logistic * (1.0 + preactivation * (1.0 - logistic))


def placement_tables(routes_micro, gates_micro, owners, capacity):
    tokens, route_count = routes_micro.shape
    flat_routes = routes_micro.reshape(-1)
    expert_ids = jnp.arange(owners, dtype=jnp.int32)
    one_hot = (flat_routes[:, None] == expert_ids[None, :]).astype(jnp.int32)
    ranks = jnp.sum((jnp.cumsum(one_hot, axis=0) - 1) * one_hot, axis=1)
    slots = (flat_routes * capacity + ranks).reshape(tokens, route_count)
    slot_ids = jnp.arange(owners * capacity, dtype=jnp.int32)
    token_table = jnp.zeros((owners * capacity, tokens), jnp.float32)
    gate_table = jnp.zeros((owners * capacity, tokens), jnp.float32)
    for route_no in range(route_count):
        hit = slot_ids[:, None] == slots[:, route_no][None, :]
        token_table = token_table + hit.astype(jnp.float32)
        gate_table = gate_table + jnp.where(hit, gates_micro[:, route_no][None, :], 0.0)
    shape = (owners, capacity, tokens)
    return token_table.astype(jnp.bfloat16).reshape(shape), gate_table.reshape(shape)


def exchange(rows):
    return lax.all_to_all(rows, "expert", split_axis=0, concat_axis=0, tiled=True)


def pick(candidates, index):
    if len(candidates) == 1:
        return candidates[0]
    chosen = candidates[-1]
    for number in range(len(candidates) - 2, -1, -1):
        chosen = jnp.where(index == number, candidates[number], chosen)
    return chosen


def on_device(saved_inputs, routes, gates, w_in, w_out, cotangent):
    section_count = lax.axis_size("pipe")
    owners = lax.axis_size("expert")
    section_id = lax.axis_index("pipe")
    micro_count = saved_inputs.shape[1]
    tokens_dev = saved_inputs.shape[2]
    model_width = saved_inputs.shape[3]
    route_count = routes.shape[3]
    expert_count = w_in.shape[1] * owners
    capacity = max(2, tokens_dev * route_count * 6 // (5 * expert_count))
    tick_count = section_count + micro_count - 1
    first_tick = section_count - 1 - section_id
    first_weights = w_in[0, 0]
    second_weights = w_out[0, 0]
    inputs_dev = saved_inputs[0]
    upstream = lax.all_gather(cotangent, "pipe", axis=2, tiled=True)
    token_tables, gate_tables = [], []
    for micro_no in range(micro_count):
        token_table, gate_table = placement_tables(routes[0, micro_no], gates[0, micro_no], owners, capacity)
        token_tables.append(token_table)
        gate_tables.append(gate_table)
    token_stack = jnp.stack(token_tables)
    gate_stack = jnp.stack(gate_tables)

    recv_inputs, slopes, hiddens = [], [], []
    incoming = jnp.zeros((tokens_dev, model_width), jnp.bfloat16)
    first_acc = jnp.zeros((model_width, first_weights.shape[1]), jnp.float32)
    second_acc = jnp.zeros((second_weights.shape[0], model_width), jnp.float32)
    final_rows = []
    for tick_no in range(tick_count):
        offset = tick_no - first_tick
        valid = (offset >= 0) & (offset < micro_count)
        micro_id = jnp.clip(offset, 0, micro_count - 1)
        grad_now = jnp.where(section_id == section_count - 1, upstream[micro_id], incoming)
        gradient_slots = jnp.einsum(
            "pqk,kd->pqd",
            gate_stack[micro_id],
            grad_now.astype(jnp.float32),
            precision=lax.Precision.HIGHEST,
            preferred_element_type=jnp.float32,
        ).astype(jnp.bfloat16)
        if tick_no < micro_count:
            input_slots = jnp.einsum(
                "pqk,kd->pqd",
                token_tables[tick_no],
                inputs_dev[tick_no],
                preferred_element_type=jnp.float32,
            ).astype(jnp.bfloat16)
            both = exchange(jnp.concatenate([gradient_slots, input_slots], axis=1))
            grad_recv = both[:, :capacity]
            input_recv = both[:, capacity:]
            preactivation = jnp.einsum(
                "pqd,df->pqf", input_recv, first_weights, preferred_element_type=jnp.float32
            )
            recv_inputs.append(input_recv)
            slopes.append(silu_slope(preactivation))
            hiddens.append(jax.nn.silu(preactivation).astype(jnp.bfloat16))
        else:
            grad_recv = exchange(gradient_slots)
        hidden_grad = jnp.einsum(
            "pqd,fd->pqf", grad_recv, second_weights, preferred_element_type=jnp.float32
        )
        pre_grad = (hidden_grad * pick(slopes, micro_id)).astype(jnp.bfloat16)
        row_grads = jnp.einsum(
            "pqf,df->pqd", pre_grad, first_weights, preferred_element_type=jnp.float32
        ).astype(jnp.bfloat16)
        returned = exchange(row_grads)
        summed = jnp.einsum(
            "pqk,pqd->kd", token_stack[micro_id], returned, preferred_element_type=jnp.float32
        )
        grad_out = (grad_now.astype(jnp.float32) + summed).astype(jnp.bfloat16)
        first_term = jnp.einsum(
            "pqd,pqf->df", pick(recv_inputs, micro_id), pre_grad, preferred_element_type=jnp.float32
        )
        second_term = jnp.einsum(
            "pqf,pqd->fd", pick(hiddens, micro_id), grad_recv, preferred_element_type=jnp.float32
        )
        first_acc = first_acc + jnp.where(valid, first_term, 0.0)
        second_acc = second_acc + jnp.where(valid, second_term, 0.0)
        if tick_no >= tick_count - micro_count:
            final_rows.append(grad_out)
        if tick_no + 1 < tick_count:
            incoming = shifted(grad_out, "pipe", -1)

    final_rows = jnp.stack(final_rows)
    final_term = jnp.where(section_id == 0, final_rows, jnp.zeros_like(final_rows))
    grad_in = lax.psum_scatter(final_term, "pipe", scatter_dimension=2, tiled=True)
    first_grad = first_acc.astype(jnp.bfloat16)
    second_grad = second_acc.astype(jnp.bfloat16)
    return (grad_in, first_grad[None, None], second_grad[None, None])


def solution(mesh):
    return jax.shard_map(
        on_device,
        mesh=mesh,
        in_specs=(
            P("pipe", None, "expert", None),
            P("pipe", None, "expert", None),
            P("pipe", None, "expert", None),
            P("pipe", "expert", None, None),
            P("pipe", "expert", None, None),
            P(None, "expert", "pipe"),
        ),
        out_specs=(
            P(None, "expert", "pipe"),
            P("pipe", "expert", None, None),
            P("pipe", "expert", None, None),
        ),
        check_vma=False,
    )
```

time: 777 us -> 713 us (0.918)
  waiting for transfers between devices: 163 us -> 242 us
  blocking collectives: 259 us -> 182 us
  local copies, waits for them, and re-layouts: 109 us -> 34 us
  matrix products: 131 us -> 162 us
  other arithmetic: 26.3 us -> 8.22 us
    all_to_all x8, waiting for transfers between devices: 119 us -> 207 us  [exchange(): lax.all_to_all(rows, 'expert', split_axis=0, concat_axis=0, tiled=True)]
    all_to_all x7 -> x4, blocking collectives: 245 us -> 166 us  [exchange(): lax.all_to_all(rows, 'expert', split_axis=0, concat_axis=0, tiled=True)]
    all_to_all x30 -> x0, local copies, waits for them, and re-layouts: 65.8 us -> none  [exchange(): lax.all_to_all(rows, 'expert', split_axis=0, concat_axis=0, tiled=True)]
    dot_general x42, matrix products: 131 us -> 162 us  [the longest x6 47 us: on_device(): jnp.einsum('pqd,pqf->df', pick(recv_inputs, micro_id), pre_grad, preferre...]
    convert_element_type x15 -> x2, other arithmetic: 18.7 us -> 1.67 us  [placement_tables(): token_table.astype(jnp.bfloat16).reshape(shape)]
    unnamed x109 -> x99, local copies, waits for them, and re-layouts: 14.5 us -> 3.17 us
    reduce_scatter x1, waiting for transfers between devices: 12.5 us -> 4.16 us  [on_device(): lax.psum_scatter(final_term, 'pipe', scatter_dimension=2, tiled=True)]
    slice x4 -> x6, local copies, waits for them, and re-layouts: 0.86 us -> 8.7 us  [the longest x3 7.97 us: on_device(): input_recv = both[:, capacity:]]
  transfers between devices with their start and end apart: 14 -> 14, of which waited for: 14 -> 13; matrix products, arithmetic and copies ran while one was open for 13% -> 14% of each run, Pallas kernels for 0% -> 0%
where the time goes in v2:
time: 713 us; the launch traced here: 706 us
  waiting for transfers between devices  242 us (34%)
  blocking collectives  182 us (26%)
  matrix products  162 us (23%)
  starting transfers between devices  62.7 us (9%)
  local copies, waits for them, and re-layouts  34 us (5%)
  between operations  15.2 us (2%)
  other arithmetic  8.22 us (1%)
    all_to_all x8, waiting for transfers between devices, exchange(): lax.all_to_all(rows, 'expert', split_axis=0, concat_axis=0, tiled=True)  207 us
    all_to_all x4, blocking collectives, exchange(): lax.all_to_all(rows, 'expert', split_axis=0, concat_axis=0, tiled=True)  166 us
    all_to_all x8, starting transfers between devices, exchange(): lax.all_to_all(rows, 'expert', split_axis=0, concat_axis=0, tiled=True)  56.2 us
    dot_general x6, matrix products, on_device(): jnp.einsum('pqd,pqf->df', pick(recv_inputs, micro_id), pre_grad, preferre...  47 us
    dot_general x6, matrix products, on_device(): jnp.einsum('pqf,pqd->fd', pick(hiddens, micro_id), grad_recv, preferred_e...  43.9 us
    ppermute x5, waiting for transfers between devices, shifted(): lax.ppermute(value, axis, [(source, source + steps) for source in range(f...  30.9 us
    dot_general x6, matrix products, on_device(): jnp.einsum('pqd,fd->pqf', grad_recv, second_weights, preferred_element_ty...  23.1 us
    dot_general x6, matrix products, on_device(): jnp.einsum('pqk,pqd->kd', token_stack[micro_id], returned, preferred_elem...  17.7 us
  transfers between devices with their start and end apart: 14, of which 13 were waited for; matrix products, arithmetic and copies ran while one was open for 14% of the time, Pallas kernels for 0%

profile of v2, /device:TPU:8, one launch (start us, length us, event | category | flops | bytes accessed | tf_op | source)
XLA Modules:
  0.0 706.0 jit_solution(10290136651369491585)
XLA Ops:
  13.3 16.1 %all_gather.3 = bf16[3,64,2048]{2,1,0:T(8,128)(2,1)} all-gather(bf16[3,64,512]{2,1,0:T(8,128)(2,1)} %param.11), channel_id=1, replica_groups=mesh['pipe'=4,'expert'=64] {'pipe'}, dimensions={2}, use_global_device_ids=true | all-gather | bytes 983040 | tf_op jit(solution)/shard_map/all_gather | solution.py:64
  36.2 63.3 %all_to_all.60 = bf16[64,8,2048]{2,1,0:T(8,128)(2,1)S(1)} all-to-all(bf16[64,8,2048]{2,1,0:T(8,128)(2,1)S(1)} %copy.46), channel_id=1, replica_groups=mesh['pipe'=4,'expert'=64] {'expert'}, dimensions={0} | all-to-all | bytes 4194304 | tf_op jit(solution)/shard_map/all_to_all | solution.py:37
  116.4 27.1 %all-to-all-done.1 = bf16[64,4,2048]{2,1,0:T(4,128)(2,1)} async-done(((bf16[64,4,2048]{2,1,0:T(4,128)(2,1)}), bf16[64,4,2048]{2,1,0:T(4,128)(2,1)}, u32[]{:S(2)}, u32[]{:S(2)}) %all-to-all-start.1) | async-done | bytes 1048608 | tf_op jit(solution)/shard_map/all_to_all | solution.py:37
  149.4 6.5 collective-permute-done
  160.6 6.6 all-to-all-start.2
  167.2 51.1 %all-to-all-done.2 = bf16[64,8,2048]{2,1,0:T(8,128)(2,1)} async-done(((bf16[64,8,2048]{2,1,0:T(8,128)(2,1)}), bf16[64,8,2048]{2,1,0:T(8,128)(2,1)}, u32[]{:S(2)}, u32[]{:S(2)}) %all-to-all-start.2) | async-done | bytes 2097184 | tf_op jit(solution)/shard_map/all_to_all | solution.py:37
  228.9 34.0 %all_to_all.61 = bf16[64,4,2048]{2,1,0:T(4,128)(2,1)S(1)} all-to-all(bf16[64,4,2048]{2,1,0:T(4,128)(2,1)S(1)} %copy.55), channel_id=1, replica_groups=mesh['pipe'=4,'expert'=64] {'expert'}, dimensions={0} | all-to-all | bytes 2097152 | tf_op jit(solution)/shard_map/all_to_all | solution.py:37
  268.6 6.5 collective-permute-done.1
  279.8 6.8 all-to-all-start.4
  286.6 51.1 %all-to-all-done.4 = bf16[64,8,2048]{2,1,0:T(8,128)(2,1)} async-done(((bf16[64,8,2048]{2,1,0:T(8,128)(2,1)}), bf16[64,8,2048]{2,1,0:T(8,128)(2,1)}, u32[]{:S(2)}, u32[]{:S(2)}) %all-to-all-start.4) | async-done | bytes 2097184 | tf_op jit(solution)/shard_map/all_to_all | solution.py:37
  348.9 34.0 %all_to_all.62 = bf16[64,4,2048]{2,1,0:T(4,128)(2,1)S(1)} all-to-all(bf16[64,4,2048]{2,1,0:T(4,128)(2,1)S(1)} %copy.61), channel_id=1, replica_groups=mesh['pipe'=4,'expert'=64] {'expert'}, dimensions={0} | all-to-all | bytes 2097152 | tf_op jit(solution)/shard_map/all_to_all | solution.py:37
  387.2 8.0 %collective-permute-done.2 = bf16[64,2048]{1,0:T(8,128)(2,1)} collective-permute-done((bf16[64,2048]{1,0:T(8,128)(2,1)}, bf16[64,2048]{1,0:T(8,128)(2,1)}, u32[]{:S(2)}, u32[]{:S(2)}) %collective-permute-start.2) | collective-permute-done | bytes 262176 | tf_op jit(solution)/shard_map/ppermute | solution.py:10
  399.0 7.0 all-to-all-start.6
  406.0 28.7 %all-to-all-done.6 = bf16[64,4,2048]{2,1,0:T(4,128)(2,1)} async-done(((bf16[64,4,2048]{2,1,0:T(4,128)(2,1)}), bf16[64,4,2048]{2,1,0:T(4,128)(2,1)}, u32[]{:S(2)}, u32[]{:S(2)}) %all-to-all-start.6) | async-done | bytes 1048608 | tf_op jit(solution)/shard_map/all_to_all | solution.py:37
  441.9 34.2 %all_to_all.63 = bf16[64,4,2048]{2,1,0:T(4,128)(2,1)S(1)} all-to-all(bf16[64,4,2048]{2,1,0:T(4,128)(2,1)S(1)} %copy.66), channel_id=1, replica_groups=mesh['pipe'=4,'expert'=64] {'expert'}, dimensions={0} | all-to-all | bytes 2097152 | tf_op jit(solution)/shard_map/all_to_all | solution.py:37
  480.5 8.0 %collective-permute-done.3 = bf16[64,2048]{1,0:T(8,128)(2,1)} collective-permute-done((bf16[64,2048]{1,0:T(8,128)(2,1)}, bf16[64,2048]{1,0:T(8,128)(2,1)}, u32[]{:S(2)}, u32[]{:S(2)}) %collective-permute-start.3) | collective-permute-done | bytes 262176 | tf_op jit(solution)/shard_map/ppermute | solution.py:10
  492.3 6.6 all-to-all-start.8
  498.9 28.7 %all-to-all-done.8 = bf16[64,4,2048]{2,1,0:T(4,128)(2,1)} async-done(((bf16[64,4,2048]{2,1,0:T(4,128)(2,1)}), bf16[64,4,2048]{2,1,0:T(4,128)(2,1)}, u32[]{:S(2)}, u32[]{:S(2)}) %all-to-all-start.8) | async-done | bytes 1048608 | tf_op jit(solution)/shard_map/all_to_all | solution.py:37
  536.5 6.2 all-to-all-start.9
  552.9 5.9 fusion.117
  558.8 12.5 %all-to-all-done.9 = bf16[64,4,2048]{2,1,0:T(4,128)(2,1)} async-done(((bf16[64,4,2048]{2,1,0:T(4,128)(2,1)}), bf16[64,4,2048]{2,1,0:T(4,128)(2,1)}, u32[]{:S(2)}, u32[]{:S(2)}) %all-to-all-start.9) | async-done | bytes 1048608 | tf_op jit(solution)/shard_map/all_to_all | solution.py:37
  575.2 5.8 fusion.131
  586.7 6.8 all-to-all-start.10
  593.5 6.1 fusion.128
  599.6 6.8 fusion.114
  612.2 7.2 %fusion.111 = f32[2048,768,1]{1,0,2:T(8,128)} fusion(bf16[64,4,768]{2,0,1:T(8,128)(2,1)S(1)} %copy-done.39, pred[]{:T(512)S(6)} %eq.771, pred[]{:T(512)S(6)} %eq.770, bf16[64,4,2048]{2,1,0:T(4,128)(2,1)S(1)} %copy-done.10, bf16[64,4,2048]{2,1,0:T(4,128)(2,1)S(1)} %copy-done.7, bf16[64,4,2048]{2,1,0:T(4,128)(2,1)S(1)} %copy-done.3), kind=kOutput, calls=%fused_computation.105 | convolution fusion | flops 806354944 | bytes 9830402 | tf_op jit(solution)/shard_map/pqd,pqf->df/dot_general | solution.py:120
  619.4 6.8 fusion.108
  635.1 10.5 %all-to-all-start.11 = ((bf16[64,4,2048]{2,1,0:T(4,128)(2,1)}), bf16[64,4,2048]{2,1,0:T(4,128)(2,1)}, u32[]{:S(2)}, u32[]{:S(2)}) async-start(bf16[64,4,2048]{2,1,0:T(4,128)(2,1)} %copy.76), calls=%async_computation.11 | async-start | bytes 2097152 | tf_op jit(solution)/shard_map/all_to_all | solution.py:37
  645.7 6.0 fusion.139
  651.7 14.8 %fusion.42 = bf16[1,1,2048,768]{3,2,1,0:T(8,128)(2,1)} fusion(bf16[64,4,768]{2,0,1:T(8,128)(2,1)S(1)} %copy-done.24, pred[]{:T(512)S(6)} %and.24, f32[2048,768,1]{1,0,2:T(8,128)} %fusion.108, pred[]{:T(512)S(6)} %and.23, f32[2048,768,1]{1,0,2:T(8,128)} %fusion.111, pred[]{:T(512)S(6)} %and.22, f32[2048,768,1]{1,0,2:T(8,128)} %fusion.114, pred[]{:T(512)S(6)} %and.21, ...), kind=kOutput, calls=%fused_computation.54 | convolution fusion | flops 825229312 | bytes 38141960 | tf_op jit(solution)/shard_map/pqd,pqf->df/dot_general | solution.py:120
  666.5 7.8 %all-to-all-done.11 = bf16[64,4,2048]{2,1,0:T(4,128)(2,1)} async-done(((bf16[64,4,2048]{2,1,0:T(4,128)(2,1)}), bf16[64,4,2048]{2,1,0:T(4,128)(2,1)}, u32[]{:S(2)}, u32[]{:S(2)}) %all-to-all-start.11) | async-done | bytes 1048608 | tf_op jit(solution)/shard_map/all_to_all | solution.py:37
  679.0 15.9 %fusion.43 = bf16[1,1,768,2048]{3,2,1,0:T(8,128)(2,1)} fusion(pred[]{:T(512)S(6)} %and.24, f32[768,2048,1]{1,0,2:T(8,128)} %fusion.139, pred[]{:T(512)S(6)} %and.23, f32[768,2048,1]{1,0,2:T(8,128)} %fusion.142, pred[]{:T(512)S(6)} %and.22, f32[768,2048,1]{1,0,2:T(8,128)} %fusion.128, pred[]{:T(512)S(6)} %and.21, f32[768,2048,1]{1,0,2:T(8,128)} %fusion.131, ...), kind=kOutput, calls=%fused_computation.55 | convolution fusion | flops 824573952 | bytes 36831240 | tf_op jit(solution)/shard_map/pqf,pqd->fd/dot_general | solution.py:123
  (203 shorter events, 147.5 us)
Async XLA Ops:
  7.2 93.5 %copy-start = (bf16[1,1,2048,768]{3,2,1,0:T(8,128)(2,1)S(1)}, bf16[1,1,2048,768]{3,2,1,0:T(8,128)(2,1)}, u32[]{:S(2)}) copy-start(bf16[1,1,2048,768]{3,2,1,0:T(8,128)(2,1)} %param.9) | copy-start | bytes 9437188
  11.1 21.8 %copy-start.25 = (s32[64]{0:T(128)}, s32[64]{0:T(128)S(1)}, u32[]{:S(2)}) copy-start(s32[64]{0:T(128)S(1)} %get-tuple-element.10) | copy-start | bytes 772
  109.1 34.3 %all-to-all-start.1 = ((bf16[64,4,2048]{2,1,0:T(4,128)(2,1)}), bf16[64,4,2048]{2,1,0:T(4,128)(2,1)}, u32[]{:S(2)}, u32[]{:S(2)}) async-start(bf16[64,4,2048]{2,1,0:T(4,128)(2,1)} %copy.49), calls=%async_computation.1 | async-start | bytes 2097152 | tf_op jit(solution)/shard_map/all_to_all | solution.py:37
  146.7 9.3 %collective-permute-start = (bf16[64,2048]{1,0:T(8,128)(2,1)}, bf16[64,2048]{1,0:T(8,128)(2,1)}, u32[]{:S(2)}, u32[]{:S(2)}) collective-permute-start(bf16[64,2048]{1,0:T(8,128)(2,1)} %fusion.63), channel_id=1, source_target_pairs={{64,0},{128,64},{192,128},{65,1},{129,65},{193,129},{66,2},{130,66... | collective-permute-start | bytes 786440 | tf_op jit(solution)/shard_map/ppermute | solution.py:10
  160.6 57.8 %all-to-all-start.2 = ((bf16[64,8,2048]{2,1,0:T(8,128)(2,1)}), bf16[64,8,2048]{2,1,0:T(8,128)(2,1)}, u32[]{:S(2)}, u32[]{:S(2)}) async-start(bf16[64,8,2048]{2,1,0:T(8,128)(2,1)} %copy.52), calls=%async_computation.2 | async-start | bytes 4194304 | tf_op jit(solution)/shard_map/all_to_all | solution.py:37
  265.9 9.3 %collective-permute-start.1 = (bf16[64,2048]{1,0:T(8,128)(2,1)}, bf16[64,2048]{1,0:T(8,128)(2,1)}, u32[]{:S(2)}, u32[]{:S(2)}) collective-permute-start(bf16[64,2048]{1,0:T(8,128)(2,1)} %add_convert_fusion.4), channel_id=1, source_target_pairs={{64,0},{128,64},{192,128},{65,1},{129,65},{193,129},{66,2},{130,66... | collective-permute-start | bytes 786440 | tf_op jit(solution)/shard_map/ppermute | solution.py:10
  279.8 58.0 %all-to-all-start.4 = ((bf16[64,8,2048]{2,1,0:T(8,128)(2,1)}), bf16[64,8,2048]{2,1,0:T(8,128)(2,1)}, u32[]{:S(2)}, u32[]{:S(2)}) async-start(bf16[64,8,2048]{2,1,0:T(8,128)(2,1)} %copy.58), calls=%async_computation.4 | async-start | bytes 4194304 | tf_op jit(solution)/shard_map/all_to_all | solution.py:37
  385.9 9.3 %collective-permute-start.2 = (bf16[64,2048]{1,0:T(8,128)(2,1)}, bf16[64,2048]{1,0:T(8,128)(2,1)}, u32[]{:S(2)}, u32[]{:S(2)}) collective-permute-start(bf16[64,2048]{1,0:T(8,128)(2,1)} %add_convert_fusion.3), channel_id=1, source_target_pairs={{64,0},{128,64},{192,128},{65,1},{129,65},{193,129},{66,2},{130,66... | collective-permute-start | bytes 786440 | tf_op jit(solution)/shard_map/ppermute | solution.py:10
  399.0 35.7 %all-to-all-start.6 = ((bf16[64,4,2048]{2,1,0:T(4,128)(2,1)}), bf16[64,4,2048]{2,1,0:T(4,128)(2,1)}, u32[]{:S(2)}, u32[]{:S(2)}) async-start(bf16[64,4,2048]{2,1,0:T(4,128)(2,1)} %copy.64), calls=%async_computation.6 | async-start | bytes 2097152 | tf_op jit(solution)/shard_map/all_to_all | solution.py:37
  479.2 9.3 %collective-permute-start.3 = (bf16[64,2048]{1,0:T(8,128)(2,1)}, bf16[64,2048]{1,0:T(8,128)(2,1)}, u32[]{:S(2)}, u32[]{:S(2)}) collective-permute-start(bf16[64,2048]{1,0:T(8,128)(2,1)} %add_convert_fusion.2), channel_id=1, source_target_pairs={{64,0},{128,64},{192,128},{65,1},{129,65},{193,129},{66,2},{130,66... | collective-permute-start | bytes 786440 | tf_op jit(solution)/shard_map/ppermute | solution.py:10
  492.3 35.3 %all-to-all-start.8 = ((bf16[64,4,2048]{2,1,0:T(4,128)(2,1)}), bf16[64,4,2048]{2,1,0:T(4,128)(2,1)}, u32[]{:S(2)}, u32[]{:S(2)}) async-start(bf16[64,4,2048]{2,1,0:T(4,128)(2,1)} %copy.69), calls=%async_computation.8 | async-start | bytes 2097152 | tf_op jit(solution)/shard_map/all_to_all | solution.py:37
  536.5 34.7 %all-to-all-start.9 = ((bf16[64,4,2048]{2,1,0:T(4,128)(2,1)}), bf16[64,4,2048]{2,1,0:T(4,128)(2,1)}, u32[]{:S(2)}, u32[]{:S(2)}) async-start(bf16[64,4,2048]{2,1,0:T(4,128)(2,1)} %copy.71), calls=%async_computation.9 | async-start | bytes 2097152 | tf_op jit(solution)/shard_map/all_to_all | solution.py:37
  542.8 5.6 copy-start.13
  573.9 7.1 %copy-start.16 = (bf16[64,2048]{1,0:T(8,128)(2,1)}, bf16[64,2048]{1,0:T(8,128)(2,1)S(1)}, u32[]{:S(2)}) copy-start(bf16[64,2048]{1,0:T(8,128)(2,1)S(1)} %add_convert_fusion.1) | copy-start | bytes 786436
  573.9 9.0 %collective-permute-start.4 = (bf16[64,2048]{1,0:T(8,128)(2,1)S(1)}, bf16[64,2048]{1,0:T(8,128)(2,1)S(1)}, u32[]{:S(2)}, u32[]{:S(2)}) collective-permute-start(bf16[64,2048]{1,0:T(8,128)(2,1)S(1)} %add_convert_fusion.1), channel_id=1, source_target_pairs={{64,0},{128,64},{192,128},{65,1},{129,65},{193,129},{66,2},{130,66... | collective-permute-start | bytes 786440 | tf_op jit(solution)/shard_map/ppermute | solution.py:10
  586.7 39.5 %all-to-all-start.10 = ((bf16[64,4,2048]{2,1,0:T(4,128)(2,1)}), bf16[64,4,2048]{2,1,0:T(4,128)(2,1)}, u32[]{:S(2)}, u32[]{:S(2)}) async-start(bf16[64,4,2048]{2,1,0:T(4,128)(2,1)} %copy.74), calls=%async_computation.10 | async-start | bytes 2097152 | tf_op jit(solution)/shard_map/all_to_all | solution.py:37
  593.5 6.1 copy-start.3
  593.5 6.1 copy-start.7
  593.5 6.1 copy-start.10
  593.5 6.1 copy-start.37
  599.6 6.8 copy-start.20
  599.6 6.8 copy-start.21
  599.6 6.8 copy-start.22
  606.4 5.7 copy-start.39
  612.2 7.2 %copy-start.41 = (bf16[64,4,768]{2,0,1:T(8,128)(2,1)S(1)}, bf16[64,4,768]{2,0,1:T(8,128)(2,1)}, u32[]{:S(2)}) copy-start(bf16[64,4,768]{2,0,1:T(8,128)(2,1)} %copy-done.40) | copy-start | bytes 1179652
  635.1 39.2 %all-to-all-start.11 = ((bf16[64,4,2048]{2,1,0:T(4,128)(2,1)}), bf16[64,4,2048]{2,1,0:T(4,128)(2,1)}, u32[]{:S(2)}, u32[]{:S(2)}) async-start(bf16[64,4,2048]{2,1,0:T(4,128)(2,1)} %copy.76), calls=%async_computation.11 | async-start | bytes 2097152 | tf_op jit(solution)/shard_map/all_to_all | solution.py:37
  645.6 53.4 %reduce-scatter.2.cloned.1.call-start = ((), (), s32[]{:S(2)}) async-start(), calls=%async_computation.13 | async-start | bytes 983040 | tf_op jit(solution)/shard_map/reduce_scatter | solution.py:135
  645.6 6.0 copy-start.4
  645.6 6.0 copy-start.8
  645.7 6.0 copy-start.11
  645.7 6.0 copy-start.24
  651.7 25.2 %copy-start.17 = (bf16[64,2048]{1,0:T(8,128)(2,1)S(1)}, bf16[64,2048]{1,0:T(8,128)(2,1)}, u32[]{:S(2)}) copy-start(bf16[64,2048]{1,0:T(8,128)(2,1)} %copy-done.16) | copy-start | bytes 786436
  (30 other events, 82.8 us)
Sparse Core Ops, SparseCore 0:
  679.1 19.8 reduce-scatter.1

commit v3 on v2

--- a/solution.py
+++ b/solution.py
@@ -61,7 +61,12 @@
     first_weights = w_in[0, 0]
     second_weights = w_out[0, 0]
     inputs_dev = saved_inputs[0]
-    upstream = lax.all_gather(cotangent, "pipe", axis=2, tiled=True)
+    last_section = section_count - 1
+    pieces = [
+        cotangent if source == last_section else lax.ppermute(cotangent, "pipe", [(source, last_section)])
+        for source in range(section_count)
+    ]
+    upstream = jnp.concatenate(pieces, axis=2)
     token_tables, gate_tables = [], []
     for micro_no in range(micro_count):
         token_table, gate_table = placement_tables(routes[0, micro_no], gates[0, micro_no], owners, capacity)
@@ -72,12 +77,10 @@
 
     recv_inputs, slopes, hiddens = [], [], []
     incoming = jnp.zeros((tokens_dev, model_width), jnp.bfloat16)
-    first_acc = jnp.zeros((model_width, first_weights.shape[1]), jnp.float32)
-    second_acc = jnp.zeros((second_weights.shape[0], model_width), jnp.float32)
+    pre_grads, grad_recvs = [], []
     final_rows = []
     for tick_no in range(tick_count):
         offset = tick_no - first_tick
-        valid = (offset >= 0) & (offset < micro_count)
         micro_id = jnp.clip(offset, 0, micro_count - 1)
         grad_now = jnp.where(section_id == section_count - 1, upstream[micro_id], incoming)
         gradient_slots = jnp.einsum(
@@ -117,14 +120,8 @@
             "pqk,pqd->kd", token_stack[micro_id], returned, preferred_element_type=jnp.float32
         )
         grad_out = (grad_now.astype(jnp.float32) + summed).astype(jnp.bfloat16)
-        first_term = jnp.einsum(
-            "pqd,pqf->df", pick(recv_inputs, micro_id), pre_grad, preferred_element_type=jnp.float32
-        )
-        second_term = jnp.einsum(
-            "pqf,pqd->fd", pick(hiddens, micro_id), grad_recv, preferred_element_type=jnp.float32
-        )
-        first_acc = first_acc + jnp.where(valid, first_term, 0.0)
-        second_acc = second_acc + jnp.where(valid, second_term, 0.0)
+        pre_grads.append(pre_grad)
+        grad_recvs.append(grad_recv)
         if tick_no >= tick_count - micro_count:
             final_rows.append(grad_out)
         if tick_no + 1 < tick_count:
@@ -133,8 +130,18 @@
     final_rows = jnp.stack(final_rows)
     final_term = jnp.where(section_id == 0, final_rows, jnp.zeros_like(final_rows))
     grad_in = lax.psum_scatter(final_term, "pipe", scatter_dimension=2, tiled=True)
-    first_grad = first_acc.astype(jnp.bfloat16)
-    second_grad = second_acc.astype(jnp.bfloat16)
+    first_terms, second_terms = [], []
+    for micro_no in range(micro_count):
+        own_pre = pick([pre_grads[micro_no + lag] for lag in range(section_count)], first_tick)
+        own_grad = pick([grad_recvs[micro_no + lag] for lag in range(section_count)], first_tick)
+        first_terms.append(jnp.einsum(
+            "pqd,pqf->df", recv_inputs[micro_no], own_pre, preferred_element_type=jnp.float32
+        ))
+        second_terms.append(jnp.einsum(
+            "pqf,pqd->fd", hiddens[micro_no], own_grad, preferred_element_type=jnp.float32
+        ))
+    first_grad = sum(first_terms[1:], first_terms[0]).astype(jnp.bfloat16)
+    second_grad = sum(second_terms[1:], second_terms[0]).astype(jnp.bfloat16)
     return (grad_in, first_grad[None, None], second_grad[None, None])
 
 

time: 713 us -> 706 us (level)
  matrix products: 162 us -> 119 us
  blocking collectives: 182 us -> 200 us
  waiting for transfers between devices: 242 us -> 256 us
    dot_general x12 -> x6, matrix products: 91 us -> 49.8 us  [the longest x3 31.6 us: on_device(): jnp.einsum('pqf,pqd->fd', hiddens[micro_no], own_grad, preferred_element_...]
    all_to_all x4 -> x5, blocking collectives: 166 us -> 200 us  [exchange(): lax.all_to_all(rows, 'expert', split_axis=0, concat_axis=0, tiled=True)]
    all_gather x1 -> x0, blocking collectives: 16.1 us -> none  [on_device(): upstream = lax.all_gather(cotangent, 'pipe', axis=2, tiled=True)]
    all_to_all x8 -> x7, starting transfers between devices: 56.2 us -> 45.1 us  [exchange(): lax.all_to_all(rows, 'expert', split_axis=0, concat_axis=0, tiled=True)]
    ppermute x0 -> x3, starting transfers between devices: none -> 8.26 us  [on_device(): lax.ppermute(cotangent, 'pipe', [(source, last_section)])]
    all_to_all x8 -> x7, waiting for transfers between devices: 207 us -> 215 us  [exchange(): lax.all_to_all(rows, 'expert', split_axis=0, concat_axis=0, tiled=True)]
  transfers between devices with their start and end apart: 14 -> 16, of which waited for: 13 -> 12; matrix products, arithmetic and copies ran while one was open for 14% -> 10% of each run, Pallas kernels for 0% -> 0%
where the time goes in v3:
time: 706 us; the launch traced here: 699 us
  waiting for transfers between devices  256 us (36%)
  blocking collectives  200 us (28%)
  matrix products  119 us (17%)
  starting transfers between devices  60.2 us (9%)
  local copies, waits for them, and re-layouts  39.4 us (6%)
  between operations  15.3 us (2%)
  other arithmetic  9.48 us (1%)
    all_to_all x7, waiting for transfers between devices, exchange(): lax.all_to_all(rows, 'expert', split_axis=0, concat_axis=0, tiled=True)  215 us
    all_to_all x5, blocking collectives, exchange(): lax.all_to_all(rows, 'expert', split_axis=0, concat_axis=0, tiled=True)  200 us
    all_to_all x7, starting transfers between devices, exchange(): lax.all_to_all(rows, 'expert', split_axis=0, concat_axis=0, tiled=True)  45.1 us
    ppermute x5, waiting for transfers between devices, shifted(): lax.ppermute(value, axis, [(source, source + steps) for source in range(f...  37 us
    dot_general x3, matrix products, on_device(): jnp.einsum('pqf,pqd->fd', hiddens[micro_no], own_grad, preferred_element_...  31.6 us
    dot_general x6, matrix products, on_device(): jnp.einsum('pqd,fd->pqf', grad_recv, second_weights, preferred_element_ty...  23.1 us
    dot_general x3, matrix products, on_device(): jnp.einsum('pqd,pqf->df', recv_inputs[micro_no], own_pre, preferred_eleme...  18.2 us
    dot_general x6, matrix products, on_device(): jnp.einsum('pqk,pqd->kd', token_stack[micro_id], returned, preferred_elem...  18.1 us
  transfers between devices with their start and end apart: 16, of which 12 were waited for; matrix products, arithmetic and copies ran while one was open for 10% of the time, Pallas kernels for 0%

profile of v3, /device:TPU:8, one launch (start us, length us, event | category | flops | bytes accessed | tf_op | source)
XLA Modules:
  0.0 699.3 jit_solution(2722374859700101058)
XLA Ops:
  8.6 5.4 collective-permute-start
  34.2 63.6 %all_to_all.60 = bf16[64,8,2048]{2,1,0:T(8,128)(2,1)S(1)} all-to-all(bf16[64,8,2048]{2,1,0:T(8,128)(2,1)S(1)} %copy.46), channel_id=1, replica_groups=mesh['pipe'=4,'expert'=64] {'expert'}, dimensions={0} | all-to-all | bytes 4194304 | tf_op jit(solution)/shard_map/all_to_all | solution.py:37
  107.3 5.6 all-to-all-start.1
  114.5 27.1 %all-to-all-done.1 = bf16[64,4,2048]{2,1,0:T(4,128)(2,1)} async-done(((bf16[64,4,2048]{2,1,0:T(4,128)(2,1)}), bf16[64,4,2048]{2,1,0:T(4,128)(2,1)}, u32[]{:S(2)}, u32[]{:S(2)}) %all-to-all-start.1) | async-done | bytes 1048608 | tf_op jit(solution)/shard_map/all_to_all | solution.py:37
  147.6 6.5 collective-permute-done.3
  158.8 6.6 all-to-all-start.2
  165.4 51.1 %all-to-all-done.2 = bf16[64,8,2048]{2,1,0:T(8,128)(2,1)} async-done(((bf16[64,8,2048]{2,1,0:T(8,128)(2,1)}), bf16[64,8,2048]{2,1,0:T(8,128)(2,1)}, u32[]{:S(2)}, u32[]{:S(2)}) %all-to-all-start.2) | async-done | bytes 2097184 | tf_op jit(solution)/shard_map/all_to_all | solution.py:37
  227.0 34.0 %all_to_all.61 = bf16[64,4,2048]{2,1,0:T(4,128)(2,1)S(1)} all-to-all(bf16[64,4,2048]{2,1,0:T(4,128)(2,1)S(1)} %copy.55), channel_id=1, replica_groups=mesh['pipe'=4,'expert'=64] {'expert'}, dimensions={0} | all-to-all | bytes 2097152 | tf_op jit(solution)/shard_map/all_to_all | solution.py:37
  266.8 6.5 collective-permute-done.4
  278.0 6.8 all-to-all-start.4
  284.8 51.1 %all-to-all-done.4 = bf16[64,8,2048]{2,1,0:T(8,128)(2,1)} async-done(((bf16[64,8,2048]{2,1,0:T(8,128)(2,1)}), bf16[64,8,2048]{2,1,0:T(8,128)(2,1)}, u32[]{:S(2)}, u32[]{:S(2)}) %all-to-all-start.4) | async-done | bytes 2097184 | tf_op jit(solution)/shard_map/all_to_all | solution.py:37
  347.2 34.0 %all_to_all.62 = bf16[64,4,2048]{2,1,0:T(4,128)(2,1)S(1)} all-to-all(bf16[64,4,2048]{2,1,0:T(4,128)(2,1)S(1)} %copy.61), channel_id=1, replica_groups=mesh['pipe'=4,'expert'=64] {'expert'}, dimensions={0} | all-to-all | bytes 2097152 | tf_op jit(solution)/shard_map/all_to_all | solution.py:37
  385.5 8.0 %collective-permute-done.5 = bf16[64,2048]{1,0:T(8,128)(2,1)} collective-permute-done((bf16[64,2048]{1,0:T(8,128)(2,1)}, bf16[64,2048]{1,0:T(8,128)(2,1)}, u32[]{:S(2)}, u32[]{:S(2)}) %collective-permute-start.5) | collective-permute-done | bytes 262176 | tf_op jit(solution)/shard_map/ppermute | solution.py:10
  397.3 6.6 all-to-all-start.6
  403.9 28.7 %all-to-all-done.6 = bf16[64,4,2048]{2,1,0:T(4,128)(2,1)} async-done(((bf16[64,4,2048]{2,1,0:T(4,128)(2,1)}), bf16[64,4,2048]{2,1,0:T(4,128)(2,1)}, u32[]{:S(2)}, u32[]{:S(2)}) %all-to-all-start.6) | async-done | bytes 1048608 | tf_op jit(solution)/shard_map/all_to_all | solution.py:37
  432.6 5.4 fusion.78
  439.9 34.2 %all_to_all.63 = bf16[64,4,2048]{2,1,0:T(4,128)(2,1)S(1)} all-to-all(bf16[64,4,2048]{2,1,0:T(4,128)(2,1)S(1)} %copy.66), channel_id=1, replica_groups=mesh['pipe'=4,'expert'=64] {'expert'}, dimensions={0} | all-to-all | bytes 2097152 | tf_op jit(solution)/shard_map/all_to_all | solution.py:37
  478.4 8.0 %collective-permute-done.6 = bf16[64,2048]{1,0:T(8,128)(2,1)} collective-permute-done((bf16[64,2048]{1,0:T(8,128)(2,1)}, bf16[64,2048]{1,0:T(8,128)(2,1)}, u32[]{:S(2)}, u32[]{:S(2)}) %collective-permute-start.6) | collective-permute-done | bytes 262176 | tf_op jit(solution)/shard_map/ppermute | solution.py:10
  490.2 7.0 all-to-all-start.8
  497.2 28.5 %all-to-all-done.8 = bf16[64,4,2048]{2,1,0:T(4,128)(2,1)} async-done(((bf16[64,4,2048]{2,1,0:T(4,128)(2,1)}), bf16[64,4,2048]{2,1,0:T(4,128)(2,1)}, u32[]{:S(2)}, u32[]{:S(2)}) %all-to-all-start.8) | async-done | bytes 1048608 | tf_op jit(solution)/shard_map/all_to_all | solution.py:37
  525.7 5.4 fusion.75
  532.9 34.2 %all_to_all.64 = bf16[64,4,2048]{2,1,0:T(4,128)(2,1)S(1)} all-to-all(bf16[64,4,2048]{2,1,0:T(4,128)(2,1)S(1)} %copy.71), channel_id=1, replica_groups=mesh['pipe'=4,'expert'=64] {'expert'}, dimensions={0} | all-to-all | bytes 2097152 | tf_op jit(solution)/shard_map/all_to_all | solution.py:37
  571.5 8.0 %collective-permute-done.7 = bf16[64,2048]{1,0:T(8,128)(2,1)} collective-permute-done((bf16[64,2048]{1,0:T(8,128)(2,1)}, bf16[64,2048]{1,0:T(8,128)(2,1)}, u32[]{:S(2)}, u32[]{:S(2)}) %collective-permute-start.7) | collective-permute-done | bytes 262176 | tf_op jit(solution)/shard_map/ppermute | solution.py:10
  583.3 6.6 all-to-all-start.10
  589.9 28.7 %all-to-all-done.10 = bf16[64,4,2048]{2,1,0:T(4,128)(2,1)} async-done(((bf16[64,4,2048]{2,1,0:T(4,128)(2,1)}), bf16[64,4,2048]{2,1,0:T(4,128)(2,1)}, u32[]{:S(2)}, u32[]{:S(2)}) %all-to-all-start.10) | async-done | bytes 1048608 | tf_op jit(solution)/shard_map/all_to_all | solution.py:37
  618.6 5.4 fusion.72
  627.5 5.9 all-to-all-start.11
  633.9 5.7 fusion.121
  639.6 9.2 %fusion.103 = f32[768,2048,1]{1,0,2:T(8,128)} fusion(pred[]{:T(512)S(6)} %eq.784, pred[]{:T(512)S(6)} %eq.783, pred[]{:T(512)S(6)} %eq.782, bf16[64,4,2048]{2,1,0:T(4,128)(2,1)S(1)} %copy-done.8, bf16[64,4,2048]{2,1,0:T(4,128)(2,1)S(1)} %copy-done.11, bf16[64,4,2048]{2,1,0:T(4,128)(2,1)S(1)} %copy-done.3, bf16[64,4,2048]{2,1,0:T(4,128)(2,1)} %all-to-all-done.6, ...), kind=kOutput, calls=%fused_computation.89 | convolution fusion | flops 807862272 | bytes 11272195 | tf_op jit(solution)/shard_map/pqf,pqd->fd/dot_general | solution.py:140
  653.0 9.6 %fusion.99 = f32[768,2048,1]{1,0,2:T(8,128)} fusion(pred[]{:T(512)S(6)} %eq.784, pred[]{:T(512)S(6)} %eq.783, pred[]{:T(512)S(6)} %eq.782, bf16[64,4,2048]{2,1,0:T(4,128)(2,1)S(1)} %copy-done.11, bf16[64,4,2048]{2,1,0:T(4,128)(2,1)} %all-to-all-done.8, bf16[64,4,2048]{2,1,0:T(4,128)(2,1)S(1)} %copy-done.3, bf16[64,4,2048]{2,1,0:T(4,128)(2,1)} %all-to-all-done.6, ...), kind=kOutput, calls=%fused_computation.85 | convolution fusion | flops 807862272 | bytes 11272195 | tf_op jit(solution)/shard_map/pqf,pqd->fd/dot_general | solution.py:140
  667.3 8.4 %fusion.32 = bf16[1,1,2048,768]{3,2,1,0:T(8,128)(2,1)} fusion(f32[2048,768,1]{1,0,2:T(8,128)} %fusion.118, f32[2048,768,1]{1,0,2:T(8,128)} %fusion.121, bf16[64,4,2048]{2,1,0:T(4,128)(2,1)} %copy-done.5, bf16[64,4,768]{2,0,1:T(8,128)(2,1)S(1)} %copy-done.17, bf16[64,4,768]{2,0,1:T(8,128)(2,1)} %copy-done.18, bf16[64,4,768]{2,0,1:T(8,128)(2,1)} %copy-done.20, ...), kind=kOutput, calls=%fused_computation.36 | convolution fusion | flops 810614784 | bytes 18350084 | tf_op jit(solution)/shard_map/pqd,pqf->df/dot_general | solution.py:137
  675.8 12.8 %fusion.33 = bf16[1,1,768,2048]{3,2,1,0:T(8,128)(2,1)} fusion(f32[768,2048,1]{1,0,2:T(8,128)} %fusion.99, f32[768,2048,1]{1,0,2:T(8,128)} %fusion.103, pred[]{:T(512)S(6)} %eq.784, pred[]{:T(512)S(6)} %eq.783, pred[]{:T(512)S(6)} %eq.782, bf16[64,4,2048]{2,1,0:T(4,128)(2,1)} %all-to-all-done.10, bf16[64,4,2048]{2,1,0:T(4,128)(2,1)} %all-to-all-done.8, ...), kind=kOutput, calls=%fused_computation.37 | convolution fusion | flops 812580864 | bytes 20709380 | tf_op jit(solution)/shard_map/pqf,pqd->fd/dot_general | solution.py:140
  (191 shorter events, 119.3 us)
Async XLA Ops:
  7.2 91.8 %copy-start = (bf16[1,1,2048,768]{3,2,1,0:T(8,128)(2,1)S(1)}, bf16[1,1,2048,768]{3,2,1,0:T(8,128)(2,1)}, u32[]{:S(2)}) copy-start(bf16[1,1,2048,768]{3,2,1,0:T(8,128)(2,1)} %param.9) | copy-start | bytes 9437188
  7.2 20.9 %collective-permute-start.1 = (bf16[3,64,512]{2,1,0:T(8,128)(2,1)}, bf16[3,64,512]{2,1,0:T(8,128)(2,1)}, u32[]{:S(2)}, u32[]{:S(2)}) collective-permute-start(bf16[3,64,512]{2,1,0:T(8,128)(2,1)} %param.11), channel_id=1, source_target_pairs={{64,192},{65,193},{66,194},{67,195},{68,196},{69,197},{70,198},{71... | collective-permute-start | bytes 589832 | tf_op jit(solution)/shard_map/ppermute | solution.py:66
  8.6 18.5 %collective-permute-start = (bf16[3,64,512]{2,1,0:T(8,128)(2,1)}, bf16[3,64,512]{2,1,0:T(8,128)(2,1)}, u32[]{:S(2)}, u32[]{:S(2)}) collective-permute-start(bf16[3,64,512]{2,1,0:T(8,128)(2,1)} %param.11), channel_id=1, source_target_pairs={{0,192},{1,193},{2,194},{3,195},{4,196},{5,197},{6,198},{7,199},{8... | collective-permute-start | bytes 589832 | tf_op jit(solution)/shard_map/ppermute | solution.py:66
  14.1 14.9 %collective-permute-start.2 = (bf16[3,64,512]{2,1,0:T(8,128)(2,1)}, bf16[3,64,512]{2,1,0:T(8,128)(2,1)}, u32[]{:S(2)}, u32[]{:S(2)}) collective-permute-start(bf16[3,64,512]{2,1,0:T(8,128)(2,1)} %param.11), channel_id=1, source_target_pairs={{128,192},{129,193},{130,194},{131,195},{132,196},{133,197},{134,1... | collective-permute-start | bytes 589832 | tf_op jit(solution)/shard_map/ppermute | solution.py:66
  19.1 6.8 copy-start.23
  21.7 4.2 copy-start.24
  21.7 4.2 copy-start.25
  25.9 6.9 copy-start.6
  107.3 34.3 %all-to-all-start.1 = ((bf16[64,4,2048]{2,1,0:T(4,128)(2,1)}), bf16[64,4,2048]{2,1,0:T(4,128)(2,1)}, u32[]{:S(2)}, u32[]{:S(2)}) async-start(bf16[64,4,2048]{2,1,0:T(4,128)(2,1)} %copy.49), calls=%async_computation.1 | async-start | bytes 2097152 | tf_op jit(solution)/shard_map/all_to_all | solution.py:37
  144.9 9.3 %collective-permute-start.3 = (bf16[64,2048]{1,0:T(8,128)(2,1)}, bf16[64,2048]{1,0:T(8,128)(2,1)}, u32[]{:S(2)}, u32[]{:S(2)}) collective-permute-start(bf16[64,2048]{1,0:T(8,128)(2,1)} %fusion.53), channel_id=1, source_target_pairs={{64,0},{128,64},{192,128},{65,1},{129,65},{193,129},{66,2},{130,66... | collective-permute-start | bytes 786440 | tf_op jit(solution)/shard_map/ppermute | solution.py:10
  158.8 57.8 %all-to-all-start.2 = ((bf16[64,8,2048]{2,1,0:T(8,128)(2,1)}), bf16[64,8,2048]{2,1,0:T(8,128)(2,1)}, u32[]{:S(2)}, u32[]{:S(2)}) async-start(bf16[64,8,2048]{2,1,0:T(8,128)(2,1)} %copy.52), calls=%async_computation.2 | async-start | bytes 4194304 | tf_op jit(solution)/shard_map/all_to_all | solution.py:37
  264.1 9.3 %collective-permute-start.4 = (bf16[64,2048]{1,0:T(8,128)(2,1)}, bf16[64,2048]{1,0:T(8,128)(2,1)}, u32[]{:S(2)}, u32[]{:S(2)}) collective-permute-start(bf16[64,2048]{1,0:T(8,128)(2,1)} %add_convert_fusion.4), channel_id=1, source_target_pairs={{64,0},{128,64},{192,128},{65,1},{129,65},{193,129},{66,2},{130,66... | collective-permute-start | bytes 786440 | tf_op jit(solution)/shard_map/ppermute | solution.py:10
  278.0 58.0 %all-to-all-start.4 = ((bf16[64,8,2048]{2,1,0:T(8,128)(2,1)}), bf16[64,8,2048]{2,1,0:T(8,128)(2,1)}, u32[]{:S(2)}, u32[]{:S(2)}) async-start(bf16[64,8,2048]{2,1,0:T(8,128)(2,1)} %copy.58), calls=%async_computation.4 | async-start | bytes 4194304 | tf_op jit(solution)/shard_map/all_to_all | solution.py:37
  384.3 9.3 %collective-permute-start.5 = (bf16[64,2048]{1,0:T(8,128)(2,1)}, bf16[64,2048]{1,0:T(8,128)(2,1)}, u32[]{:S(2)}, u32[]{:S(2)}) collective-permute-start(bf16[64,2048]{1,0:T(8,128)(2,1)} %add_convert_fusion.3), channel_id=1, source_target_pairs={{64,0},{128,64},{192,128},{65,1},{129,65},{193,129},{66,2},{130,66... | collective-permute-start | bytes 786440 | tf_op jit(solution)/shard_map/ppermute | solution.py:10
  397.3 35.3 %all-to-all-start.6 = ((bf16[64,4,2048]{2,1,0:T(4,128)(2,1)}), bf16[64,4,2048]{2,1,0:T(4,128)(2,1)}, u32[]{:S(2)}, u32[]{:S(2)}) async-start(bf16[64,4,2048]{2,1,0:T(4,128)(2,1)} %copy.64), calls=%async_computation.6 | async-start | bytes 2097152 | tf_op jit(solution)/shard_map/all_to_all | solution.py:37
  477.2 9.3 %collective-permute-start.6 = (bf16[64,2048]{1,0:T(8,128)(2,1)}, bf16[64,2048]{1,0:T(8,128)(2,1)}, u32[]{:S(2)}, u32[]{:S(2)}) collective-permute-start(bf16[64,2048]{1,0:T(8,128)(2,1)} %add_convert_fusion.2), channel_id=1, source_target_pairs={{64,0},{128,64},{192,128},{65,1},{129,65},{193,129},{66,2},{130,66... | collective-permute-start | bytes 786440 | tf_op jit(solution)/shard_map/ppermute | solution.py:10
  490.2 35.5 %all-to-all-start.8 = ((bf16[64,4,2048]{2,1,0:T(4,128)(2,1)}), bf16[64,4,2048]{2,1,0:T(4,128)(2,1)}, u32[]{:S(2)}, u32[]{:S(2)}) async-start(bf16[64,4,2048]{2,1,0:T(4,128)(2,1)} %copy.69), calls=%async_computation.8 | async-start | bytes 2097152 | tf_op jit(solution)/shard_map/all_to_all | solution.py:37
  570.2 9.3 %collective-permute-start.7 = (bf16[64,2048]{1,0:T(8,128)(2,1)}, bf16[64,2048]{1,0:T(8,128)(2,1)}, u32[]{:S(2)}, u32[]{:S(2)}) collective-permute-start(bf16[64,2048]{1,0:T(8,128)(2,1)} %add_convert_fusion.1), channel_id=1, source_target_pairs={{64,0},{128,64},{192,128},{65,1},{129,65},{193,129},{66,2},{130,66... | collective-permute-start | bytes 786440 | tf_op jit(solution)/shard_map/ppermute | solution.py:10
  583.3 35.3 %all-to-all-start.10 = ((bf16[64,4,2048]{2,1,0:T(4,128)(2,1)}), bf16[64,4,2048]{2,1,0:T(4,128)(2,1)}, u32[]{:S(2)}, u32[]{:S(2)}) async-start(bf16[64,4,2048]{2,1,0:T(4,128)(2,1)} %copy.74), calls=%async_computation.10 | async-start | bytes 2097152 | tf_op jit(solution)/shard_map/all_to_all | solution.py:37
  625.7 8.1 %copy-start.17 = (bf16[64,4,768]{2,0,1:T(8,128)(2,1)S(1)}, bf16[64,4,768]{2,0,1:T(8,128)(2,1)}, u32[]{:S(2)}) copy-start(bf16[64,4,768]{2,0,1:T(8,128)(2,1)} %copy-done.16) | copy-start | bytes 1179652
  627.5 35.1 %all-to-all-start.11 = ((bf16[64,4,2048]{2,1,0:T(4,128)(2,1)}), bf16[64,4,2048]{2,1,0:T(4,128)(2,1)}, u32[]{:S(2)}, u32[]{:S(2)}) async-start(bf16[64,4,2048]{2,1,0:T(4,128)(2,1)} %copy.76), calls=%async_computation.11 | async-start | bytes 2097152 | tf_op jit(solution)/shard_map/all_to_all | solution.py:37
  633.4 58.8 %reduce-scatter.2.cloned.1.call-start = ((), (), s32[]{:S(2)}) async-start(), calls=%async_computation.13 | async-start | bytes 983040 | tf_op jit(solution)/shard_map/reduce_scatter | solution.py:132
  633.9 5.7 copy-start.3
  633.9 5.7 copy-start.8
  633.9 5.7 copy-start.11
  633.9 5.7 copy-start.37
  639.6 9.3 %copy-start.13 = (bf16[64,4,2048]{2,1,0:T(4,128)(2,1)S(1)}, bf16[64,4,2048]{2,1,0:T(4,128)(2,1)}, u32[]{:S(2)}) copy-start(bf16[64,4,2048]{2,1,0:T(4,128)(2,1)} %copy-done.12) | copy-start | bytes 3145732
  639.6 9.3 %copy-start.19 = (bf16[64,4,768]{2,0,1:T(8,128)(2,1)S(1)}, bf16[64,4,768]{2,0,1:T(8,128)(2,1)}, u32[]{:S(2)}) copy-start(bf16[64,4,768]{2,0,1:T(8,128)(2,1)} %copy-done.18) | copy-start | bytes 1179652
  639.6 9.3 %copy-start.21 = (bf16[64,4,768]{2,0,1:T(8,128)(2,1)S(1)}, bf16[64,4,768]{2,0,1:T(8,128)(2,1)}, u32[]{:S(2)}) copy-start(bf16[64,4,768]{2,0,1:T(8,128)(2,1)} %copy-done.20) | copy-start | bytes 1179652
  639.6 9.3 %copy-start.33 = (bf16[64,4,768]{2,0,1:T(8,128)(2,1)S(1)}, bf16[64,4,768]{2,0,1:T(8,128)(2,1)}, u32[]{:S(2)}) copy-start(bf16[64,4,768]{2,0,1:T(8,128)(2,1)} %copy-done.32) | copy-start | bytes 1179652
  667.3 8.5 %copy-start.4 = (bf16[64,4,2048]{2,1,0:T(4,128)(2,1)S(1)}, bf16[64,4,2048]{2,1,0:T(4,128)(2,1)}, u32[]{:S(2)}) copy-start(bf16[64,4,2048]{2,1,0:T(4,128)(2,1)} %copy-done.2) | copy-start | bytes 3145732
  667.3 8.4 %copy-start.15 = (f32[64,4,768]{2,0,1:T(8,128)S(1)}, f32[64,4,768]{2,0,1:T(8,128)}, u32[]{:S(2)}) copy-start(f32[64,4,768]{2,0,1:T(8,128)} %copy-done.14) | copy-start | bytes 2359300
  (25 other events, 61.2 us)
Sparse Core Ops, SparseCore 0:
  667.4 24.7 reduce-scatter.1

commit v4 on v3

--- a/solution.py
+++ b/solution.py
@@ -77,7 +77,8 @@
 
     recv_inputs, slopes, hiddens = [], [], []
     incoming = jnp.zeros((tokens_dev, model_width), jnp.bfloat16)
-    pre_grads, grad_recvs = [], []
+    pre_keep = jnp.zeros((micro_count + 1, owners, capacity, first_weights.shape[1]), jnp.bfloat16)
+    grad_keep = jnp.zeros((micro_count + 1, owners, capacity, model_width), jnp.bfloat16)
     final_rows = []
     for tick_no in range(tick_count):
         offset = tick_no - first_tick
@@ -120,8 +121,9 @@
             "pqk,pqd->kd", token_stack[micro_id], returned, preferred_element_type=jnp.float32
         )
         grad_out = (grad_now.astype(jnp.float32) + summed).astype(jnp.bfloat16)
-        pre_grads.append(pre_grad)
-        grad_recvs.append(grad_recv)
+        keep_at = jnp.where(offset >= micro_count, micro_count, micro_id)
+        pre_keep = lax.dynamic_update_slice_in_dim(pre_keep, pre_grad[None], keep_at, 0)
+        grad_keep = lax.dynamic_update_slice_in_dim(grad_keep, grad_recv[None], keep_at, 0)
         if tick_no >= tick_count - micro_count:
             final_rows.append(grad_out)
         if tick_no + 1 < tick_count:
@@ -130,18 +132,12 @@
     final_rows = jnp.stack(final_rows)
     final_term = jnp.where(section_id == 0, final_rows, jnp.zeros_like(final_rows))
     grad_in = lax.psum_scatter(final_term, "pipe", scatter_dimension=2, tiled=True)
-    first_terms, second_terms = [], []
-    for micro_no in range(micro_count):
-        own_pre = pick([pre_grads[micro_no + lag] for lag in range(section_count)], first_tick)
-        own_grad = pick([grad_recvs[micro_no + lag] for lag in range(section_count)], first_tick)
-        first_terms.append(jnp.einsum(
-            "pqd,pqf->df", recv_inputs[micro_no], own_pre, preferred_element_type=jnp.float32
-        ))
-        second_terms.append(jnp.einsum(
-            "pqf,pqd->fd", hiddens[micro_no], own_grad, preferred_element_type=jnp.float32
-        ))
-    first_grad = sum(first_terms[1:], first_terms[0]).astype(jnp.bfloat16)
-    second_grad = sum(second_terms[1:], second_terms[0]).astype(jnp.bfloat16)
+    first_grad = jnp.einsum(
+        "mpqd,mpqf->df", jnp.stack(recv_inputs), pre_keep[:micro_count], preferred_element_type=jnp.float32
+    ).astype(jnp.bfloat16)
+    second_grad = jnp.einsum(
+        "mpqf,mpqd->fd", jnp.stack(hiddens), grad_keep[:micro_count], preferred_element_type=jnp.float32
+    ).astype(jnp.bfloat16)
     return (grad_in, first_grad[None, None], second_grad[None, None])
 
 

time: 706 us -> 703 us (level)
  blocking collectives: 200 us -> 137 us
  waiting for transfers between devices: 256 us -> 311 us
  matrix products: 119 us -> 83 us
  local copies, waits for them, and re-layouts: 39.4 us -> 64.5 us
  starting transfers between devices: 60.2 us -> 73.3 us
    all_to_all x5 -> x4, blocking collectives: 200 us -> 137 us  [exchange(): lax.all_to_all(rows, 'expert', split_axis=0, concat_axis=0, tiled=True)]
    all_to_all x7 -> x8, waiting for transfers between devices: 215 us -> 270 us  [exchange(): lax.all_to_all(rows, 'expert', split_axis=0, concat_axis=0, tiled=True)]
    dot_general x6 -> x2, matrix products: 49.8 us -> 12.6 us  [the longest x1 6.64 us: on_device(): jnp.einsum('mpqd,mpqf->df', jnp.stack(recv_inputs), pre_keep[:micro_count...]
    dynamic_update_slice x0 -> x6, local copies, waits for them, and re-layouts: none -> 14.4 us  [on_device(): lax.dynamic_update_slice_in_dim(grad_keep, grad_recv[None], keep_at, 0)]
    all_to_all x7 -> x8, starting transfers between devices: 45.1 us -> 57.8 us  [exchange(): lax.all_to_all(rows, 'expert', split_axis=0, concat_axis=0, tiled=True)]
  transfers between devices with their start and end apart: 16 -> 17, of which waited for: 12 -> 14; matrix products, arithmetic and copies ran while one was open for 10% -> 8% of each run, Pallas kernels for 0% -> 0%
where the time goes in v4:
time: 703 us; the launch traced here: 697 us
  waiting for transfers between devices  311 us (44%)
  blocking collectives  137 us (19%)
  matrix products  83 us (12%)
  starting transfers between devices  73.3 us (10%)
  local copies, waits for them, and re-layouts  64.5 us (9%)
  between operations  15.1 us (2%)
  other arithmetic  12.9 us (2%)
    all_to_all x8, waiting for transfers between devices, exchange(): lax.all_to_all(rows, 'expert', split_axis=0, concat_axis=0, tiled=True)  270 us
    all_to_all x4, blocking collectives, exchange(): lax.all_to_all(rows, 'expert', split_axis=0, concat_axis=0, tiled=True)  137 us
    all_to_all x8, starting transfers between devices, exchange(): lax.all_to_all(rows, 'expert', split_axis=0, concat_axis=0, tiled=True)  57.8 us
    ppermute x5, waiting for transfers between devices, shifted(): lax.ppermute(value, axis, [(source, source + steps) for source in range(f...  36.4 us
    dot_general x6, matrix products, on_device(): jnp.einsum('pqd,fd->pqf', grad_recv, second_weights, preferred_element_ty...  24.5 us
    dot_general x6, matrix products, on_device(): jnp.einsum('pqk,pqd->kd', token_stack[micro_id], returned, preferred_elem...  18.1 us
    dynamic_update_slice x6, local copies, waits for them, and re-layouts, on_device(): lax.dynamic_update_slice_in_dim(grad_keep, grad_recv[None], keep_at, 0)  14.4 us
  transfers between devices with their start and end apart: 17, of which 14 were waited for; matrix products, arithmetic and copies ran while one was open for 8% of the time, Pallas kernels for 0%

profile of v4, /device:TPU:8, one launch (start us, length us, event | category | flops | bytes accessed | tf_op | source)
XLA Modules:
  0.0 696.6 jit_solution(4110516001540046619)
XLA Ops:
  7.2 5.6 collective-permute-start
  35.5 12.6 %all-to-all-start = ((bf16[64,8,2048]{2,1,0:T(8,128)(2,1)}), bf16[64,8,2048]{2,1,0:T(8,128)(2,1)}, u32[]{:S(2)}, u32[]{:S(2)}) async-start(bf16[64,8,2048]{2,1,0:T(8,128)(2,1)} %copy.46), calls=%async_computation | async-start | bytes 4194304 | tf_op jit(solution)/shard_map/all_to_all | solution.py:37
  48.1 51.0 %all-to-all-done = bf16[64,8,2048]{2,1,0:T(8,128)(2,1)} async-done(((bf16[64,8,2048]{2,1,0:T(8,128)(2,1)}), bf16[64,8,2048]{2,1,0:T(8,128)(2,1)}, u32[]{:S(2)}, u32[]{:S(2)}) %all-to-all-start) | async-done | bytes 2097184 | tf_op jit(solution)/shard_map/all_to_all | solution.py:37
  110.9 5.6 all-to-all-start.1
  118.1 27.1 %all-to-all-done.1 = bf16[64,4,2048]{2,1,0:T(4,128)(2,1)} async-done(((bf16[64,4,2048]{2,1,0:T(4,128)(2,1)}), bf16[64,4,2048]{2,1,0:T(4,128)(2,1)}, u32[]{:S(2)}, u32[]{:S(2)}) %all-to-all-start.1) | async-done | bytes 1048608 | tf_op jit(solution)/shard_map/all_to_all | solution.py:37
  151.2 6.5 collective-permute-done.3
  162.4 6.6 all-to-all-start.2
  169.0 51.1 %all-to-all-done.2 = bf16[64,8,2048]{2,1,0:T(8,128)(2,1)} async-done(((bf16[64,8,2048]{2,1,0:T(8,128)(2,1)}), bf16[64,8,2048]{2,1,0:T(8,128)(2,1)}, u32[]{:S(2)}, u32[]{:S(2)}) %all-to-all-start.2) | async-done | bytes 2097184 | tf_op jit(solution)/shard_map/all_to_all | solution.py:37
  230.6 34.0 %all_to_all.60 = bf16[64,4,2048]{2,1,0:T(4,128)(2,1)S(1)} all-to-all(bf16[64,4,2048]{2,1,0:T(4,128)(2,1)S(1)} %copy.55), channel_id=1, replica_groups=mesh['pipe'=4,'expert'=64] {'expert'}, dimensions={0} | all-to-all | bytes 2097152 | tf_op jit(solution)/shard_map/all_to_all | solution.py:37
  270.8 6.1 collective-permute-done.4
  281.6 6.6 all-to-all-start.4
  288.2 51.1 %all-to-all-done.4 = bf16[64,8,2048]{2,1,0:T(8,128)(2,1)} async-done(((bf16[64,8,2048]{2,1,0:T(8,128)(2,1)}), bf16[64,8,2048]{2,1,0:T(8,128)(2,1)}, u32[]{:S(2)}, u32[]{:S(2)}) %all-to-all-start.4) | async-done | bytes 2097184 | tf_op jit(solution)/shard_map/all_to_all | solution.py:37
  350.3 34.2 %all_to_all.61 = bf16[64,4,2048]{2,1,0:T(4,128)(2,1)S(1)} all-to-all(bf16[64,4,2048]{2,1,0:T(4,128)(2,1)S(1)} %copy.61), channel_id=1, replica_groups=mesh['pipe'=4,'expert'=64] {'expert'}, dimensions={0} | all-to-all | bytes 2097152 | tf_op jit(solution)/shard_map/all_to_all | solution.py:37
  388.7 8.0 %collective-permute-done.5 = bf16[64,2048]{1,0:T(8,128)(2,1)} collective-permute-done((bf16[64,2048]{1,0:T(8,128)(2,1)}, bf16[64,2048]{1,0:T(8,128)(2,1)}, u32[]{:S(2)}, u32[]{:S(2)}) %collective-permute-start.5) | collective-permute-done | bytes 262176 | tf_op jit(solution)/shard_map/ppermute | solution.py:10
  400.5 6.6 all-to-all-start.6
  407.1 28.7 %all-to-all-done.6 = bf16[64,4,2048]{2,1,0:T(4,128)(2,1)} async-done(((bf16[64,4,2048]{2,1,0:T(4,128)(2,1)}), bf16[64,4,2048]{2,1,0:T(4,128)(2,1)}, u32[]{:S(2)}, u32[]{:S(2)}) %all-to-all-start.6) | async-done | bytes 1048608 | tf_op jit(solution)/shard_map/all_to_all | solution.py:37
  435.8 5.3 bitcast_dynamic-update-slice_fusion.8
  443.0 34.2 %all_to_all.62 = bf16[64,4,2048]{2,1,0:T(4,128)(2,1)S(1)} all-to-all(bf16[64,4,2048]{2,1,0:T(4,128)(2,1)S(1)} %copy.66), channel_id=1, replica_groups=mesh['pipe'=4,'expert'=64] {'expert'}, dimensions={0} | all-to-all | bytes 2097152 | tf_op jit(solution)/shard_map/all_to_all | solution.py:37
  481.8 7.8 %collective-permute-done.6 = bf16[64,2048]{1,0:T(8,128)(2,1)} collective-permute-done((bf16[64,2048]{1,0:T(8,128)(2,1)}, bf16[64,2048]{1,0:T(8,128)(2,1)}, u32[]{:S(2)}, u32[]{:S(2)}) %collective-permute-start.6) | collective-permute-done | bytes 262176 | tf_op jit(solution)/shard_map/ppermute | solution.py:10
  493.3 6.6 all-to-all-start.8
  499.9 28.7 %all-to-all-done.8 = bf16[64,4,2048]{2,1,0:T(4,128)(2,1)} async-done(((bf16[64,4,2048]{2,1,0:T(4,128)(2,1)}), bf16[64,4,2048]{2,1,0:T(4,128)(2,1)}, u32[]{:S(2)}, u32[]{:S(2)}) %all-to-all-start.8) | async-done | bytes 1048608 | tf_op jit(solution)/shard_map/all_to_all | solution.py:37
  528.6 5.3 bitcast_dynamic-update-slice_fusion.7
  535.8 34.2 %all_to_all.63 = bf16[64,4,2048]{2,1,0:T(4,128)(2,1)S(1)} all-to-all(bf16[64,4,2048]{2,1,0:T(4,128)(2,1)S(1)} %copy.71), channel_id=1, replica_groups=mesh['pipe'=4,'expert'=64] {'expert'}, dimensions={0} | all-to-all | bytes 2097152 | tf_op jit(solution)/shard_map/all_to_all | solution.py:37
  574.4 8.0 %collective-permute-done.7 = bf16[64,2048]{1,0:T(8,128)(2,1)} collective-permute-done((bf16[64,2048]{1,0:T(8,128)(2,1)}, bf16[64,2048]{1,0:T(8,128)(2,1)}, u32[]{:S(2)}, u32[]{:S(2)}) %collective-permute-start.7) | collective-permute-done | bytes 262176 | tf_op jit(solution)/shard_map/ppermute | solution.py:10
  586.1 7.2 %all-to-all-start.10 = ((bf16[64,4,2048]{2,1,0:T(4,128)(2,1)}), bf16[64,4,2048]{2,1,0:T(4,128)(2,1)}, u32[]{:S(2)}, u32[]{:S(2)}) async-start(bf16[64,4,2048]{2,1,0:T(4,128)(2,1)} %copy.74), calls=%async_computation.10 | async-start | bytes 2097152 | tf_op jit(solution)/shard_map/all_to_all | solution.py:37
  601.6 20.2 %all-to-all-done.10 = bf16[64,4,2048]{2,1,0:T(4,128)(2,1)} async-done(((bf16[64,4,2048]{2,1,0:T(4,128)(2,1)}), bf16[64,4,2048]{2,1,0:T(4,128)(2,1)}, u32[]{:S(2)}, u32[]{:S(2)}) %all-to-all-start.10) | async-done | bytes 1048608 | tf_op jit(solution)/shard_map/all_to_all | solution.py:37
  621.8 5.3 bitcast_dynamic-update-slice_fusion.6
  630.0 5.9 all-to-all-start.11
  652.6 12.0 %all-to-all-done.11 = bf16[64,4,2048]{2,1,0:T(4,128)(2,1)} async-done(((bf16[64,4,2048]{2,1,0:T(4,128)(2,1)}), bf16[64,4,2048]{2,1,0:T(4,128)(2,1)}, u32[]{:S(2)}, u32[]{:S(2)}) %all-to-all-start.11) | async-done | bytes 1048608 | tf_op jit(solution)/shard_map/all_to_all | solution.py:37
  669.3 6.6 fusion.36
  678.8 5.9 fusion.39
  684.7 4.8 reduce-scatter.2.cloned.1.call-done
  (188 shorter events, 141.7 us)
Async XLA Ops:
  7.2 97.6 %copy-start = (bf16[1,1,768,2048]{3,2,1,0:T(8,128)(2,1)S(1)}, bf16[1,1,768,2048]{3,2,1,0:T(8,128)(2,1)}, u32[]{:S(2)}) copy-start(bf16[1,1,768,2048]{3,2,1,0:T(8,128)(2,1)} %param.10) | copy-start | bytes 9437188
  7.2 19.9 %collective-permute-start = (bf16[3,64,512]{2,1,0:T(8,128)(2,1)}, bf16[3,64,512]{2,1,0:T(8,128)(2,1)}, u32[]{:S(2)}, u32[]{:S(2)}) collective-permute-start(bf16[3,64,512]{2,1,0:T(8,128)(2,1)} %param.11), channel_id=1, source_target_pairs={{0,192},{1,193},{2,194},{3,195},{4,196},{5,197},{6,198},{7,199},{8... | collective-permute-start | bytes 589832 | tf_op jit(solution)/shard_map/ppermute | solution.py:66
  12.8 15.3 %collective-permute-start.1 = (bf16[3,64,512]{2,1,0:T(8,128)(2,1)}, bf16[3,64,512]{2,1,0:T(8,128)(2,1)}, u32[]{:S(2)}, u32[]{:S(2)}) collective-permute-start(bf16[3,64,512]{2,1,0:T(8,128)(2,1)} %param.11), channel_id=1, source_target_pairs={{64,192},{65,193},{66,194},{67,195},{68,196},{69,197},{70,198},{71... | collective-permute-start | bytes 589832 | tf_op jit(solution)/shard_map/ppermute | solution.py:66
  14.1 14.9 %collective-permute-start.2 = (bf16[3,64,512]{2,1,0:T(8,128)(2,1)}, bf16[3,64,512]{2,1,0:T(8,128)(2,1)}, u32[]{:S(2)}, u32[]{:S(2)}) collective-permute-start(bf16[3,64,512]{2,1,0:T(8,128)(2,1)} %param.11), channel_id=1, source_target_pairs={{128,192},{129,193},{130,194},{131,195},{132,196},{133,197},{134,1... | collective-permute-start | bytes 589832 | tf_op jit(solution)/shard_map/ppermute | solution.py:66
  21.4 4.6 copy-start.23
  21.7 4.2 copy-start.24
  21.7 4.2 copy-start.25
  21.7 4.2 copy-start.26
  25.9 6.9 copy-start.7
  35.5 63.6 %all-to-all-start = ((bf16[64,8,2048]{2,1,0:T(8,128)(2,1)}), bf16[64,8,2048]{2,1,0:T(8,128)(2,1)}, u32[]{:S(2)}, u32[]{:S(2)}) async-start(bf16[64,8,2048]{2,1,0:T(8,128)(2,1)} %copy.46), calls=%async_computation | async-start | bytes 4194304 | tf_op jit(solution)/shard_map/all_to_all | solution.py:37
  110.9 34.3 %all-to-all-start.1 = ((bf16[64,4,2048]{2,1,0:T(4,128)(2,1)}), bf16[64,4,2048]{2,1,0:T(4,128)(2,1)}, u32[]{:S(2)}, u32[]{:S(2)}) async-start(bf16[64,4,2048]{2,1,0:T(4,128)(2,1)} %copy.49), calls=%async_computation.1 | async-start | bytes 2097152 | tf_op jit(solution)/shard_map/all_to_all | solution.py:37
  148.5 9.3 %collective-permute-start.3 = (bf16[64,2048]{1,0:T(8,128)(2,1)}, bf16[64,2048]{1,0:T(8,128)(2,1)}, u32[]{:S(2)}, u32[]{:S(2)}) collective-permute-start(bf16[64,2048]{1,0:T(8,128)(2,1)} %fusion.61), channel_id=1, source_target_pairs={{64,0},{128,64},{192,128},{65,1},{129,65},{193,129},{66,2},{130,66... | collective-permute-start | bytes 786440 | tf_op jit(solution)/shard_map/ppermute | solution.py:10
  162.4 57.8 %all-to-all-start.2 = ((bf16[64,8,2048]{2,1,0:T(8,128)(2,1)}), bf16[64,8,2048]{2,1,0:T(8,128)(2,1)}, u32[]{:S(2)}, u32[]{:S(2)}) async-start(bf16[64,8,2048]{2,1,0:T(8,128)(2,1)} %copy.52), calls=%async_computation.2 | async-start | bytes 4194304 | tf_op jit(solution)/shard_map/all_to_all | solution.py:37
  267.7 9.3 %collective-permute-start.4 = (bf16[64,2048]{1,0:T(8,128)(2,1)}, bf16[64,2048]{1,0:T(8,128)(2,1)}, u32[]{:S(2)}, u32[]{:S(2)}) collective-permute-start(bf16[64,2048]{1,0:T(8,128)(2,1)} %add_convert_fusion.4), channel_id=1, source_target_pairs={{64,0},{128,64},{192,128},{65,1},{129,65},{193,129},{66,2},{130,66... | collective-permute-start | bytes 786440 | tf_op jit(solution)/shard_map/ppermute | solution.py:10
  281.6 57.8 %all-to-all-start.4 = ((bf16[64,8,2048]{2,1,0:T(8,128)(2,1)}), bf16[64,8,2048]{2,1,0:T(8,128)(2,1)}, u32[]{:S(2)}, u32[]{:S(2)}) async-start(bf16[64,8,2048]{2,1,0:T(8,128)(2,1)} %copy.58), calls=%async_computation.4 | async-start | bytes 4194304 | tf_op jit(solution)/shard_map/all_to_all | solution.py:37
  387.4 9.3 %collective-permute-start.5 = (bf16[64,2048]{1,0:T(8,128)(2,1)}, bf16[64,2048]{1,0:T(8,128)(2,1)}, u32[]{:S(2)}, u32[]{:S(2)}) collective-permute-start(bf16[64,2048]{1,0:T(8,128)(2,1)} %add_convert_fusion.3), channel_id=1, source_target_pairs={{64,0},{128,64},{192,128},{65,1},{129,65},{193,129},{66,2},{130,66... | collective-permute-start | bytes 786440 | tf_op jit(solution)/shard_map/ppermute | solution.py:10
  400.5 35.3 %all-to-all-start.6 = ((bf16[64,4,2048]{2,1,0:T(4,128)(2,1)}), bf16[64,4,2048]{2,1,0:T(4,128)(2,1)}, u32[]{:S(2)}, u32[]{:S(2)}) async-start(bf16[64,4,2048]{2,1,0:T(4,128)(2,1)} %copy.64), calls=%async_computation.6 | async-start | bytes 2097152 | tf_op jit(solution)/shard_map/all_to_all | solution.py:37
  435.8 5.4 copy-start.31
  480.3 9.3 %collective-permute-start.6 = (bf16[64,2048]{1,0:T(8,128)(2,1)}, bf16[64,2048]{1,0:T(8,128)(2,1)}, u32[]{:S(2)}, u32[]{:S(2)}) collective-permute-start(bf16[64,2048]{1,0:T(8,128)(2,1)} %add_convert_fusion.2), channel_id=1, source_target_pairs={{64,0},{128,64},{192,128},{65,1},{129,65},{193,129},{66,2},{130,66... | collective-permute-start | bytes 786440 | tf_op jit(solution)/shard_map/ppermute | solution.py:10
  493.3 35.3 %all-to-all-start.8 = ((bf16[64,4,2048]{2,1,0:T(4,128)(2,1)}), bf16[64,4,2048]{2,1,0:T(4,128)(2,1)}, u32[]{:S(2)}, u32[]{:S(2)}) async-start(bf16[64,4,2048]{2,1,0:T(4,128)(2,1)} %copy.69), calls=%async_computation.8 | async-start | bytes 2097152 | tf_op jit(solution)/shard_map/all_to_all | solution.py:37
  528.6 5.4 copy-start.32
  573.1 9.3 %collective-permute-start.7 = (bf16[64,2048]{1,0:T(8,128)(2,1)}, bf16[64,2048]{1,0:T(8,128)(2,1)}, u32[]{:S(2)}, u32[]{:S(2)}) collective-permute-start(bf16[64,2048]{1,0:T(8,128)(2,1)} %add_convert_fusion.1), channel_id=1, source_target_pairs={{64,0},{128,64},{192,128},{65,1},{129,65},{193,129},{66,2},{130,66... | collective-permute-start | bytes 786440 | tf_op jit(solution)/shard_map/ppermute | solution.py:10
  586.1 35.7 %all-to-all-start.10 = ((bf16[64,4,2048]{2,1,0:T(4,128)(2,1)}), bf16[64,4,2048]{2,1,0:T(4,128)(2,1)}, u32[]{:S(2)}, u32[]{:S(2)}) async-start(bf16[64,4,2048]{2,1,0:T(4,128)(2,1)} %copy.74), calls=%async_computation.10 | async-start | bytes 2097152 | tf_op jit(solution)/shard_map/all_to_all | solution.py:37
  621.8 5.3 copy-start.33
  630.0 34.6 %all-to-all-start.11 = ((bf16[64,4,2048]{2,1,0:T(4,128)(2,1)}), bf16[64,4,2048]{2,1,0:T(4,128)(2,1)}, u32[]{:S(2)}, u32[]{:S(2)}) async-start(bf16[64,4,2048]{2,1,0:T(4,128)(2,1)} %copy.76), calls=%async_computation.11 | async-start | bytes 2097152 | tf_op jit(solution)/shard_map/all_to_all | solution.py:37
  635.9 53.7 %reduce-scatter.2.cloned.1.call-start = ((), (), s32[]{:S(2)}) async-start(), calls=%async_computation.13 | async-start | bytes 983040 | tf_op jit(solution)/shard_map/reduce_scatter | solution.py:134
  636.1 5.9 copy-start.18
  636.1 6.8 copy-start.11
  639.0 5.5 copy-start.20
  639.0 6.4 copy-start.6
  669.3 9.5 %copy-start.21 = (bf16[1,64,4,768]{3,1,2,0:T(8,128)(2,1)S(1)}, bf16[1,64,4,768]{3,1,2,0:T(8,128)(2,1)}, u32[]{:S(2)}) copy-start(bf16[1,64,4,768]{3,1,2,0:T(8,128)(2,1)} %fusion.120) | copy-start | bytes 1179652
  669.3 9.5 %copy-start.22 = (bf16[1,64,4,768]{3,1,2,0:T(8,128)(2,1)S(1)}, bf16[1,64,4,768]{3,1,2,0:T(8,128)(2,1)}, u32[]{:S(2)}) copy-start(bf16[1,64,4,768]{3,1,2,0:T(8,128)(2,1)} %fusion.121) | copy-start | bytes 1179652
  (19 other events, 47.7 us)
Sparse Core Ops, SparseCore 0:
  669.4 20.0 reduce-scatter.1

commit v5 on v4

--- a/solution.py
+++ b/solution.py
@@ -75,7 +75,34 @@
     token_stack = jnp.stack(token_tables)
     gate_stack = jnp.stack(gate_tables)
 
+    above_inputs = shifted(inputs_dev, "pipe", -1)
+    above_routes = shifted(routes[0], "pipe", -1)
+    above_tables = [
+        placement_tables(above_routes[micro_no], gates[0, micro_no], owners, capacity)[0]
+        for micro_no in range(micro_count)
+    ]
+    is_last = section_id == section_count - 1
+    is_first = section_id == 0
+
+    def slot_rows(table, source):
+        return jnp.einsum(
+            "pqk,kd->pqd",
+            table,
+            source,
+            precision=lax.Precision.HIGHEST,
+            preferred_element_type=jnp.float32,
+        ).astype(jnp.bfloat16)
+
     recv_inputs, slopes, hiddens = [], [], []
+
+    def add_inputs(input_recv):
+        preactivation = jnp.einsum(
+            "pqd,df->pqf", input_recv, first_weights, preferred_element_type=jnp.float32
+        )
+        recv_inputs.append(input_recv)
+        slopes.append(silu_slope(preactivation))
+        hiddens.append(jax.nn.silu(preactivation).astype(jnp.bfloat16))
+
     incoming = jnp.zeros((tokens_dev, model_width), jnp.bfloat16)
     pre_keep = jnp.zeros((micro_count + 1, owners, capacity, first_weights.shape[1]), jnp.bfloat16)
     grad_keep = jnp.zeros((micro_count + 1, owners, capacity, model_width), jnp.bfloat16)
@@ -84,31 +111,26 @@
         offset = tick_no - first_tick
         micro_id = jnp.clip(offset, 0, micro_count - 1)
         grad_now = jnp.where(section_id == section_count - 1, upstream[micro_id], incoming)
-        gradient_slots = jnp.einsum(
-            "pqk,kd->pqd",
-            gate_stack[micro_id],
-            grad_now.astype(jnp.float32),
-            precision=lax.Precision.HIGHEST,
-            preferred_element_type=jnp.float32,
-        ).astype(jnp.bfloat16)
-        if tick_no < micro_count:
-            input_slots = jnp.einsum(
-                "pqk,kd->pqd",
-                token_tables[tick_no],
-                inputs_dev[tick_no],
-                preferred_element_type=jnp.float32,
+        if tick_no == 0:
+            first_half = slot_rows(
+                jnp.where(is_last, gate_stack[micro_id], above_tables[1].astype(jnp.float32)),
+                jnp.where(is_last, grad_now, above_inputs[1]).astype(jnp.float32),
+            )
+            own_inputs = jnp.einsum(
+                "pqk,kd->pqd", token_tables[0], inputs_dev[0], preferred_element_type=jnp.float32
             ).astype(jnp.bfloat16)
-            both = exchange(jnp.concatenate([gradient_slots, input_slots], axis=1))
+            both = exchange(jnp.concatenate([first_half, own_inputs], axis=1))
             grad_recv = both[:, :capacity]
-            input_recv = both[:, capacity:]
-            preactivation = jnp.einsum(
-                "pqd,df->pqf", input_recv, first_weights, preferred_element_type=jnp.float32
-            )
-            recv_inputs.append(input_recv)
-            slopes.append(silu_slope(preactivation))
-            hiddens.append(jax.nn.silu(preactivation).astype(jnp.bfloat16))
+            from_below_1 = shifted(grad_recv, "pipe", 1)
+            add_inputs(both[:, capacity:])
+        elif tick_no == 1:
+            grad_recv = exchange(slot_rows(
+                jnp.where(is_first, token_tables[1].astype(jnp.float32), gate_stack[micro_id]),
+                jnp.where(is_first, inputs_dev[1], grad_now).astype(jnp.float32),
+            ))
+            add_inputs(jnp.where(is_first, grad_recv, from_below_1))
         else:
-            grad_recv = exchange(gradient_slots)
+            grad_recv = exchange(slot_rows(gate_stack[micro_id], grad_now.astype(jnp.float32)))
         hidden_grad = jnp.einsum(
             "pqd,fd->pqf", grad_recv, second_weights, preferred_element_type=jnp.float32
         )
@@ -116,7 +138,20 @@
         row_grads = jnp.einsum(
             "pqf,df->pqd", pre_grad, first_weights, preferred_element_type=jnp.float32
         ).astype(jnp.bfloat16)
-        returned = exchange(row_grads)
+        if tick_no == 0:
+            above_second = jnp.einsum(
+                "pqk,kd->pqd", above_tables[2], above_inputs[2], preferred_element_type=jnp.float32
+            ).astype(jnp.bfloat16)
+            returned = exchange(jnp.where(is_last, row_grads, above_second))
+            from_below_2 = shifted(returned, "pipe", 1)
+        elif tick_no == 1:
+            own_second = jnp.einsum(
+                "pqk,kd->pqd", token_tables[2], inputs_dev[2], preferred_element_type=jnp.float32
+            ).astype(jnp.bfloat16)
+            returned = exchange(jnp.where(is_first, own_second, row_grads))
+            add_inputs(jnp.where(is_first, returned, from_below_2))
+        else:
+            returned = exchange(row_grads)
         summed = jnp.einsum(
             "pqk,pqd->kd", token_stack[micro_id], returned, preferred_element_type=jnp.float32
         )

time: 703 us -> 713 us (1.014)
  waiting for transfers between devices: 311 us -> 255 us
  other arithmetic: 12.9 us -> 33.4 us
  starting transfers between devices: 73.3 us -> 85.9 us
  local copies, waits for them, and re-layouts: 64.5 us -> 75.6 us
  matrix products: 83 us -> 93.2 us
  blocking collectives: 137 us -> 146 us
    all_to_all x8, waiting for transfers between devices: 270 us -> 161 us  [exchange(): lax.all_to_all(rows, 'expert', split_axis=0, concat_axis=0, tiled=True)]
    ppermute x5 -> x9, waiting for transfers between devices: 36.4 us -> 87.6 us  [shifted(): lax.ppermute(value, axis, [(source, source + steps) for source in range(f...]
    another operation x6 -> x12, other arithmetic: 1.94 us -> 15.1 us
    ppermute x5 -> x9, starting transfers between devices: 7.02 us -> 18.6 us  [shifted(): lax.ppermute(value, axis, [(source, source + steps) for source in range(f...]
    all_to_all x4, blocking collectives: 137 us -> 146 us  [exchange(): lax.all_to_all(rows, 'expert', split_axis=0, concat_axis=0, tiled=True)]
  transfers between devices with their start and end apart: 17 -> 21, of which waited for: 14 -> 14; matrix products, arithmetic and copies ran while one was open for 8% -> 15% of each run, Pallas kernels for 0% -> 0%
where the time goes in v5:
time: 713 us; the launch traced here: 705 us
  waiting for transfers between devices  255 us (36%)
  blocking collectives  146 us (20%)
  matrix products  93.2 us (13%)
  starting transfers between devices  85.9 us (12%)
  local copies, waits for them, and re-layouts  75.6 us (11%)
  other arithmetic  33.4 us (5%)
  between operations  15.2 us (2%)
    all_to_all x8, waiting for transfers between devices, exchange(): lax.all_to_all(rows, 'expert', split_axis=0, concat_axis=0, tiled=True)  161 us
    all_to_all x4, blocking collectives, exchange(): lax.all_to_all(rows, 'expert', split_axis=0, concat_axis=0, tiled=True)  146 us
    ppermute x9, waiting for transfers between devices, shifted(): lax.ppermute(value, axis, [(source, source + steps) for source in range(f...  87.6 us
    all_to_all x8, starting transfers between devices, exchange(): lax.all_to_all(rows, 'expert', split_axis=0, concat_axis=0, tiled=True)  58.9 us
    dot_general x6, matrix products, on_device(): jnp.einsum('pqd,fd->pqf', grad_recv, second_weights, preferred_element_ty...  28 us
    ppermute x9, starting transfers between devices, shifted(): lax.ppermute(value, axis, [(source, source + steps) for source in range(f...  18.6 us
    dot_general x6, matrix products, on_device(): jnp.einsum('pqk,pqd->kd', token_stack[micro_id], returned, preferred_elem...  18 us
    dynamic_update_slice x6, local copies, waits for them, and re-layouts, on_device(): lax.dynamic_update_slice_in_dim(grad_keep, grad_recv[None], keep_at, 0)  15.6 us
  transfers between devices with their start and end apart: 21, of which 14 were waited for; matrix products, arithmetic and copies ran while one was open for 15% of the time, Pallas kernels for 0%

profile of v5, /device:TPU:8, one launch (start us, length us, event | category | flops | bytes accessed | tf_op | source)
XLA Modules:
  0.0 704.7 jit_solution(13824889670098382005)
XLA Ops:
  8.7 5.4 collective-permute-start
  68.0 12.9 %all-to-all-start = ((bf16[64,8,2048]{2,1,0:T(8,128)(2,1)}), bf16[64,8,2048]{2,1,0:T(8,128)(2,1)}, u32[]{:S(2)}, u32[]{:S(2)}) async-start(bf16[64,8,2048]{2,1,0:T(8,128)(2,1)} %copy.54), calls=%async_computation | async-start | bytes 4194304 | tf_op jit(solution)/shard_map/all_to_all | solution.py:37
  82.7 49.2 %all-to-all-done = bf16[64,8,2048]{2,1,0:T(8,128)(2,1)} async-done(((bf16[64,8,2048]{2,1,0:T(8,128)(2,1)}), bf16[64,8,2048]{2,1,0:T(8,128)(2,1)}, u32[]{:S(2)}, u32[]{:S(2)}) %all-to-all-start) | async-done | bytes 2097184 | tf_op jit(solution)/shard_map/all_to_all | solution.py:37
  144.0 5.6 all-to-all-start.1
  151.3 27.1 %all-to-all-done.1 = bf16[64,4,2048]{2,1,0:T(4,128)(2,1)} async-done(((bf16[64,4,2048]{2,1,0:T(4,128)(2,1)}), bf16[64,4,2048]{2,1,0:T(4,128)(2,1)}, u32[]{:S(2)}, u32[]{:S(2)}) %all-to-all-start.1) | async-done | bytes 1048608 | tf_op jit(solution)/shard_map/all_to_all | solution.py:37
  182.9 9.5 %collective-permute-done.5 = bf16[64,2048]{1,0:T(8,128)(2,1)} collective-permute-done((bf16[64,2048]{1,0:T(8,128)(2,1)}, bf16[64,2048]{1,0:T(8,128)(2,1)}, u32[]{:S(2)}, u32[]{:S(2)}) %collective-permute-start.5) | collective-permute-done | bytes 262176 | tf_op jit(solution)/shard_map/ppermute | solution.py:10
  196.4 6.6 all-to-all-start.2
  210.7 22.0 %collective-permute-done.6 = bf16[64,4,2048]{2,0,1:T(8,128)(2,1)} collective-permute-done((bf16[64,4,2048]{2,0,1:T(8,128)(2,1)}, bf16[64,4,2048]{2,0,1:T(8,128)(2,1)}, u32[]{:S(2)}, u32[]{:S(2)}) %collective-permute-start.6) | collective-permute-done | bytes 1048608 | tf_op jit(solution)/shard_map/ppermute | solution.py:10
  244.9 38.9 %all_to_all.60 = bf16[64,4,2048]{2,1,0:T(4,128)(2,1)S(1)} all-to-all(bf16[64,4,2048]{2,1,0:T(4,128)(2,1)S(1)} %copy.64), channel_id=1, replica_groups=mesh['pipe'=4,'expert'=64] {'expert'}, dimensions={0} | all-to-all | bytes 2097152 | tf_op jit(solution)/shard_map/all_to_all | solution.py:37
  289.2 9.0 %collective-permute-done.7 = bf16[64,2048]{1,0:T(8,128)(2,1)} collective-permute-done((bf16[64,2048]{1,0:T(8,128)(2,1)}, bf16[64,2048]{1,0:T(8,128)(2,1)}, u32[]{:S(2)}, u32[]{:S(2)}) %collective-permute-start.7) | collective-permute-done | bytes 262176 | tf_op jit(solution)/shard_map/ppermute | solution.py:10
  302.0 6.6 all-to-all-start.4
  316.1 21.9 %collective-permute-done.8 = bf16[64,4,2048]{2,0,1:T(8,128)(2,1)} collective-permute-done((bf16[64,4,2048]{2,0,1:T(8,128)(2,1)}, bf16[64,4,2048]{2,0,1:T(8,128)(2,1)}, u32[]{:S(2)}, u32[]{:S(2)}) %collective-permute-start.8) | collective-permute-done | bytes 1048608 | tf_op jit(solution)/shard_map/ppermute | solution.py:10
  343.1 5.3 bitcast_dynamic-update-slice_fusion.9
  350.3 38.9 %all_to_all.61 = bf16[64,4,2048]{2,1,0:T(4,128)(2,1)S(1)} all-to-all(bf16[64,4,2048]{2,1,0:T(4,128)(2,1)S(1)} %copy.71), channel_id=1, replica_groups=mesh['pipe'=4,'expert'=64] {'expert'}, dimensions={0} | all-to-all | bytes 2097152 | tf_op jit(solution)/shard_map/all_to_all | solution.py:37
  393.5 9.1 %collective-permute-done.9 = bf16[64,2048]{1,0:T(8,128)(2,1)} collective-permute-done((bf16[64,2048]{1,0:T(8,128)(2,1)}, bf16[64,2048]{1,0:T(8,128)(2,1)}, u32[]{:S(2)}, u32[]{:S(2)}) %collective-permute-start.9) | collective-permute-done | bytes 262176 | tf_op jit(solution)/shard_map/ppermute | solution.py:10
  406.3 7.2 %all-to-all-start.6 = ((bf16[64,4,2048]{2,1,0:T(4,128)(2,1)}), bf16[64,4,2048]{2,1,0:T(4,128)(2,1)}, u32[]{:S(2)}, u32[]{:S(2)}) async-start(bf16[64,4,2048]{2,1,0:T(4,128)(2,1)} %copy.74), calls=%async_computation.6 | async-start | bytes 2097152 | tf_op jit(solution)/shard_map/all_to_all | solution.py:37
  413.5 28.5 %all-to-all-done.6 = bf16[64,4,2048]{2,1,0:T(4,128)(2,1)} async-done(((bf16[64,4,2048]{2,1,0:T(4,128)(2,1)}), bf16[64,4,2048]{2,1,0:T(4,128)(2,1)}, u32[]{:S(2)}, u32[]{:S(2)}) %all-to-all-start.6) | async-done | bytes 1048608 | tf_op jit(solution)/shard_map/all_to_all | solution.py:37
  449.2 34.2 %all_to_all.62 = bf16[64,4,2048]{2,1,0:T(4,128)(2,1)S(1)} all-to-all(bf16[64,4,2048]{2,1,0:T(4,128)(2,1)S(1)} %copy.76), channel_id=1, replica_groups=mesh['pipe'=4,'expert'=64] {'expert'}, dimensions={0} | all-to-all | bytes 2097152 | tf_op jit(solution)/shard_map/all_to_all | solution.py:37
  487.7 8.0 %collective-permute-done.10 = bf16[64,2048]{1,0:T(8,128)(2,1)} collective-permute-done((bf16[64,2048]{1,0:T(8,128)(2,1)}, bf16[64,2048]{1,0:T(8,128)(2,1)}, u32[]{:S(2)}, u32[]{:S(2)}) %collective-permute-start.10) | collective-permute-done | bytes 262176 | tf_op jit(solution)/shard_map/ppermute | solution.py:10
  499.5 7.0 all-to-all-start.8
  506.5 28.5 %all-to-all-done.8 = bf16[64,4,2048]{2,1,0:T(4,128)(2,1)} async-done(((bf16[64,4,2048]{2,1,0:T(4,128)(2,1)}), bf16[64,4,2048]{2,1,0:T(4,128)(2,1)}, u32[]{:S(2)}, u32[]{:S(2)}) %all-to-all-start.8) | async-done | bytes 1048608 | tf_op jit(solution)/shard_map/all_to_all | solution.py:37
  535.0 5.3 bitcast_dynamic-update-slice_fusion.7
  542.1 34.2 %all_to_all.63 = bf16[64,4,2048]{2,1,0:T(4,128)(2,1)S(1)} all-to-all(bf16[64,4,2048]{2,1,0:T(4,128)(2,1)S(1)} %copy.81), channel_id=1, replica_groups=mesh['pipe'=4,'expert'=64] {'expert'}, dimensions={0} | all-to-all | bytes 2097152 | tf_op jit(solution)/shard_map/all_to_all | solution.py:37
  580.7 8.0 %collective-permute-done.11 = bf16[64,2048]{1,0:T(8,128)(2,1)} collective-permute-done((bf16[64,2048]{1,0:T(8,128)(2,1)}, bf16[64,2048]{1,0:T(8,128)(2,1)}, u32[]{:S(2)}, u32[]{:S(2)}) %collective-permute-start.11) | collective-permute-done | bytes 262176 | tf_op jit(solution)/shard_map/ppermute | solution.py:10
  592.5 7.0 all-to-all-start.10
  614.9 13.1 %all-to-all-done.10 = bf16[64,4,2048]{2,1,0:T(4,128)(2,1)} async-done(((bf16[64,4,2048]{2,1,0:T(4,128)(2,1)}), bf16[64,4,2048]{2,1,0:T(4,128)(2,1)}, u32[]{:S(2)}, u32[]{:S(2)}) %all-to-all-start.10) | async-done | bytes 1048608 | tf_op jit(solution)/shard_map/all_to_all | solution.py:37
  628.0 5.3 bitcast_dynamic-update-slice_fusion.6
  636.1 5.9 all-to-all-start.11
  656.2 14.5 %all-to-all-done.11 = bf16[64,4,2048]{2,1,0:T(4,128)(2,1)} async-done(((bf16[64,4,2048]{2,1,0:T(4,128)(2,1)}), bf16[64,4,2048]{2,1,0:T(4,128)(2,1)}, u32[]{:S(2)}, u32[]{:S(2)}) %all-to-all-start.11) | async-done | bytes 1048608 | tf_op jit(solution)/shard_map/all_to_all | solution.py:37
  675.4 6.6 fusion.36
  684.8 5.9 fusion.39
  690.7 6.9 reduce-scatter.2.cloned.1.call-done
  (210 shorter events, 195.2 us)
Async XLA Ops:
  7.2 130.4 %copy-start = (bf16[1,1,768,2048]{3,2,1,0:T(8,128)(2,1)S(1)}, bf16[1,1,768,2048]{3,2,1,0:T(8,128)(2,1)}, u32[]{:S(2)}) copy-start(bf16[1,1,768,2048]{3,2,1,0:T(8,128)(2,1)} %param.10) | copy-start | bytes 9437188
  7.2 52.4 %collective-permute-start.1 = (bf16[3,64,512]{2,1,0:T(8,128)(2,1)}, bf16[3,64,512]{2,1,0:T(8,128)(2,1)}, u32[]{:S(2)}, u32[]{:S(2)}) collective-permute-start(bf16[3,64,512]{2,1,0:T(8,128)(2,1)} %param.11), channel_id=1, source_target_pairs={{64,192},{65,193},{66,194},{67,195},{68,196},{69,197},{70,198},{71... | collective-permute-start | bytes 589832 | tf_op jit(solution)/shard_map/ppermute | solution.py:66
  8.7 49.9 %collective-permute-start = (bf16[3,64,512]{2,1,0:T(8,128)(2,1)}, bf16[3,64,512]{2,1,0:T(8,128)(2,1)}, u32[]{:S(2)}, u32[]{:S(2)}) collective-permute-start(bf16[3,64,512]{2,1,0:T(8,128)(2,1)} %param.11), channel_id=1, source_target_pairs={{0,192},{1,193},{2,194},{3,195},{4,196},{5,197},{6,198},{7,199},{8... | collective-permute-start | bytes 589832 | tf_op jit(solution)/shard_map/ppermute | solution.py:66
  14.1 46.4 %collective-permute-start.2 = (bf16[3,64,512]{2,1,0:T(8,128)(2,1)}, bf16[3,64,512]{2,1,0:T(8,128)(2,1)}, u32[]{:S(2)}, u32[]{:S(2)}) collective-permute-start(bf16[3,64,512]{2,1,0:T(8,128)(2,1)} %param.11), channel_id=1, source_target_pairs={{128,192},{129,193},{130,194},{131,195},{132,196},{133,197},{134,1... | collective-permute-start | bytes 589832 | tf_op jit(solution)/shard_map/ppermute | solution.py:66
  16.9 13.6 %collective-permute-start.3 = (s32[3,64,4]{2,1,0:T(8,128)}, s32[3,64,4]{2,1,0:T(8,128)}, u32[]{:S(2)}, u32[]{:S(2)}) collective-permute-start(s32[3,64,4]{2,1,0:T(8,128)} %bitcast.26), channel_id=1, source_target_pairs={{64,0},{128,64},{192,128},{65,1},{129,65},{193,129},{66,2},{130,66... | collective-permute-start | bytes 9224 | tf_op jit(solution)/shard_map/ppermute | solution.py:10
  18.1 44.3 %collective-permute-start.4 = (bf16[3,64,2048]{2,1,0:T(8,128)(2,1)}, bf16[3,64,2048]{2,1,0:T(8,128)(2,1)}, u32[]{:S(2)}, u32[]{:S(2)}) collective-permute-start(bf16[3,64,2048]{2,1,0:T(8,128)(2,1)} %bitcast.431), channel_id=1, source_target_pairs={{64,0},{128,64},{192,128},{65,1},{129,65},{193,129},{66,2},{130,66... | collective-permute-start | bytes 2359304 | tf_op jit(solution)/shard_map/ppermute | solution.py:10
  25.9 4.4 copy-start.14
  56.8 8.4 %copy-start.5 = (bf16[64,4,2048]{2,0,1:T(8,128)(2,1)S(1)}, bf16[64,4,2048]{2,0,1:T(8,128)(2,1)}, u32[]{:S(2)}) copy-start(bf16[64,4,2048]{2,0,1:T(8,128)(2,1)} %convolution_convert_fusion.8) | copy-start | bytes 3145732
  68.0 63.9 %all-to-all-start = ((bf16[64,8,2048]{2,1,0:T(8,128)(2,1)}), bf16[64,8,2048]{2,1,0:T(8,128)(2,1)}, u32[]{:S(2)}, u32[]{:S(2)}) async-start(bf16[64,8,2048]{2,1,0:T(8,128)(2,1)} %copy.54), calls=%async_computation | async-start | bytes 4194304 | tf_op jit(solution)/shard_map/all_to_all | solution.py:37
  144.0 34.3 %all-to-all-start.1 = ((bf16[64,4,2048]{2,1,0:T(4,128)(2,1)}), bf16[64,4,2048]{2,1,0:T(4,128)(2,1)}, u32[]{:S(2)}, u32[]{:S(2)}) async-start(bf16[64,4,2048]{2,1,0:T(4,128)(2,1)} %copy.58), calls=%async_computation.1 | async-start | bytes 2097152 | tf_op jit(solution)/shard_map/all_to_all | solution.py:37
  181.6 10.8 %collective-permute-start.5 = (bf16[64,2048]{1,0:T(8,128)(2,1)}, bf16[64,2048]{1,0:T(8,128)(2,1)}, u32[]{:S(2)}, u32[]{:S(2)}) collective-permute-start(bf16[64,2048]{1,0:T(8,128)(2,1)} %fusion.63), channel_id=1, source_target_pairs={{64,0},{128,64},{192,128},{65,1},{129,65},{193,129},{66,2},{130,66... | collective-permute-start | bytes 786440 | tf_op jit(solution)/shard_map/ppermute | solution.py:10
  196.4 36.3 %all-to-all-start.2 = ((bf16[64,4,2048]{2,1,0:T(4,128)(2,1)}), bf16[64,4,2048]{2,1,0:T(4,128)(2,1)}, u32[]{:S(2)}, u32[]{:S(2)}) async-start(bf16[64,4,2048]{2,1,0:T(4,128)(2,1)} %copy.61), calls=%async_computation.2 | async-start | bytes 2097152 | tf_op jit(solution)/shard_map/all_to_all | solution.py:37
  205.8 26.9 %collective-permute-start.6 = (bf16[64,4,2048]{2,0,1:T(8,128)(2,1)}, bf16[64,4,2048]{2,0,1:T(8,128)(2,1)}, u32[]{:S(2)}, u32[]{:S(2)}) collective-permute-start(bf16[64,4,2048]{2,0,1:T(8,128)(2,1)} %copy.95), channel_id=1, source_target_pairs={{0,64},{64,128},{128,192},{1,65},{65,129},{129,193},{2,66},{66,130... | collective-permute-start | bytes 3145736 | tf_op jit(solution)/shard_map/ppermute | solution.py:10
  236.9 4.6 copy-start.10
  236.9 4.6 copy-start.28
  287.9 10.3 %collective-permute-start.7 = (bf16[64,2048]{1,0:T(8,128)(2,1)}, bf16[64,2048]{1,0:T(8,128)(2,1)}, u32[]{:S(2)}, u32[]{:S(2)}) collective-permute-start(bf16[64,2048]{1,0:T(8,128)(2,1)} %add_convert_fusion.4), channel_id=1, source_target_pairs={{64,0},{128,64},{192,128},{65,1},{129,65},{193,129},{66,2},{130,66... | collective-permute-start | bytes 786440 | tf_op jit(solution)/shard_map/ppermute | solution.py:10
  302.0 41.1 %all-to-all-start.4 = ((bf16[64,4,2048]{2,1,0:T(4,128)(2,1)}), bf16[64,4,2048]{2,1,0:T(4,128)(2,1)}, u32[]{:S(2)}, u32[]{:S(2)}) async-start(bf16[64,4,2048]{2,1,0:T(4,128)(2,1)} %copy.67), calls=%async_computation.4 | async-start | bytes 2097152 | tf_op jit(solution)/shard_map/all_to_all | solution.py:37
  311.4 26.6 %collective-permute-start.8 = (bf16[64,4,2048]{2,0,1:T(8,128)(2,1)}, bf16[64,4,2048]{2,0,1:T(8,128)(2,1)}, u32[]{:S(2)}, u32[]{:S(2)}) collective-permute-start(bf16[64,4,2048]{2,0,1:T(8,128)(2,1)} %copy.59), channel_id=1, source_target_pairs={{0,64},{64,128},{128,192},{1,65},{65,129},{129,193},{2,66},{66,130... | collective-permute-start | bytes 3145736 | tf_op jit(solution)/shard_map/ppermute | solution.py:10
  343.1 5.3 copy-start.29
  392.2 10.3 %collective-permute-start.9 = (bf16[64,2048]{1,0:T(8,128)(2,1)}, bf16[64,2048]{1,0:T(8,128)(2,1)}, u32[]{:S(2)}, u32[]{:S(2)}) collective-permute-start(bf16[64,2048]{1,0:T(8,128)(2,1)} %add_convert_fusion.3), channel_id=1, source_target_pairs={{64,0},{128,64},{192,128},{65,1},{129,65},{193,129},{66,2},{130,66... | collective-permute-start | bytes 786440 | tf_op jit(solution)/shard_map/ppermute | solution.py:10
  406.3 35.7 %all-to-all-start.6 = ((bf16[64,4,2048]{2,1,0:T(4,128)(2,1)}), bf16[64,4,2048]{2,1,0:T(4,128)(2,1)}, u32[]{:S(2)}, u32[]{:S(2)}) async-start(bf16[64,4,2048]{2,1,0:T(4,128)(2,1)} %copy.74), calls=%async_computation.6 | async-start | bytes 2097152 | tf_op jit(solution)/shard_map/all_to_all | solution.py:37
  442.0 5.3 copy-start.30
  486.4 9.3 %collective-permute-start.10 = (bf16[64,2048]{1,0:T(8,128)(2,1)}, bf16[64,2048]{1,0:T(8,128)(2,1)}, u32[]{:S(2)}, u32[]{:S(2)}) collective-permute-start(bf16[64,2048]{1,0:T(8,128)(2,1)} %add_convert_fusion.2), channel_id=1, source_target_pairs={{64,0},{128,64},{192,128},{65,1},{129,65},{193,129},{66,2},{130,66... | collective-permute-start | bytes 786440 | tf_op jit(solution)/shard_map/ppermute | solution.py:10
  499.5 35.5 %all-to-all-start.8 = ((bf16[64,4,2048]{2,1,0:T(4,128)(2,1)}), bf16[64,4,2048]{2,1,0:T(4,128)(2,1)}, u32[]{:S(2)}, u32[]{:S(2)}) async-start(bf16[64,4,2048]{2,1,0:T(4,128)(2,1)} %copy.79), calls=%async_computation.8 | async-start | bytes 2097152 | tf_op jit(solution)/shard_map/all_to_all | solution.py:37
  535.0 5.4 copy-start.31
  579.4 9.3 %collective-permute-start.11 = (bf16[64,2048]{1,0:T(8,128)(2,1)}, bf16[64,2048]{1,0:T(8,128)(2,1)}, u32[]{:S(2)}, u32[]{:S(2)}) collective-permute-start(bf16[64,2048]{1,0:T(8,128)(2,1)} %add_convert_fusion.1), channel_id=1, source_target_pairs={{64,0},{128,64},{192,128},{65,1},{129,65},{193,129},{66,2},{130,66... | collective-permute-start | bytes 786440 | tf_op jit(solution)/shard_map/ppermute | solution.py:10
  592.5 35.5 %all-to-all-start.10 = ((bf16[64,4,2048]{2,1,0:T(4,128)(2,1)}), bf16[64,4,2048]{2,1,0:T(4,128)(2,1)}, u32[]{:S(2)}, u32[]{:S(2)}) async-start(bf16[64,4,2048]{2,1,0:T(4,128)(2,1)} %copy.84), calls=%async_computation.10 | async-start | bytes 2097152 | tf_op jit(solution)/shard_map/all_to_all | solution.py:37
  628.0 5.3 copy-start.32
  636.1 34.6 %all-to-all-start.11 = ((bf16[64,4,2048]{2,1,0:T(4,128)(2,1)}), bf16[64,4,2048]{2,1,0:T(4,128)(2,1)}, u32[]{:S(2)}, u32[]{:S(2)}) async-start(bf16[64,4,2048]{2,1,0:T(4,128)(2,1)} %copy.86), calls=%async_computation.11 | async-start | bytes 2097152 | tf_op jit(solution)/shard_map/all_to_all | solution.py:37
  642.0 55.6 %reduce-scatter.2.cloned.1.call-start = ((), (), s32[]{:S(2)}) async-start(), calls=%async_computation.13 | async-start | bytes 983040 | tf_op jit(solution)/shard_map/reduce_scatter | solution.py:169
  675.4 9.5 %copy-start.12 = (bf16[1,64,4,768]{3,1,2,0:T(8,128)(2,1)S(1)}, bf16[1,64,4,768]{3,1,2,0:T(8,128)(2,1)}, u32[]{:S(2)}) copy-start(bf16[1,64,4,768]{3,1,2,0:T(8,128)(2,1)} %fusion.118) | copy-start | bytes 1179652
  675.4 9.4 %copy-start.13 = (bf16[1,64,4,768]{3,1,2,0:T(8,128)(2,1)S(1)}, bf16[1,64,4,768]{3,1,2,0:T(8,128)(2,1)}, u32[]{:S(2)}) copy-start(bf16[1,64,4,768]{3,1,2,0:T(8,128)(2,1)} %fusion.119) | copy-start | bytes 1179652
  (22 other events, 51.5 us)
Sparse Core Ops, SparseCore 0:
  675.5 22.0 reduce-scatter.1

commit v6 on v5

--- a/solution.py
+++ b/solution.py
@@ -15,22 +15,24 @@
     return logistic * (1.0 + preactivation * (1.0 - logistic))
 
 
-def placement_tables(routes_micro, gates_micro, owners, capacity):
-    tokens, route_count = routes_micro.shape
-    flat_routes = routes_micro.reshape(-1)
+def placement_tables(routes_all, gates_all, owners, capacity):
+    micro_count, tokens, route_count = routes_all.shape
+    flat_routes = routes_all.reshape(micro_count, tokens * route_count)
     expert_ids = jnp.arange(owners, dtype=jnp.int32)
-    one_hot = (flat_routes[:, None] == expert_ids[None, :]).astype(jnp.int32)
-    ranks = jnp.sum((jnp.cumsum(one_hot, axis=0) - 1) * one_hot, axis=1)
-    slots = (flat_routes * capacity + ranks).reshape(tokens, route_count)
+    one_hot = (flat_routes[:, :, None] == expert_ids[None, None, :]).astype(jnp.bfloat16)
+    order = jnp.arange(tokens * route_count, dtype=jnp.int32)
+    earlier = (order[None, :] < order[:, None]).astype(jnp.bfloat16)
+    counts = jnp.einsum("ij,mje->mie", earlier, one_hot, preferred_element_type=jnp.float32)
+    ranks = jnp.sum(counts * one_hot.astype(jnp.float32), axis=2).astype(jnp.int32)
+    slots = (flat_routes * capacity + ranks).reshape(micro_count, tokens, route_count)
     slot_ids = jnp.arange(owners * capacity, dtype=jnp.int32)
-    token_table = jnp.zeros((owners * capacity, tokens), jnp.float32)
-    gate_table = jnp.zeros((owners * capacity, tokens), jnp.float32)
-    for route_no in range(route_count):
-        hit = slot_ids[:, None] == slots[:, route_no][None, :]
-        token_table = token_table + hit.astype(jnp.float32)
-        gate_table = gate_table + jnp.where(hit, gates_micro[:, route_no][None, :], 0.0)
-    shape = (owners, capacity, tokens)
-    return token_table.astype(jnp.bfloat16).reshape(shape), gate_table.reshape(shape)
+    hit = slots[:, :, :, None] == slot_ids[None, None, None, :]
+    token_table = jnp.sum(hit.astype(jnp.float32), axis=2)
+    gate_table = jnp.sum(jnp.where(hit, gates_all[:, :, :, None], 0.0), axis=2)
+    shape = (micro_count, owners, capacity, tokens)
+    token_table = jnp.swapaxes(token_table, 1, 2).reshape(shape)
+    gate_table = jnp.swapaxes(gate_table, 1, 2).reshape(shape)
+    return token_table.astype(jnp.bfloat16), gate_table
 
 
 def exchange(rows):
@@ -67,20 +69,13 @@
         for source in range(section_count)
     ]
     upstream = jnp.concatenate(pieces, axis=2)
-    token_tables, gate_tables = [], []
-    for micro_no in range(micro_count):
-        token_table, gate_table = placement_tables(routes[0, micro_no], gates[0, micro_no], owners, capacity)
-        token_tables.append(token_table)
-        gate_tables.append(gate_table)
-    token_stack = jnp.stack(token_tables)
-    gate_stack = jnp.stack(gate_tables)
+    token_stack, gate_stack = placement_tables(routes[0], gates[0], owners, capacity)
+    token_tables = [token_stack[micro_no] for micro_no in range(micro_count)]
 
     above_inputs = shifted(inputs_dev, "pipe", -1)
     above_routes = shifted(routes[0], "pipe", -1)
-    above_tables = [
-        placement_tables(above_routes[micro_no], gates[0, micro_no], owners, capacity)[0]
-        for micro_no in range(micro_count)
-    ]
+    above_stack = placement_tables(above_routes, gates[0], owners, capacity)[0]
+    above_tables = [above_stack[micro_no] for micro_no in range(micro_count)]
     is_last = section_id == section_count - 1
     is_first = section_id == 0
 

time: 713 us -> 693 us (0.972)
  blocking collectives: 146 us -> 0 us
  waiting for transfers between devices: 255 us -> 367 us
  starting transfers between devices: 85.9 us -> 119 us
  other arithmetic: 33.4 us -> 21 us
    all_to_all x4 -> x0, blocking collectives: 146 us -> none  [exchange(): lax.all_to_all(rows, 'expert', split_axis=0, concat_axis=0, tiled=True)]
    all_to_all x8 -> x12, waiting for transfers between devices: 161 us -> 275 us  [exchange(): lax.all_to_all(rows, 'expert', split_axis=0, concat_axis=0, tiled=True)]
    all_to_all x8 -> x12, starting transfers between devices: 58.9 us -> 91.7 us  [exchange(): lax.all_to_all(rows, 'expert', split_axis=0, concat_axis=0, tiled=True)]
    another operation x12 -> x0, other arithmetic: 10 us -> none
    unnamed x72 -> x82, local copies, waits for them, and re-layouts: 11.9 us -> 14.3 us
  transfers between devices with their start and end apart: 21 -> 25, of which waited for: 14 -> 18; matrix products, arithmetic and copies ran while one was open for 15% -> 12% of each run, Pallas kernels for 0% -> 0%
where the time goes in v6:
time: 693 us; the launch traced here: 686 us
  waiting for transfers between devices  367 us (53%)
  starting transfers between devices  119 us (17%)
  matrix products  90.5 us (13%)
  local copies, waits for them, and re-layouts  72.6 us (10%)
  other arithmetic  21 us (3%)
  between operations  15.1 us (2%)
    all_to_all x12, waiting for transfers between devices, exchange(): lax.all_to_all(rows, 'expert', split_axis=0, concat_axis=0, tiled=True)  275 us
    all_to_all x12, starting transfers between devices, exchange(): lax.all_to_all(rows, 'expert', split_axis=0, concat_axis=0, tiled=True)  91.7 us
    ppermute x9, waiting for transfers between devices, shifted(): lax.ppermute(value, axis, [(source, source + steps) for source in range(f...  85.8 us
    dot_general x6, matrix products, on_device(): jnp.einsum('pqd,fd->pqf', grad_recv, second_weights, preferred_element_ty...  28 us
    ppermute x9, starting transfers between devices, shifted(): lax.ppermute(value, axis, [(source, source + steps) for source in range(f...  18.7 us
    dynamic_update_slice x6, local copies, waits for them, and re-layouts, on_device(): lax.dynamic_update_slice_in_dim(grad_keep, grad_recv[None], keep_at, 0)  15.7 us
    dot_general x6, matrix products, on_device(): jnp.einsum('pqk,pqd->kd', token_stack[micro_id], returned, preferred_elem...  15.5 us
    unnamed x82, local copies, waits for them, and re-layouts  14.3 us
  transfers between devices with their start and end apart: 25, of which 18 were waited for; matrix products, arithmetic and copies ran while one was open for 12% of the time, Pallas kernels for 0%

profile of v6, /device:TPU:8, one launch (start us, length us, event | category | flops | bytes accessed | tf_op | source)
XLA Modules:
  0.0 685.6 jit_solution(15048718079896488777)
XLA Ops:
  46.4 13.1 %all-to-all-start = ((bf16[64,8,2048]{2,1,0:T(8,128)(2,1)}), bf16[64,8,2048]{2,1,0:T(8,128)(2,1)}, u32[]{:S(2)}, u32[]{:S(2)}) async-start(bf16[64,8,2048]{2,1,0:T(8,128)(2,1)} %copy.92), calls=%async_computation | async-start | bytes 4194304 | tf_op jit(solution)/shard_map/all_to_all | solution.py:39
  59.6 50.8 %all-to-all-done = bf16[64,8,2048]{2,1,0:T(8,128)(2,1)} async-done(((bf16[64,8,2048]{2,1,0:T(8,128)(2,1)}), bf16[64,8,2048]{2,1,0:T(8,128)(2,1)}, u32[]{:S(2)}, u32[]{:S(2)}) %all-to-all-start) | async-done | bytes 2097184 | tf_op jit(solution)/shard_map/all_to_all | solution.py:39
  122.5 5.6 all-to-all-start.1
  129.2 27.6 %all-to-all-done.1 = bf16[64,4,2048]{2,1,0:T(4,128)(2,1)} async-done(((bf16[64,4,2048]{2,1,0:T(4,128)(2,1)}), bf16[64,4,2048]{2,1,0:T(4,128)(2,1)}, u32[]{:S(2)}, u32[]{:S(2)}) %all-to-all-start.1) | async-done | bytes 1048608 | tf_op jit(solution)/shard_map/all_to_all | solution.py:39
  160.6 9.2 %collective-permute-done.5 = bf16[64,2048]{1,0:T(8,128)(2,1)S(1)} collective-permute-done((bf16[64,2048]{1,0:T(8,128)(2,1)S(1)}, bf16[64,2048]{1,0:T(8,128)(2,1)S(1)}, u32[]{:S(2)}, u32[]{:S(2)}) %collective-permute-start.5) | collective-permute-done | bytes 262176 | tf_op jit(solution)/shard_map/ppermute | solution.py:10
  173.7 6.6 all-to-all-start.2
  188.1 21.8 %collective-permute-done.6 = bf16[64,4,2048]{2,0,1:T(8,128)(2,1)} collective-permute-done((bf16[64,4,2048]{2,0,1:T(8,128)(2,1)}, bf16[64,4,2048]{2,0,1:T(8,128)(2,1)}, u32[]{:S(2)}, u32[]{:S(2)}) %collective-permute-start.6) | collective-permute-done | bytes 1048608 | tf_op jit(solution)/shard_map/ppermute | solution.py:10
  223.0 10.5 %all-to-all-start.3 = ((bf16[64,4,2048]{2,1,0:T(4,128)(2,1)}), bf16[64,4,2048]{2,1,0:T(4,128)(2,1)}, u32[]{:S(2)}, u32[]{:S(2)}) async-start(bf16[64,4,2048]{2,1,0:T(4,128)(2,1)} %copy.107), calls=%async_computation.3 | async-start | bytes 2097152 | tf_op jit(solution)/shard_map/all_to_all | solution.py:39
  235.0 27.1 %all-to-all-done.3 = bf16[64,4,2048]{2,1,0:T(4,128)(2,1)} async-done(((bf16[64,4,2048]{2,1,0:T(4,128)(2,1)}), bf16[64,4,2048]{2,1,0:T(4,128)(2,1)}, u32[]{:S(2)}, u32[]{:S(2)}) %all-to-all-start.3) | async-done | bytes 1048608 | tf_op jit(solution)/shard_map/all_to_all | solution.py:39
  266.0 8.7 %collective-permute-done.7 = bf16[64,2048]{1,0:T(8,128)(2,1)S(1)} collective-permute-done((bf16[64,2048]{1,0:T(8,128)(2,1)S(1)}, bf16[64,2048]{1,0:T(8,128)(2,1)S(1)}, u32[]{:S(2)}, u32[]{:S(2)}) %collective-permute-start.7) | collective-permute-done | bytes 262176 | tf_op jit(solution)/shard_map/ppermute | solution.py:10
  279.2 6.6 all-to-all-start.4
  293.2 22.0 %collective-permute-done.8 = bf16[64,4,2048]{2,0,1:T(8,128)(2,1)} collective-permute-done((bf16[64,4,2048]{2,0,1:T(8,128)(2,1)}, bf16[64,4,2048]{2,0,1:T(8,128)(2,1)}, u32[]{:S(2)}, u32[]{:S(2)}) %collective-permute-start.8) | collective-permute-done | bytes 1048608 | tf_op jit(solution)/shard_map/ppermute | solution.py:10
  328.4 10.5 %all-to-all-start.5 = ((bf16[64,4,2048]{2,1,0:T(4,128)(2,1)}), bf16[64,4,2048]{2,1,0:T(4,128)(2,1)}, u32[]{:S(2)}, u32[]{:S(2)}) async-start(bf16[64,4,2048]{2,1,0:T(4,128)(2,1)} %copy.115), calls=%async_computation.5 | async-start | bytes 2097152 | tf_op jit(solution)/shard_map/all_to_all | solution.py:39
  339.0 28.6 %all-to-all-done.5 = bf16[64,4,2048]{2,1,0:T(4,128)(2,1)} async-done(((bf16[64,4,2048]{2,1,0:T(4,128)(2,1)}), bf16[64,4,2048]{2,1,0:T(4,128)(2,1)}, u32[]{:S(2)}, u32[]{:S(2)}) %all-to-all-start.5) | async-done | bytes 1048608 | tf_op jit(solution)/shard_map/all_to_all | solution.py:39
  371.5 8.7 %collective-permute-done.9 = bf16[64,2048]{1,0:T(8,128)(2,1)S(1)} collective-permute-done((bf16[64,2048]{1,0:T(8,128)(2,1)S(1)}, bf16[64,2048]{1,0:T(8,128)(2,1)S(1)}, u32[]{:S(2)}, u32[]{:S(2)}) %collective-permute-start.9) | collective-permute-done | bytes 262176 | tf_op jit(solution)/shard_map/ppermute | solution.py:10
  384.6 7.2 %all-to-all-start.6 = ((bf16[64,4,2048]{2,1,0:T(4,128)(2,1)}), bf16[64,4,2048]{2,1,0:T(4,128)(2,1)}, u32[]{:S(2)}, u32[]{:S(2)}) async-start(bf16[64,4,2048]{2,1,0:T(4,128)(2,1)} %copy.119), calls=%async_computation.6 | async-start | bytes 2097152 | tf_op jit(solution)/shard_map/all_to_all | solution.py:39
  391.9 28.5 %all-to-all-done.6 = bf16[64,4,2048]{2,1,0:T(4,128)(2,1)} async-done(((bf16[64,4,2048]{2,1,0:T(4,128)(2,1)}), bf16[64,4,2048]{2,1,0:T(4,128)(2,1)}, u32[]{:S(2)}, u32[]{:S(2)}) %all-to-all-start.6) | async-done | bytes 1048608 | tf_op jit(solution)/shard_map/all_to_all | solution.py:39
  428.5 5.9 all-to-all-start.7
  434.5 28.6 %all-to-all-done.7 = bf16[64,4,2048]{2,1,0:T(4,128)(2,1)} async-done(((bf16[64,4,2048]{2,1,0:T(4,128)(2,1)}), bf16[64,4,2048]{2,1,0:T(4,128)(2,1)}, u32[]{:S(2)}, u32[]{:S(2)}) %all-to-all-start.7) | async-done | bytes 1048608 | tf_op jit(solution)/shard_map/all_to_all | solution.py:39
  467.0 7.7 %collective-permute-done.10 = bf16[64,2048]{1,0:T(8,128)(2,1)S(1)} collective-permute-done((bf16[64,2048]{1,0:T(8,128)(2,1)S(1)}, bf16[64,2048]{1,0:T(8,128)(2,1)S(1)}, u32[]{:S(2)}, u32[]{:S(2)}) %collective-permute-start.10) | collective-permute-done | bytes 262176 | tf_op jit(solution)/shard_map/ppermute | solution.py:10
  479.0 7.0 %all-to-all-start.8 = ((bf16[64,4,2048]{2,1,0:T(4,128)(2,1)}), bf16[64,4,2048]{2,1,0:T(4,128)(2,1)}, u32[]{:S(2)}, u32[]{:S(2)}) async-start(bf16[64,4,2048]{2,1,0:T(4,128)(2,1)} %copy.125), calls=%async_computation.8 | async-start | bytes 2097152 | tf_op jit(solution)/shard_map/all_to_all | solution.py:39
  486.0 28.5 %all-to-all-done.8 = bf16[64,4,2048]{2,1,0:T(4,128)(2,1)} async-done(((bf16[64,4,2048]{2,1,0:T(4,128)(2,1)}), bf16[64,4,2048]{2,1,0:T(4,128)(2,1)}, u32[]{:S(2)}, u32[]{:S(2)}) %all-to-all-start.8) | async-done | bytes 1048608 | tf_op jit(solution)/shard_map/all_to_all | solution.py:39
  522.7 5.9 all-to-all-start.9
  528.7 28.6 %all-to-all-done.9 = bf16[64,4,2048]{2,1,0:T(4,128)(2,1)} async-done(((bf16[64,4,2048]{2,1,0:T(4,128)(2,1)}), bf16[64,4,2048]{2,1,0:T(4,128)(2,1)}, u32[]{:S(2)}, u32[]{:S(2)}) %all-to-all-start.9) | async-done | bytes 1048608 | tf_op jit(solution)/shard_map/all_to_all | solution.py:39
  561.3 7.7 %collective-permute-done.11 = bf16[64,2048]{1,0:T(8,128)(2,1)S(1)} collective-permute-done((bf16[64,2048]{1,0:T(8,128)(2,1)S(1)}, bf16[64,2048]{1,0:T(8,128)(2,1)S(1)}, u32[]{:S(2)}, u32[]{:S(2)}) %collective-permute-start.11) | collective-permute-done | bytes 262176 | tf_op jit(solution)/shard_map/ppermute | solution.py:10
  573.4 7.0 %all-to-all-start.10 = ((bf16[64,4,2048]{2,1,0:T(4,128)(2,1)}), bf16[64,4,2048]{2,1,0:T(4,128)(2,1)}, u32[]{:S(2)}, u32[]{:S(2)}) async-start(bf16[64,4,2048]{2,1,0:T(4,128)(2,1)} %copy.131), calls=%async_computation.10 | async-start | bytes 2097152 | tf_op jit(solution)/shard_map/all_to_all | solution.py:39
  596.7 12.2 %all-to-all-done.10 = bf16[64,4,2048]{2,1,0:T(4,128)(2,1)} async-done(((bf16[64,4,2048]{2,1,0:T(4,128)(2,1)}), bf16[64,4,2048]{2,1,0:T(4,128)(2,1)}, u32[]{:S(2)}, u32[]{:S(2)}) %all-to-all-start.10) | async-done | bytes 1048608 | tf_op jit(solution)/shard_map/all_to_all | solution.py:39
  617.0 5.9 all-to-all-start.11
  637.2 14.4 %all-to-all-done.11 = bf16[64,4,2048]{2,1,0:T(4,128)(2,1)} async-done(((bf16[64,4,2048]{2,1,0:T(4,128)(2,1)}), bf16[64,4,2048]{2,1,0:T(4,128)(2,1)}, u32[]{:S(2)}, u32[]{:S(2)}) %all-to-all-start.11) | async-done | bytes 1048608 | tf_op jit(solution)/shard_map/all_to_all | solution.py:39
  656.3 6.6 fusion.36
  665.7 5.9 fusion.39
  671.7 6.9 %reduce-scatter.2.cloned.1.call-done = bf16[3,64,512]{2,1,0:T(8,128)(2,1)} async-done(((bf16[3,64,2048]{2,1,0:T(8,128)(2,1)}), bf16[3,64,512]{2,1,0:T(8,128)(2,1)}) %reduce-scatter.2.cloned.1.call-update) | async-done | bytes 196624 | tf_op jit(solution)/shard_map/reduce_scatter | solution.py:164
  (194 shorter events, 198.8 us)
Async XLA Ops:
  7.2 109.0 %copy-start = (bf16[1,1,768,2048]{3,2,1,0:T(8,128)(2,1)S(1)}, bf16[1,1,768,2048]{3,2,1,0:T(8,128)(2,1)}, u32[]{:S(2)}) copy-start(bf16[1,1,768,2048]{3,2,1,0:T(8,128)(2,1)} %param.10) | copy-start | bytes 9437188
  7.2 31.8 %collective-permute-start.1 = (bf16[3,64,512]{2,1,0:T(8,128)(2,1)}, bf16[3,64,512]{2,1,0:T(8,128)(2,1)}, u32[]{:S(2)}, u32[]{:S(2)}) collective-permute-start(bf16[3,64,512]{2,1,0:T(8,128)(2,1)} %param.11), channel_id=1, source_target_pairs={{64,192},{65,193},{66,194},{67,195},{68,196},{69,197},{70,198},{71... | collective-permute-start | bytes 589832 | tf_op jit(solution)/shard_map/ppermute | solution.py:68
  8.7 29.4 %collective-permute-start = (bf16[3,64,512]{2,1,0:T(8,128)(2,1)}, bf16[3,64,512]{2,1,0:T(8,128)(2,1)}, u32[]{:S(2)}, u32[]{:S(2)}) collective-permute-start(bf16[3,64,512]{2,1,0:T(8,128)(2,1)} %param.11), channel_id=1, source_target_pairs={{0,192},{1,193},{2,194},{3,195},{4,196},{5,197},{6,198},{7,199},{8... | collective-permute-start | bytes 589832 | tf_op jit(solution)/shard_map/ppermute | solution.py:68
  14.1 25.8 %collective-permute-start.2 = (bf16[3,64,512]{2,1,0:T(8,128)(2,1)}, bf16[3,64,512]{2,1,0:T(8,128)(2,1)}, u32[]{:S(2)}, u32[]{:S(2)}) collective-permute-start(bf16[3,64,512]{2,1,0:T(8,128)(2,1)} %param.11), channel_id=1, source_target_pairs={{128,192},{129,193},{130,194},{131,195},{132,196},{133,197},{134,1... | collective-permute-start | bytes 589832 | tf_op jit(solution)/shard_map/ppermute | solution.py:68
  16.9 12.2 %collective-permute-start.3 = (s32[3,64,4]{2,1,0:T(8,128)}, s32[3,64,4]{2,1,0:T(8,128)}, u32[]{:S(2)}, u32[]{:S(2)}) collective-permute-start(s32[3,64,4]{2,1,0:T(8,128)} %bitcast.4), channel_id=1, source_target_pairs={{64,0},{128,64},{192,128},{65,1},{129,65},{193,129},{66,2},{130,66... | collective-permute-start | bytes 9224 | tf_op jit(solution)/shard_map/ppermute | solution.py:10
  18.2 22.8 %collective-permute-start.4 = (bf16[3,64,2048]{2,1,0:T(8,128)(2,1)}, bf16[3,64,2048]{2,1,0:T(8,128)(2,1)}, u32[]{:S(2)}, u32[]{:S(2)}) collective-permute-start(bf16[3,64,2048]{2,1,0:T(8,128)(2,1)} %bitcast.335), channel_id=1, source_target_pairs={{64,0},{128,64},{192,128},{65,1},{129,65},{193,129},{66,2},{130,66... | collective-permute-start | bytes 2359304 | tf_op jit(solution)/shard_map/ppermute | solution.py:10
  46.4 64.0 %all-to-all-start = ((bf16[64,8,2048]{2,1,0:T(8,128)(2,1)}), bf16[64,8,2048]{2,1,0:T(8,128)(2,1)}, u32[]{:S(2)}, u32[]{:S(2)}) async-start(bf16[64,8,2048]{2,1,0:T(8,128)(2,1)} %copy.92), calls=%async_computation | async-start | bytes 4194304 | tf_op jit(solution)/shard_map/all_to_all | solution.py:39
  122.5 34.3 %all-to-all-start.1 = ((bf16[64,4,2048]{2,1,0:T(4,128)(2,1)}), bf16[64,4,2048]{2,1,0:T(4,128)(2,1)}, u32[]{:S(2)}, u32[]{:S(2)}) async-start(bf16[64,4,2048]{2,1,0:T(4,128)(2,1)} %copy.97), calls=%async_computation.1 | async-start | bytes 2097152 | tf_op jit(solution)/shard_map/all_to_all | solution.py:39
  159.3 10.4 %collective-permute-start.5 = (bf16[64,2048]{1,0:T(8,128)(2,1)S(1)}, bf16[64,2048]{1,0:T(8,128)(2,1)S(1)}, u32[]{:S(2)}, u32[]{:S(2)}) collective-permute-start(bf16[64,2048]{1,0:T(8,128)(2,1)S(1)} %fusion.63), channel_id=1, source_target_pairs={{64,0},{128,64},{192,128},{65,1},{129,65},{193,129},{66,2},{130,66... | collective-permute-start | bytes 786440 | tf_op jit(solution)/shard_map/ppermute | solution.py:10
  171.8 16.2 %copy-start.30 = (bf16[1,256,64]{1,2,0:T(8,128)(2,1)S(1)}, bf16[1,256,64]{1,2,0:T(8,128)(2,1)}, u32[]{:S(2)}) copy-start(bf16[1,256,64]{1,2,0:T(8,128)(2,1)} %get-tuple-element.19) | copy-start | bytes 98308
  173.7 36.3 %all-to-all-start.2 = ((bf16[64,4,2048]{2,1,0:T(4,128)(2,1)}), bf16[64,4,2048]{2,1,0:T(4,128)(2,1)}, u32[]{:S(2)}, u32[]{:S(2)}) async-start(bf16[64,4,2048]{2,1,0:T(4,128)(2,1)} %copy.104), calls=%async_computation.2 | async-start | bytes 2097152 | tf_op jit(solution)/shard_map/all_to_all | solution.py:39
  183.1 26.9 %collective-permute-start.6 = (bf16[64,4,2048]{2,0,1:T(8,128)(2,1)}, bf16[64,4,2048]{2,0,1:T(8,128)(2,1)}, u32[]{:S(2)}, u32[]{:S(2)}) collective-permute-start(bf16[64,4,2048]{2,0,1:T(8,128)(2,1)} %copy.142), channel_id=1, source_target_pairs={{0,64},{64,128},{128,192},{1,65},{65,129},{129,193},{2,66},{66,130... | collective-permute-start | bytes 3145736 | tf_op jit(solution)/shard_map/ppermute | solution.py:10
  221.2 54.3 %copy-start.16 = (f32[1,64,4,64]{3,2,1,0:T(4,128)S(1)}, f32[1,64,4,64]{3,2,1,0:T(4,128)}, u32[]{:S(2)}) copy-start(f32[1,64,4,64]{3,2,1,0:T(4,128)} %get-tuple-element.10) | copy-start | bytes 196612
  223.0 39.2 %all-to-all-start.3 = ((bf16[64,4,2048]{2,1,0:T(4,128)(2,1)}), bf16[64,4,2048]{2,1,0:T(4,128)(2,1)}, u32[]{:S(2)}, u32[]{:S(2)}) async-start(bf16[64,4,2048]{2,1,0:T(4,128)(2,1)} %copy.107), calls=%async_computation.3 | async-start | bytes 2097152 | tf_op jit(solution)/shard_map/all_to_all | solution.py:39
  264.7 10.0 %collective-permute-start.7 = (bf16[64,2048]{1,0:T(8,128)(2,1)S(1)}, bf16[64,2048]{1,0:T(8,128)(2,1)S(1)}, u32[]{:S(2)}, u32[]{:S(2)}) collective-permute-start(bf16[64,2048]{1,0:T(8,128)(2,1)S(1)} %add_convert_fusion.4), channel_id=1, source_target_pairs={{64,0},{128,64},{192,128},{65,1},{129,65},{193,129},{66,2},{130,66... | collective-permute-start | bytes 786440 | tf_op jit(solution)/shard_map/ppermute | solution.py:10
  279.2 41.1 %all-to-all-start.4 = ((bf16[64,4,2048]{2,1,0:T(4,128)(2,1)}), bf16[64,4,2048]{2,1,0:T(4,128)(2,1)}, u32[]{:S(2)}, u32[]{:S(2)}) async-start(bf16[64,4,2048]{2,1,0:T(4,128)(2,1)} %copy.111), calls=%async_computation.4 | async-start | bytes 2097152 | tf_op jit(solution)/shard_map/all_to_all | solution.py:39
  288.6 26.6 %collective-permute-start.8 = (bf16[64,4,2048]{2,0,1:T(8,128)(2,1)}, bf16[64,4,2048]{2,0,1:T(8,128)(2,1)}, u32[]{:S(2)}, u32[]{:S(2)}) collective-permute-start(bf16[64,4,2048]{2,0,1:T(8,128)(2,1)} %copy.98), channel_id=1, source_target_pairs={{0,64},{64,128},{128,192},{1,65},{65,129},{129,193},{2,66},{66,130... | collective-permute-start | bytes 3145736 | tf_op jit(solution)/shard_map/ppermute | solution.py:10
  326.6 54.3 %copy-start.15 = (f32[1,64,4,64]{3,2,1,0:T(4,128)S(1)}, f32[1,64,4,64]{3,2,1,0:T(4,128)}, u32[]{:S(2)}) copy-start(f32[1,64,4,64]{3,2,1,0:T(4,128)} %get-tuple-element.9) | copy-start | bytes 196612
  328.4 39.2 %all-to-all-start.5 = ((bf16[64,4,2048]{2,1,0:T(4,128)(2,1)}), bf16[64,4,2048]{2,1,0:T(4,128)(2,1)}, u32[]{:S(2)}, u32[]{:S(2)}) async-start(bf16[64,4,2048]{2,1,0:T(4,128)(2,1)} %copy.115), calls=%async_computation.5 | async-start | bytes 2097152 | tf_op jit(solution)/shard_map/all_to_all | solution.py:39
  370.2 10.0 %collective-permute-start.9 = (bf16[64,2048]{1,0:T(8,128)(2,1)S(1)}, bf16[64,2048]{1,0:T(8,128)(2,1)S(1)}, u32[]{:S(2)}, u32[]{:S(2)}) collective-permute-start(bf16[64,2048]{1,0:T(8,128)(2,1)S(1)} %add_convert_fusion.3), channel_id=1, source_target_pairs={{64,0},{128,64},{192,128},{65,1},{129,65},{193,129},{66,2},{130,66... | collective-permute-start | bytes 786440 | tf_op jit(solution)/shard_map/ppermute | solution.py:10
  384.6 35.7 %all-to-all-start.6 = ((bf16[64,4,2048]{2,1,0:T(4,128)(2,1)}), bf16[64,4,2048]{2,1,0:T(4,128)(2,1)}, u32[]{:S(2)}, u32[]{:S(2)}) async-start(bf16[64,4,2048]{2,1,0:T(4,128)(2,1)} %copy.119), calls=%async_computation.6 | async-start | bytes 2097152 | tf_op jit(solution)/shard_map/all_to_all | solution.py:39
  426.7 48.6 %copy-start.14 = (f32[1,64,4,64]{3,2,1,0:T(4,128)S(1)}, f32[1,64,4,64]{3,2,1,0:T(4,128)}, u32[]{:S(2)}) copy-start(f32[1,64,4,64]{3,2,1,0:T(4,128)} %get-tuple-element.8) | copy-start | bytes 196612
  428.5 34.6 %all-to-all-start.7 = ((bf16[64,4,2048]{2,1,0:T(4,128)(2,1)}), bf16[64,4,2048]{2,1,0:T(4,128)(2,1)}, u32[]{:S(2)}, u32[]{:S(2)}) async-start(bf16[64,4,2048]{2,1,0:T(4,128)(2,1)} %copy.121), calls=%async_computation.7 | async-start | bytes 2097152 | tf_op jit(solution)/shard_map/all_to_all | solution.py:39
  465.7 9.0 %collective-permute-start.10 = (bf16[64,2048]{1,0:T(8,128)(2,1)S(1)}, bf16[64,2048]{1,0:T(8,128)(2,1)S(1)}, u32[]{:S(2)}, u32[]{:S(2)}) collective-permute-start(bf16[64,2048]{1,0:T(8,128)(2,1)S(1)} %add_convert_fusion.2), channel_id=1, source_target_pairs={{64,0},{128,64},{192,128},{65,1},{129,65},{193,129},{66,2},{130,66... | collective-permute-start | bytes 786440 | tf_op jit(solution)/shard_map/ppermute | solution.py:10
  479.0 35.5 %all-to-all-start.8 = ((bf16[64,4,2048]{2,1,0:T(4,128)(2,1)}), bf16[64,4,2048]{2,1,0:T(4,128)(2,1)}, u32[]{:S(2)}, u32[]{:S(2)}) async-start(bf16[64,4,2048]{2,1,0:T(4,128)(2,1)} %copy.125), calls=%async_computation.8 | async-start | bytes 2097152 | tf_op jit(solution)/shard_map/all_to_all | solution.py:39
  520.9 48.8 %copy-start.13 = (f32[1,64,4,64]{3,2,1,0:T(4,128)S(1)}, f32[1,64,4,64]{3,2,1,0:T(4,128)}, u32[]{:S(2)}) copy-start(f32[1,64,4,64]{3,2,1,0:T(4,128)} %get-tuple-element.7) | copy-start | bytes 196612
  522.7 34.6 %all-to-all-start.9 = ((bf16[64,4,2048]{2,1,0:T(4,128)(2,1)}), bf16[64,4,2048]{2,1,0:T(4,128)(2,1)}, u32[]{:S(2)}, u32[]{:S(2)}) async-start(bf16[64,4,2048]{2,1,0:T(4,128)(2,1)} %copy.127), calls=%async_computation.9 | async-start | bytes 2097152 | tf_op jit(solution)/shard_map/all_to_all | solution.py:39
  559.8 20.6 %copy-start.19 = (bf16[1,64,4,64]{3,2,1,0:T(4,128)(2,1)S(1)}, bf16[1,64,4,64]{3,2,1,0:T(4,128)(2,1)}, u32[]{:S(2)}) copy-start(bf16[1,64,4,64]{3,2,1,0:T(4,128)(2,1)} %get-tuple-element.13) | copy-start | bytes 98308
  559.8 9.1 %collective-permute-start.11 = (bf16[64,2048]{1,0:T(8,128)(2,1)S(1)}, bf16[64,2048]{1,0:T(8,128)(2,1)S(1)}, u32[]{:S(2)}, u32[]{:S(2)}) collective-permute-start(bf16[64,2048]{1,0:T(8,128)(2,1)S(1)} %add_convert_fusion.1), channel_id=1, source_target_pairs={{64,0},{128,64},{192,128},{65,1},{129,65},{193,129},{66,2},{130,66... | collective-permute-start | bytes 786440 | tf_op jit(solution)/shard_map/ppermute | solution.py:10
  573.4 35.5 %all-to-all-start.10 = ((bf16[64,4,2048]{2,1,0:T(4,128)(2,1)}), bf16[64,4,2048]{2,1,0:T(4,128)(2,1)}, u32[]{:S(2)}, u32[]{:S(2)}) async-start(bf16[64,4,2048]{2,1,0:T(4,128)(2,1)} %copy.131), calls=%async_computation.10 | async-start | bytes 2097152 | tf_op jit(solution)/shard_map/all_to_all | solution.py:39
  617.0 34.6 %all-to-all-start.11 = ((bf16[64,4,2048]{2,1,0:T(4,128)(2,1)}), bf16[64,4,2048]{2,1,0:T(4,128)(2,1)}, u32[]{:S(2)}, u32[]{:S(2)}) async-start(bf16[64,4,2048]{2,1,0:T(4,128)(2,1)} %copy.133), calls=%async_computation.11 | async-start | bytes 2097152 | tf_op jit(solution)/shard_map/all_to_all | solution.py:39
  622.9 55.6 %reduce-scatter.2.cloned.1.call-start = ((), (), s32[]{:S(2)}) async-start(), calls=%async_computation.13 | async-start | bytes 983040 | tf_op jit(solution)/shard_map/reduce_scatter | solution.py:164
  (31 other events, 158.7 us)
Sparse Core Ops, SparseCore 0:
  656.4 22.0 reduce-scatter.1

commit v7 on v6

--- a/solution.py
+++ b/solution.py
@@ -147,13 +147,27 @@
             add_inputs(jnp.where(is_first, returned, from_below_2))
         else:
             returned = exchange(row_grads)
+        if tick_no == tick_count - 1:
+            keep_at = jnp.where(offset >= micro_count, micro_count, micro_id)
+            pre_keep = lax.dynamic_update_slice_in_dim(pre_keep, pre_grad[None], keep_at, 0)
+            grad_keep = lax.dynamic_update_slice_in_dim(grad_keep, grad_recv[None], keep_at, 0)
+            first_sum = jnp.einsum(
+                "mpqd,mpqf->df", jnp.stack(recv_inputs), pre_keep[:micro_count],
+                preferred_element_type=jnp.float32,
+            )
+            second_sum = jnp.einsum(
+                "mpqf,mpqd->fd", jnp.stack(hiddens), grad_keep[:micro_count],
+                preferred_element_type=jnp.float32,
+            )
+            returned, first_sum, second_sum = lax.optimization_barrier((returned, first_sum, second_sum))
         summed = jnp.einsum(
             "pqk,pqd->kd", token_stack[micro_id], returned, preferred_element_type=jnp.float32
         )
         grad_out = (grad_now.astype(jnp.float32) + summed).astype(jnp.bfloat16)
-        keep_at = jnp.where(offset >= micro_count, micro_count, micro_id)
-        pre_keep = lax.dynamic_update_slice_in_dim(pre_keep, pre_grad[None], keep_at, 0)
-        grad_keep = lax.dynamic_update_slice_in_dim(grad_keep, grad_recv[None], keep_at, 0)
+        if tick_no < tick_count - 1:
+            keep_at = jnp.where(offset >= micro_count, micro_count, micro_id)
+            pre_keep = lax.dynamic_update_slice_in_dim(pre_keep, pre_grad[None], keep_at, 0)
+            grad_keep = lax.dynamic_update_slice_in_dim(grad_keep, grad_recv[None], keep_at, 0)
         if tick_no >= tick_count - micro_count:
             final_rows.append(grad_out)
         if tick_no + 1 < tick_count:
@@ -162,12 +176,8 @@
     final_rows = jnp.stack(final_rows)
     final_term = jnp.where(section_id == 0, final_rows, jnp.zeros_like(final_rows))
     grad_in = lax.psum_scatter(final_term, "pipe", scatter_dimension=2, tiled=True)
-    first_grad = jnp.einsum(
-        "mpqd,mpqf->df", jnp.stack(recv_inputs), pre_keep[:micro_count], preferred_element_type=jnp.float32
-    ).astype(jnp.bfloat16)
-    second_grad = jnp.einsum(
-        "mpqf,mpqd->fd", jnp.stack(hiddens), grad_keep[:micro_count], preferred_element_type=jnp.float32
-    ).astype(jnp.bfloat16)
+    first_grad = first_sum.astype(jnp.bfloat16)
+    second_grad = second_sum.astype(jnp.bfloat16)
     return (grad_in, first_grad[None, None], second_grad[None, None])
 
 

time: 693 us -> 692 us (level)
    reduce_scatter x1, waiting for transfers between devices: 6.86 us -> 22.3 us  [on_device(): lax.psum_scatter(final_term, 'pipe', scatter_dimension=2, tiled=True)]
    all_to_all x12, waiting for transfers between devices: 275 us -> 263 us  [exchange(): lax.all_to_all(rows, 'expert', split_axis=0, concat_axis=0, tiled=True)]
    unnamed x82 -> x80, local copies, waits for them, and re-layouts: 14.3 us -> 13.6 us
where the time goes in v7:
time: 692 us; the launch traced here: 684 us
  waiting for transfers between devices  367 us (53%)
  starting transfers between devices  118 us (17%)
  matrix products  90.6 us (13%)
  local copies, waits for them, and re-layouts  72.7 us (11%)
  other arithmetic  21.1 us (3%)
  between operations  15 us (2%)
    all_to_all x12, waiting for transfers between devices, exchange(): lax.all_to_all(rows, 'expert', split_axis=0, concat_axis=0, tiled=True)  263 us
    all_to_all x12, starting transfers between devices, exchange(): lax.all_to_all(rows, 'expert', split_axis=0, concat_axis=0, tiled=True)  90.8 us
    ppermute x9, waiting for transfers between devices, shifted(): lax.ppermute(value, axis, [(source, source + steps) for source in range(f...  81.7 us
    dot_general x6, matrix products, on_device(): jnp.einsum('pqd,fd->pqf', grad_recv, second_weights, preferred_element_ty...  28 us
    reduce_scatter x1, waiting for transfers between devices, on_device(): lax.psum_scatter(final_term, 'pipe', scatter_dimension=2, tiled=True)  22.3 us
    ppermute x9, starting transfers between devices, shifted(): lax.ppermute(value, axis, [(source, source + steps) for source in range(f...  18.9 us
    dynamic_update_slice x6, local copies, waits for them, and re-layouts, on_device(): lax.dynamic_update_slice_in_dim(grad_keep, grad_recv[None], keep_at, 0)  15.7 us
    dot_general x6, matrix products, on_device(): jnp.einsum('pqk,pqd->kd', token_stack[micro_id], returned, preferred_elem...  15.5 us
  transfers between devices with their start and end apart: 25, of which 18 were waited for; matrix products, arithmetic and copies ran while one was open for 12% of the time, Pallas kernels for 0%

profile of v7, /device:TPU:8, one launch (start us, length us, event | category | flops | bytes accessed | tf_op | source)
XLA Modules:
  0.0 684.2 jit_solution(2789596124297112210)
XLA Ops:
  7.2 5.6 collective-permute-start
  46.4 12.8 %all-to-all-start = ((bf16[64,8,2048]{2,1,0:T(8,128)(2,1)}), bf16[64,8,2048]{2,1,0:T(8,128)(2,1)}, u32[]{:S(2)}, u32[]{:S(2)}) async-start(bf16[64,8,2048]{2,1,0:T(8,128)(2,1)} %copy.92), calls=%async_computation | async-start | bytes 4194304 | tf_op jit(solution)/shard_map/all_to_all | solution.py:39
  59.4 50.8 %all-to-all-done = bf16[64,8,2048]{2,1,0:T(8,128)(2,1)} async-done(((bf16[64,8,2048]{2,1,0:T(8,128)(2,1)}), bf16[64,8,2048]{2,1,0:T(8,128)(2,1)}, u32[]{:S(2)}, u32[]{:S(2)}) %all-to-all-start) | async-done | bytes 2097184 | tf_op jit(solution)/shard_map/all_to_all | solution.py:39
  122.2 5.6 all-to-all-start.1
  129.0 27.5 %all-to-all-done.1 = bf16[64,4,2048]{2,1,0:T(4,128)(2,1)} async-done(((bf16[64,4,2048]{2,1,0:T(4,128)(2,1)}), bf16[64,4,2048]{2,1,0:T(4,128)(2,1)}, u32[]{:S(2)}, u32[]{:S(2)}) %all-to-all-start.1) | async-done | bytes 1048608 | tf_op jit(solution)/shard_map/all_to_all | solution.py:39
  160.4 9.2 %collective-permute-done.5 = bf16[64,2048]{1,0:T(8,128)(2,1)S(1)} collective-permute-done((bf16[64,2048]{1,0:T(8,128)(2,1)S(1)}, bf16[64,2048]{1,0:T(8,128)(2,1)S(1)}, u32[]{:S(2)}, u32[]{:S(2)}) %collective-permute-start.5) | collective-permute-done | bytes 262176 | tf_op jit(solution)/shard_map/ppermute | solution.py:10
  173.4 6.6 all-to-all-start.2
  187.8 21.9 %collective-permute-done.6 = bf16[64,4,2048]{2,0,1:T(8,128)(2,1)} collective-permute-done((bf16[64,4,2048]{2,0,1:T(8,128)(2,1)}, bf16[64,4,2048]{2,0,1:T(8,128)(2,1)}, u32[]{:S(2)}, u32[]{:S(2)}) %collective-permute-start.6) | collective-permute-done | bytes 1048608 | tf_op jit(solution)/shard_map/ppermute | solution.py:10
  222.7 10.5 %all-to-all-start.3 = ((bf16[64,4,2048]{2,1,0:T(4,128)(2,1)}), bf16[64,4,2048]{2,1,0:T(4,128)(2,1)}, u32[]{:S(2)}, u32[]{:S(2)}) async-start(bf16[64,4,2048]{2,1,0:T(4,128)(2,1)} %copy.107), calls=%async_computation.3 | async-start | bytes 2097152 | tf_op jit(solution)/shard_map/all_to_all | solution.py:39
  234.8 27.1 %all-to-all-done.3 = bf16[64,4,2048]{2,1,0:T(4,128)(2,1)} async-done(((bf16[64,4,2048]{2,1,0:T(4,128)(2,1)}), bf16[64,4,2048]{2,1,0:T(4,128)(2,1)}, u32[]{:S(2)}, u32[]{:S(2)}) %all-to-all-start.3) | async-done | bytes 1048608 | tf_op jit(solution)/shard_map/all_to_all | solution.py:39
  265.7 8.7 %collective-permute-done.7 = bf16[64,2048]{1,0:T(8,128)(2,1)S(1)} collective-permute-done((bf16[64,2048]{1,0:T(8,128)(2,1)S(1)}, bf16[64,2048]{1,0:T(8,128)(2,1)S(1)}, u32[]{:S(2)}, u32[]{:S(2)}) %collective-permute-start.7) | collective-permute-done | bytes 262176 | tf_op jit(solution)/shard_map/ppermute | solution.py:10
  278.9 6.6 all-to-all-start.4
  292.9 22.0 %collective-permute-done.8 = bf16[64,4,2048]{2,0,1:T(8,128)(2,1)} collective-permute-done((bf16[64,4,2048]{2,0,1:T(8,128)(2,1)}, bf16[64,4,2048]{2,0,1:T(8,128)(2,1)}, u32[]{:S(2)}, u32[]{:S(2)}) %collective-permute-start.8) | collective-permute-done | bytes 1048608 | tf_op jit(solution)/shard_map/ppermute | solution.py:10
  328.2 10.5 %all-to-all-start.5 = ((bf16[64,4,2048]{2,1,0:T(4,128)(2,1)}), bf16[64,4,2048]{2,1,0:T(4,128)(2,1)}, u32[]{:S(2)}, u32[]{:S(2)}) async-start(bf16[64,4,2048]{2,1,0:T(4,128)(2,1)} %copy.115), calls=%async_computation.5 | async-start | bytes 2097152 | tf_op jit(solution)/shard_map/all_to_all | solution.py:39
  338.8 28.6 %all-to-all-done.5 = bf16[64,4,2048]{2,1,0:T(4,128)(2,1)} async-done(((bf16[64,4,2048]{2,1,0:T(4,128)(2,1)}), bf16[64,4,2048]{2,1,0:T(4,128)(2,1)}, u32[]{:S(2)}, u32[]{:S(2)}) %all-to-all-start.5) | async-done | bytes 1048608 | tf_op jit(solution)/shard_map/all_to_all | solution.py:39
  371.3 8.7 %collective-permute-done.9 = bf16[64,2048]{1,0:T(8,128)(2,1)S(1)} collective-permute-done((bf16[64,2048]{1,0:T(8,128)(2,1)S(1)}, bf16[64,2048]{1,0:T(8,128)(2,1)S(1)}, u32[]{:S(2)}, u32[]{:S(2)}) %collective-permute-start.9) | collective-permute-done | bytes 262176 | tf_op jit(solution)/shard_map/ppermute | solution.py:10
  384.4 7.0 %all-to-all-start.6 = ((bf16[64,4,2048]{2,1,0:T(4,128)(2,1)}), bf16[64,4,2048]{2,1,0:T(4,128)(2,1)}, u32[]{:S(2)}, u32[]{:S(2)}) async-start(bf16[64,4,2048]{2,1,0:T(4,128)(2,1)} %copy.119), calls=%async_computation.6 | async-start | bytes 2097152 | tf_op jit(solution)/shard_map/all_to_all | solution.py:39
  391.4 28.5 %all-to-all-done.6 = bf16[64,4,2048]{2,1,0:T(4,128)(2,1)} async-done(((bf16[64,4,2048]{2,1,0:T(4,128)(2,1)}), bf16[64,4,2048]{2,1,0:T(4,128)(2,1)}, u32[]{:S(2)}, u32[]{:S(2)}) %all-to-all-start.6) | async-done | bytes 1048608 | tf_op jit(solution)/shard_map/all_to_all | solution.py:39
  428.0 5.9 all-to-all-start.7
  434.0 28.6 %all-to-all-done.7 = bf16[64,4,2048]{2,1,0:T(4,128)(2,1)} async-done(((bf16[64,4,2048]{2,1,0:T(4,128)(2,1)}), bf16[64,4,2048]{2,1,0:T(4,128)(2,1)}, u32[]{:S(2)}, u32[]{:S(2)}) %all-to-all-start.7) | async-done | bytes 1048608 | tf_op jit(solution)/shard_map/all_to_all | solution.py:39
  466.5 7.7 %collective-permute-done.10 = bf16[64,2048]{1,0:T(8,128)(2,1)S(1)} collective-permute-done((bf16[64,2048]{1,0:T(8,128)(2,1)S(1)}, bf16[64,2048]{1,0:T(8,128)(2,1)S(1)}, u32[]{:S(2)}, u32[]{:S(2)}) %collective-permute-start.10) | collective-permute-done | bytes 262176 | tf_op jit(solution)/shard_map/ppermute | solution.py:10
  477.9 7.0 %all-to-all-start.8 = ((bf16[64,4,2048]{2,1,0:T(4,128)(2,1)}), bf16[64,4,2048]{2,1,0:T(4,128)(2,1)}, u32[]{:S(2)}, u32[]{:S(2)}) async-start(bf16[64,4,2048]{2,1,0:T(4,128)(2,1)} %copy.125), calls=%async_computation.8 | async-start | bytes 2097152 | tf_op jit(solution)/shard_map/all_to_all | solution.py:39
  484.9 28.5 %all-to-all-done.8 = bf16[64,4,2048]{2,1,0:T(4,128)(2,1)} async-done(((bf16[64,4,2048]{2,1,0:T(4,128)(2,1)}), bf16[64,4,2048]{2,1,0:T(4,128)(2,1)}, u32[]{:S(2)}, u32[]{:S(2)}) %all-to-all-start.8) | async-done | bytes 1048608 | tf_op jit(solution)/shard_map/all_to_all | solution.py:39
  521.5 5.9 all-to-all-start.9
  541.4 14.6 %all-to-all-done.9 = bf16[64,4,2048]{2,1,0:T(4,128)(2,1)} async-done(((bf16[64,4,2048]{2,1,0:T(4,128)(2,1)}), bf16[64,4,2048]{2,1,0:T(4,128)(2,1)}, u32[]{:S(2)}, u32[]{:S(2)}) %all-to-all-start.9) | async-done | bytes 1048608 | tf_op jit(solution)/shard_map/all_to_all | solution.py:39
  572.1 6.6 all-to-all-start.10
  592.0 15.4 %all-to-all-done.10 = bf16[64,4,2048]{2,1,0:T(4,128)(2,1)} async-done(((bf16[64,4,2048]{2,1,0:T(4,128)(2,1)}), bf16[64,4,2048]{2,1,0:T(4,128)(2,1)}, u32[]{:S(2)}, u32[]{:S(2)}) %all-to-all-start.10) | async-done | bytes 1048608 | tf_op jit(solution)/shard_map/all_to_all | solution.py:39
  615.6 5.9 all-to-all-start.11
  624.5 6.6 convolution_bitcast_fusion.1
  631.2 5.9 convolution_bitcast_fusion
  637.1 13.1 %all-to-all-done.11 = bf16[64,4,2048]{2,1,0:T(4,128)(2,1)} async-done(((bf16[64,4,2048]{2,1,0:T(4,128)(2,1)}), bf16[64,4,2048]{2,1,0:T(4,128)(2,1)}, u32[]{:S(2)}, u32[]{:S(2)}) %all-to-all-start.11) | async-done | bytes 1048608 | tf_op jit(solution)/shard_map/all_to_all | solution.py:39
  654.9 22.3 %reduce-scatter.2.cloned.1.call-done = bf16[3,64,512]{2,1,0:T(8,128)(2,1)} async-done(((bf16[3,64,2048]{2,1,0:T(8,128)(2,1)}), bf16[3,64,512]{2,1,0:T(8,128)(2,1)}) %reduce-scatter.2.cloned.1.call-update) | async-done | bytes 196624 | tf_op jit(solution)/shard_map/reduce_scatter | solution.py:178
  (192 shorter events, 197.0 us)
Async XLA Ops:
  7.2 108.7 %copy-start = (bf16[1,1,768,2048]{3,2,1,0:T(8,128)(2,1)S(1)}, bf16[1,1,768,2048]{3,2,1,0:T(8,128)(2,1)}, u32[]{:S(2)}) copy-start(bf16[1,1,768,2048]{3,2,1,0:T(8,128)(2,1)} %param.10) | copy-start | bytes 9437188
  7.2 30.9 %collective-permute-start = (bf16[3,64,512]{2,1,0:T(8,128)(2,1)}, bf16[3,64,512]{2,1,0:T(8,128)(2,1)}, u32[]{:S(2)}, u32[]{:S(2)}) collective-permute-start(bf16[3,64,512]{2,1,0:T(8,128)(2,1)} %param.11), channel_id=1, source_target_pairs={{0,192},{1,193},{2,194},{3,195},{4,196},{5,197},{6,198},{7,199},{8... | collective-permute-start | bytes 589832 | tf_op jit(solution)/shard_map/ppermute | solution.py:68
  12.8 26.2 %collective-permute-start.1 = (bf16[3,64,512]{2,1,0:T(8,128)(2,1)}, bf16[3,64,512]{2,1,0:T(8,128)(2,1)}, u32[]{:S(2)}, u32[]{:S(2)}) collective-permute-start(bf16[3,64,512]{2,1,0:T(8,128)(2,1)} %param.11), channel_id=1, source_target_pairs={{64,192},{65,193},{66,194},{67,195},{68,196},{69,197},{70,198},{71... | collective-permute-start | bytes 589832 | tf_op jit(solution)/shard_map/ppermute | solution.py:68
  14.1 25.8 %collective-permute-start.2 = (bf16[3,64,512]{2,1,0:T(8,128)(2,1)}, bf16[3,64,512]{2,1,0:T(8,128)(2,1)}, u32[]{:S(2)}, u32[]{:S(2)}) collective-permute-start(bf16[3,64,512]{2,1,0:T(8,128)(2,1)} %param.11), channel_id=1, source_target_pairs={{128,192},{129,193},{130,194},{131,195},{132,196},{133,197},{134,1... | collective-permute-start | bytes 589832 | tf_op jit(solution)/shard_map/ppermute | solution.py:68
  16.9 12.2 %collective-permute-start.3 = (s32[3,64,4]{2,1,0:T(8,128)}, s32[3,64,4]{2,1,0:T(8,128)}, u32[]{:S(2)}, u32[]{:S(2)}) collective-permute-start(s32[3,64,4]{2,1,0:T(8,128)} %bitcast.4), channel_id=1, source_target_pairs={{64,0},{128,64},{192,128},{65,1},{129,65},{193,129},{66,2},{130,66... | collective-permute-start | bytes 9224 | tf_op jit(solution)/shard_map/ppermute | solution.py:10
  18.2 22.8 %collective-permute-start.4 = (bf16[3,64,2048]{2,1,0:T(8,128)(2,1)}, bf16[3,64,2048]{2,1,0:T(8,128)(2,1)}, u32[]{:S(2)}, u32[]{:S(2)}) collective-permute-start(bf16[3,64,2048]{2,1,0:T(8,128)(2,1)} %bitcast.333), channel_id=1, source_target_pairs={{64,0},{128,64},{192,128},{65,1},{129,65},{193,129},{66,2},{130,66... | collective-permute-start | bytes 2359304 | tf_op jit(solution)/shard_map/ppermute | solution.py:10
  46.4 12.8 %copy-start.30 = (bf16[1,256,64]{1,2,0:T(8,128)(2,1)S(1)}, bf16[1,256,64]{1,2,0:T(8,128)(2,1)}, u32[]{:S(2)}) copy-start(bf16[1,256,64]{1,2,0:T(8,128)(2,1)} %get-tuple-element.28) | copy-start | bytes 98308
  46.4 63.7 %all-to-all-start = ((bf16[64,8,2048]{2,1,0:T(8,128)(2,1)}), bf16[64,8,2048]{2,1,0:T(8,128)(2,1)}, u32[]{:S(2)}, u32[]{:S(2)}) async-start(bf16[64,8,2048]{2,1,0:T(8,128)(2,1)} %copy.92), calls=%async_computation | async-start | bytes 4194304 | tf_op jit(solution)/shard_map/all_to_all | solution.py:39
  122.2 34.3 %all-to-all-start.1 = ((bf16[64,4,2048]{2,1,0:T(4,128)(2,1)}), bf16[64,4,2048]{2,1,0:T(4,128)(2,1)}, u32[]{:S(2)}, u32[]{:S(2)}) async-start(bf16[64,4,2048]{2,1,0:T(4,128)(2,1)} %copy.97), calls=%async_computation.1 | async-start | bytes 2097152 | tf_op jit(solution)/shard_map/all_to_all | solution.py:39
  159.1 10.4 %collective-permute-start.5 = (bf16[64,2048]{1,0:T(8,128)(2,1)S(1)}, bf16[64,2048]{1,0:T(8,128)(2,1)S(1)}, u32[]{:S(2)}, u32[]{:S(2)}) collective-permute-start(bf16[64,2048]{1,0:T(8,128)(2,1)S(1)} %fusion.57), channel_id=1, source_target_pairs={{64,0},{128,64},{192,128},{65,1},{129,65},{193,129},{66,2},{130,66... | collective-permute-start | bytes 786440 | tf_op jit(solution)/shard_map/ppermute | solution.py:10
  171.6 16.1 %copy-start.29 = (bf16[1,256,64]{1,2,0:T(8,128)(2,1)S(1)}, bf16[1,256,64]{1,2,0:T(8,128)(2,1)}, u32[]{:S(2)}) copy-start(bf16[1,256,64]{1,2,0:T(8,128)(2,1)} %get-tuple-element.25) | copy-start | bytes 98308
  173.4 36.3 %all-to-all-start.2 = ((bf16[64,4,2048]{2,1,0:T(4,128)(2,1)}), bf16[64,4,2048]{2,1,0:T(4,128)(2,1)}, u32[]{:S(2)}, u32[]{:S(2)}) async-start(bf16[64,4,2048]{2,1,0:T(4,128)(2,1)} %copy.104), calls=%async_computation.2 | async-start | bytes 2097152 | tf_op jit(solution)/shard_map/all_to_all | solution.py:39
  182.8 26.9 %collective-permute-start.6 = (bf16[64,4,2048]{2,0,1:T(8,128)(2,1)}, bf16[64,4,2048]{2,0,1:T(8,128)(2,1)}, u32[]{:S(2)}, u32[]{:S(2)}) collective-permute-start(bf16[64,4,2048]{2,0,1:T(8,128)(2,1)} %copy.142), channel_id=1, source_target_pairs={{0,64},{64,128},{128,192},{1,65},{65,129},{129,193},{2,66},{66,130... | collective-permute-start | bytes 3145736 | tf_op jit(solution)/shard_map/ppermute | solution.py:10
  220.9 54.3 %copy-start.16 = (f32[1,64,4,64]{3,2,1,0:T(4,128)S(1)}, f32[1,64,4,64]{3,2,1,0:T(4,128)}, u32[]{:S(2)}) copy-start(f32[1,64,4,64]{3,2,1,0:T(4,128)} %get-tuple-element.16) | copy-start | bytes 196612
  222.7 39.2 %all-to-all-start.3 = ((bf16[64,4,2048]{2,1,0:T(4,128)(2,1)}), bf16[64,4,2048]{2,1,0:T(4,128)(2,1)}, u32[]{:S(2)}, u32[]{:S(2)}) async-start(bf16[64,4,2048]{2,1,0:T(4,128)(2,1)} %copy.107), calls=%async_computation.3 | async-start | bytes 2097152 | tf_op jit(solution)/shard_map/all_to_all | solution.py:39
  264.5 10.0 %collective-permute-start.7 = (bf16[64,2048]{1,0:T(8,128)(2,1)S(1)}, bf16[64,2048]{1,0:T(8,128)(2,1)S(1)}, u32[]{:S(2)}, u32[]{:S(2)}) collective-permute-start(bf16[64,2048]{1,0:T(8,128)(2,1)S(1)} %add_convert_fusion.4), channel_id=1, source_target_pairs={{64,0},{128,64},{192,128},{65,1},{129,65},{193,129},{66,2},{130,66... | collective-permute-start | bytes 786440 | tf_op jit(solution)/shard_map/ppermute | solution.py:10
  278.9 41.1 %all-to-all-start.4 = ((bf16[64,4,2048]{2,1,0:T(4,128)(2,1)}), bf16[64,4,2048]{2,1,0:T(4,128)(2,1)}, u32[]{:S(2)}, u32[]{:S(2)}) async-start(bf16[64,4,2048]{2,1,0:T(4,128)(2,1)} %copy.111), calls=%async_computation.4 | async-start | bytes 2097152 | tf_op jit(solution)/shard_map/all_to_all | solution.py:39
  288.3 26.6 %collective-permute-start.8 = (bf16[64,4,2048]{2,0,1:T(8,128)(2,1)}, bf16[64,4,2048]{2,0,1:T(8,128)(2,1)}, u32[]{:S(2)}, u32[]{:S(2)}) collective-permute-start(bf16[64,4,2048]{2,0,1:T(8,128)(2,1)} %copy.98), channel_id=1, source_target_pairs={{0,64},{64,128},{128,192},{1,65},{65,129},{129,193},{2,66},{66,130... | collective-permute-start | bytes 3145736 | tf_op jit(solution)/shard_map/ppermute | solution.py:10
  326.4 54.3 %copy-start.15 = (f32[1,64,4,64]{3,2,1,0:T(4,128)S(1)}, f32[1,64,4,64]{3,2,1,0:T(4,128)}, u32[]{:S(2)}) copy-start(f32[1,64,4,64]{3,2,1,0:T(4,128)} %get-tuple-element.15) | copy-start | bytes 196612
  328.2 39.2 %all-to-all-start.5 = ((bf16[64,4,2048]{2,1,0:T(4,128)(2,1)}), bf16[64,4,2048]{2,1,0:T(4,128)(2,1)}, u32[]{:S(2)}, u32[]{:S(2)}) async-start(bf16[64,4,2048]{2,1,0:T(4,128)(2,1)} %copy.115), calls=%async_computation.5 | async-start | bytes 2097152 | tf_op jit(solution)/shard_map/all_to_all | solution.py:39
  370.0 10.0 %collective-permute-start.9 = (bf16[64,2048]{1,0:T(8,128)(2,1)S(1)}, bf16[64,2048]{1,0:T(8,128)(2,1)S(1)}, u32[]{:S(2)}, u32[]{:S(2)}) collective-permute-start(bf16[64,2048]{1,0:T(8,128)(2,1)S(1)} %add_convert_fusion.3), channel_id=1, source_target_pairs={{64,0},{128,64},{192,128},{65,1},{129,65},{193,129},{66,2},{130,66... | collective-permute-start | bytes 786440 | tf_op jit(solution)/shard_map/ppermute | solution.py:10
  384.4 35.5 %all-to-all-start.6 = ((bf16[64,4,2048]{2,1,0:T(4,128)(2,1)}), bf16[64,4,2048]{2,1,0:T(4,128)(2,1)}, u32[]{:S(2)}, u32[]{:S(2)}) async-start(bf16[64,4,2048]{2,1,0:T(4,128)(2,1)} %copy.119), calls=%async_computation.6 | async-start | bytes 2097152 | tf_op jit(solution)/shard_map/all_to_all | solution.py:39
  426.2 47.9 %copy-start.14 = (f32[1,64,4,64]{3,2,1,0:T(4,128)S(1)}, f32[1,64,4,64]{3,2,1,0:T(4,128)}, u32[]{:S(2)}) copy-start(f32[1,64,4,64]{3,2,1,0:T(4,128)} %get-tuple-element.14) | copy-start | bytes 196612
  428.0 34.6 %all-to-all-start.7 = ((bf16[64,4,2048]{2,1,0:T(4,128)(2,1)}), bf16[64,4,2048]{2,1,0:T(4,128)(2,1)}, u32[]{:S(2)}, u32[]{:S(2)}) async-start(bf16[64,4,2048]{2,1,0:T(4,128)(2,1)} %copy.121), calls=%async_computation.7 | async-start | bytes 2097152 | tf_op jit(solution)/shard_map/all_to_all | solution.py:39
  465.2 9.0 %collective-permute-start.10 = (bf16[64,2048]{1,0:T(8,128)(2,1)S(1)}, bf16[64,2048]{1,0:T(8,128)(2,1)S(1)}, u32[]{:S(2)}, u32[]{:S(2)}) collective-permute-start(bf16[64,2048]{1,0:T(8,128)(2,1)S(1)} %add_convert_fusion.2), channel_id=1, source_target_pairs={{64,0},{128,64},{192,128},{65,1},{129,65},{193,129},{66,2},{130,66... | collective-permute-start | bytes 786440 | tf_op jit(solution)/shard_map/ppermute | solution.py:10
  477.9 35.5 %all-to-all-start.8 = ((bf16[64,4,2048]{2,1,0:T(4,128)(2,1)}), bf16[64,4,2048]{2,1,0:T(4,128)(2,1)}, u32[]{:S(2)}, u32[]{:S(2)}) async-start(bf16[64,4,2048]{2,1,0:T(4,128)(2,1)} %copy.125), calls=%async_computation.8 | async-start | bytes 2097152 | tf_op jit(solution)/shard_map/all_to_all | solution.py:39
  521.5 34.6 %all-to-all-start.9 = ((bf16[64,4,2048]{2,1,0:T(4,128)(2,1)}), bf16[64,4,2048]{2,1,0:T(4,128)(2,1)}, u32[]{:S(2)}, u32[]{:S(2)}) async-start(bf16[64,4,2048]{2,1,0:T(4,128)(2,1)} %copy.127), calls=%async_computation.9 | async-start | bytes 2097152 | tf_op jit(solution)/shard_map/all_to_all | solution.py:39
  541.4 27.0 %copy-start.13 = (f32[1,64,4,64]{3,2,1,0:T(4,128)S(1)}, f32[1,64,4,64]{3,2,1,0:T(4,128)}, u32[]{:S(2)}) copy-start(f32[1,64,4,64]{3,2,1,0:T(4,128)} %get-tuple-element.13) | copy-start | bytes 196612
  558.7 9.0 %collective-permute-start.11 = (bf16[64,2048]{1,0:T(8,128)(2,1)S(1)}, bf16[64,2048]{1,0:T(8,128)(2,1)S(1)}, u32[]{:S(2)}, u32[]{:S(2)}) collective-permute-start(bf16[64,2048]{1,0:T(8,128)(2,1)S(1)} %add_convert_fusion.1), channel_id=1, source_target_pairs={{64,0},{128,64},{192,128},{65,1},{129,65},{193,129},{66,2},{130,66... | collective-permute-start | bytes 786440 | tf_op jit(solution)/shard_map/ppermute | solution.py:10
  572.1 35.3 %all-to-all-start.10 = ((bf16[64,4,2048]{2,1,0:T(4,128)(2,1)}), bf16[64,4,2048]{2,1,0:T(4,128)(2,1)}, u32[]{:S(2)}, u32[]{:S(2)}) async-start(bf16[64,4,2048]{2,1,0:T(4,128)(2,1)} %copy.131), calls=%async_computation.10 | async-start | bytes 2097152 | tf_op jit(solution)/shard_map/all_to_all | solution.py:39
  615.6 34.6 %all-to-all-start.11 = ((bf16[64,4,2048]{2,1,0:T(4,128)(2,1)}), bf16[64,4,2048]{2,1,0:T(4,128)(2,1)}, u32[]{:S(2)}, u32[]{:S(2)}) async-start(bf16[64,4,2048]{2,1,0:T(4,128)(2,1)} %copy.133), calls=%async_computation.11 | async-start | bytes 2097152 | tf_op jit(solution)/shard_map/all_to_all | solution.py:39
  621.5 55.6 %reduce-scatter.2.cloned.1.call-start = ((), (), s32[]{:S(2)}) async-start(), calls=%async_computation.13 | async-start | bytes 983040 | tf_op jit(solution)/shard_map/reduce_scatter | solution.py:178
  (30 other events, 151.4 us)
Sparse Core Ops, SparseCore 0:
  655.0 22.0 reduce-scatter.1

commit v8 on v7

--- a/solution.py
+++ b/solution.py
@@ -169,13 +169,17 @@
             pre_keep = lax.dynamic_update_slice_in_dim(pre_keep, pre_grad[None], keep_at, 0)
             grad_keep = lax.dynamic_update_slice_in_dim(grad_keep, grad_recv[None], keep_at, 0)
         if tick_no >= tick_count - micro_count:
-            final_rows.append(grad_out)
+            width_part = model_width // section_count
+            parts = [grad_out[:, number * width_part:(number + 1) * width_part] for number in range(section_count)]
+            landed = parts[0]
+            for number in range(1, section_count):
+                moved = lax.ppermute(parts[number], "pipe", [(0, number)])
+                landed = jnp.where(section_id == number, moved, landed)
+            final_rows.append(landed)
         if tick_no + 1 < tick_count:
             incoming = shifted(grad_out, "pipe", -1)
 
-    final_rows = jnp.stack(final_rows)
-    final_term = jnp.where(section_id == 0, final_rows, jnp.zeros_like(final_rows))
-    grad_in = lax.psum_scatter(final_term, "pipe", scatter_dimension=2, tiled=True)
+    grad_in = jnp.stack(final_rows)
     first_grad = first_sum.astype(jnp.bfloat16)
     second_grad = second_sum.astype(jnp.bfloat16)
     return (grad_in, first_grad[None, None], second_grad[None, None])

time: 692 us -> 665 us (0.961)
  waiting for transfers between devices: 367 us -> 330 us
  starting transfers between devices: 118 us -> 140 us
  between operations: 15 us -> 1.73 us
    reduce_scatter x1 -> x0, waiting for transfers between devices: 22.3 us -> none  [on_device(): lax.psum_scatter(final_term, 'pipe', scatter_dimension=2, tiled=True)]
    ppermute x0 -> x9, starting transfers between devices: none -> 20.6 us  [on_device(): moved = lax.ppermute(parts[number], 'pipe', [(0, number)])]
    all_to_all x12, waiting for transfers between devices: 263 us -> 247 us  [exchange(): lax.all_to_all(rows, 'expert', split_axis=0, concat_axis=0, tiled=True)]
  transfers between devices with their start and end apart: 25 -> 33, of which waited for: 18 -> 19; matrix products, arithmetic and copies ran while one was open for 12% -> 14% of each run, Pallas kernels for 0% -> 0%
where the time goes in v8:
time: 665 us; the launch traced here: 657 us
  waiting for transfers between devices  330 us (50%)
  starting transfers between devices  140 us (21%)
  matrix products  90.7 us (14%)
  local copies, waits for them, and re-layouts  73.8 us (11%)
  other arithmetic  20.3 us (3%)
    all_to_all x12, waiting for transfers between devices, exchange(): lax.all_to_all(rows, 'expert', split_axis=0, concat_axis=0, tiled=True)  247 us
    all_to_all x12, starting transfers between devices, exchange(): lax.all_to_all(rows, 'expert', split_axis=0, concat_axis=0, tiled=True)  92.5 us
    ppermute x9, waiting for transfers between devices, shifted(): lax.ppermute(value, axis, [(source, source + steps) for source in range(f...  81 us
    dot_general x6, matrix products, on_device(): jnp.einsum('pqd,fd->pqf', grad_recv, second_weights, preferred_element_ty...  28 us
    ppermute x9, starting transfers between devices, on_device(): moved = lax.ppermute(parts[number], 'pipe', [(0, number)])  20.6 us
    ppermute x9, starting transfers between devices, shifted(): lax.ppermute(value, axis, [(source, source + steps) for source in range(f...  19 us
    dot_general x6, matrix products, on_device(): jnp.einsum('pqk,pqd->kd', token_stack[micro_id], returned, preferred_elem...  15.6 us
    dynamic_update_slice x6, local copies, waits for them, and re-layouts, on_device(): lax.dynamic_update_slice_in_dim(grad_keep, grad_recv[None], keep_at, 0)  15.5 us
  transfers between devices with their start and end apart: 33, of which 19 were waited for; matrix products, arithmetic and copies ran while one was open for 14% of the time, Pallas kernels for 0%

profile of v8, /device:TPU:8, one launch (start us, length us, event | category | flops | bytes accessed | tf_op | source)
XLA Modules:
  0.0 656.6 jit_solution(11673292098116501640)
XLA Ops:
  2.1 5.4 collective-permute-start
  39.8 12.8 %all-to-all-start = ((bf16[64,8,2048]{2,1,0:T(8,128)(2,1)}), bf16[64,8,2048]{2,1,0:T(8,128)(2,1)}, u32[]{:S(2)}, u32[]{:S(2)}) async-start(bf16[64,8,2048]{2,1,0:T(8,128)(2,1)} %copy.92), calls=%async_computation | async-start | bytes 4194304 | tf_op jit(solution)/shard_map/all_to_all | solution.py:39
  52.7 50.8 %all-to-all-done = bf16[64,8,2048]{2,1,0:T(8,128)(2,1)} async-done(((bf16[64,8,2048]{2,1,0:T(8,128)(2,1)}), bf16[64,8,2048]{2,1,0:T(8,128)(2,1)}, u32[]{:S(2)}, u32[]{:S(2)}) %all-to-all-start) | async-done | bytes 2097184 | tf_op jit(solution)/shard_map/all_to_all | solution.py:39
  115.6 5.6 all-to-all-start.1
  122.4 27.5 %all-to-all-done.1 = bf16[64,4,2048]{2,1,0:T(4,128)(2,1)} async-done(((bf16[64,4,2048]{2,1,0:T(4,128)(2,1)}), bf16[64,4,2048]{2,1,0:T(4,128)(2,1)}, u32[]{:S(2)}, u32[]{:S(2)}) %all-to-all-start.1) | async-done | bytes 1048608 | tf_op jit(solution)/shard_map/all_to_all | solution.py:39
  153.7 9.2 %collective-permute-done.5 = bf16[64,2048]{1,0:T(8,128)(2,1)S(1)} collective-permute-done((bf16[64,2048]{1,0:T(8,128)(2,1)S(1)}, bf16[64,2048]{1,0:T(8,128)(2,1)S(1)}, u32[]{:S(2)}, u32[]{:S(2)}) %collective-permute-start.5) | collective-permute-done | bytes 262176 | tf_op jit(solution)/shard_map/ppermute | solution.py:10
  166.7 6.6 %all-to-all-start.2 = ((bf16[64,4,2048]{2,1,0:T(4,128)(2,1)}), bf16[64,4,2048]{2,1,0:T(4,128)(2,1)}, u32[]{:S(2)}, u32[]{:S(2)}) async-start(bf16[64,4,2048]{2,1,0:T(4,128)(2,1)} %copy.104), calls=%async_computation.2 | async-start | bytes 2097152 | tf_op jit(solution)/shard_map/all_to_all | solution.py:39
  181.2 21.9 %collective-permute-done.6 = bf16[64,4,2048]{2,0,1:T(8,128)(2,1)} collective-permute-done((bf16[64,4,2048]{2,0,1:T(8,128)(2,1)}, bf16[64,4,2048]{2,0,1:T(8,128)(2,1)}, u32[]{:S(2)}, u32[]{:S(2)}) %collective-permute-start.6) | collective-permute-done | bytes 1048608 | tf_op jit(solution)/shard_map/ppermute | solution.py:10
  216.1 10.5 %all-to-all-start.3 = ((bf16[64,4,2048]{2,1,0:T(4,128)(2,1)}), bf16[64,4,2048]{2,1,0:T(4,128)(2,1)}, u32[]{:S(2)}, u32[]{:S(2)}) async-start(bf16[64,4,2048]{2,1,0:T(4,128)(2,1)} %copy.107), calls=%async_computation.3 | async-start | bytes 2097152 | tf_op jit(solution)/shard_map/all_to_all | solution.py:39
  228.1 27.1 %all-to-all-done.3 = bf16[64,4,2048]{2,1,0:T(4,128)(2,1)} async-done(((bf16[64,4,2048]{2,1,0:T(4,128)(2,1)}), bf16[64,4,2048]{2,1,0:T(4,128)(2,1)}, u32[]{:S(2)}, u32[]{:S(2)}) %all-to-all-start.3) | async-done | bytes 1048608 | tf_op jit(solution)/shard_map/all_to_all | solution.py:39
  259.1 8.7 %collective-permute-done.7 = bf16[64,2048]{1,0:T(8,128)(2,1)S(1)} collective-permute-done((bf16[64,2048]{1,0:T(8,128)(2,1)S(1)}, bf16[64,2048]{1,0:T(8,128)(2,1)S(1)}, u32[]{:S(2)}, u32[]{:S(2)}) %collective-permute-start.7) | collective-permute-done | bytes 262176 | tf_op jit(solution)/shard_map/ppermute | solution.py:10
  272.2 6.6 %all-to-all-start.4 = ((bf16[64,4,2048]{2,1,0:T(4,128)(2,1)}), bf16[64,4,2048]{2,1,0:T(4,128)(2,1)}, u32[]{:S(2)}, u32[]{:S(2)}) async-start(bf16[64,4,2048]{2,1,0:T(4,128)(2,1)} %copy.111), calls=%async_computation.4 | async-start | bytes 2097152 | tf_op jit(solution)/shard_map/all_to_all | solution.py:39
  286.3 22.0 %collective-permute-done.8 = bf16[64,4,2048]{2,0,1:T(8,128)(2,1)} collective-permute-done((bf16[64,4,2048]{2,0,1:T(8,128)(2,1)}, bf16[64,4,2048]{2,0,1:T(8,128)(2,1)}, u32[]{:S(2)}, u32[]{:S(2)}) %collective-permute-start.8) | collective-permute-done | bytes 1048608 | tf_op jit(solution)/shard_map/ppermute | solution.py:10
  321.5 10.5 %all-to-all-start.5 = ((bf16[64,4,2048]{2,1,0:T(4,128)(2,1)}), bf16[64,4,2048]{2,1,0:T(4,128)(2,1)}, u32[]{:S(2)}, u32[]{:S(2)}) async-start(bf16[64,4,2048]{2,1,0:T(4,128)(2,1)} %copy.115), calls=%async_computation.5 | async-start | bytes 2097152 | tf_op jit(solution)/shard_map/all_to_all | solution.py:39
  332.1 28.6 %all-to-all-done.5 = bf16[64,4,2048]{2,1,0:T(4,128)(2,1)} async-done(((bf16[64,4,2048]{2,1,0:T(4,128)(2,1)}), bf16[64,4,2048]{2,1,0:T(4,128)(2,1)}, u32[]{:S(2)}, u32[]{:S(2)}) %all-to-all-start.5) | async-done | bytes 1048608 | tf_op jit(solution)/shard_map/all_to_all | solution.py:39
  364.5 8.7 %collective-permute-done.9 = bf16[64,2048]{1,0:T(8,128)(2,1)S(1)} collective-permute-done((bf16[64,2048]{1,0:T(8,128)(2,1)S(1)}, bf16[64,2048]{1,0:T(8,128)(2,1)S(1)}, u32[]{:S(2)}, u32[]{:S(2)}) %collective-permute-start.9) | collective-permute-done | bytes 262176 | tf_op jit(solution)/shard_map/ppermute | solution.py:10
  377.7 7.0 %all-to-all-start.6 = ((bf16[64,4,2048]{2,1,0:T(4,128)(2,1)}), bf16[64,4,2048]{2,1,0:T(4,128)(2,1)}, u32[]{:S(2)}, u32[]{:S(2)}) async-start(bf16[64,4,2048]{2,1,0:T(4,128)(2,1)} %copy.119), calls=%async_computation.6 | async-start | bytes 2097152 | tf_op jit(solution)/shard_map/all_to_all | solution.py:39
  384.7 28.5 %all-to-all-done.6 = bf16[64,4,2048]{2,1,0:T(4,128)(2,1)} async-done(((bf16[64,4,2048]{2,1,0:T(4,128)(2,1)}), bf16[64,4,2048]{2,1,0:T(4,128)(2,1)}, u32[]{:S(2)}, u32[]{:S(2)}) %all-to-all-start.6) | async-done | bytes 1048608 | tf_op jit(solution)/shard_map/all_to_all | solution.py:39
  413.1 5.3 bitcast_dynamic-update-slice_fusion.8
  421.3 5.9 all-to-all-start.7
  427.3 28.6 %all-to-all-done.7 = bf16[64,4,2048]{2,1,0:T(4,128)(2,1)} async-done(((bf16[64,4,2048]{2,1,0:T(4,128)(2,1)}), bf16[64,4,2048]{2,1,0:T(4,128)(2,1)}, u32[]{:S(2)}, u32[]{:S(2)}) %all-to-all-start.7) | async-done | bytes 1048608 | tf_op jit(solution)/shard_map/all_to_all | solution.py:39
  459.8 7.7 %collective-permute-done.13 = bf16[64,2048]{1,0:T(8,128)(2,1)S(1)} collective-permute-done((bf16[64,2048]{1,0:T(8,128)(2,1)S(1)}, bf16[64,2048]{1,0:T(8,128)(2,1)S(1)}, u32[]{:S(2)}, u32[]{:S(2)}) %collective-permute-start.13) | collective-permute-done | bytes 262176 | tf_op jit(solution)/shard_map/ppermute | solution.py:10
  471.8 7.0 %all-to-all-start.8 = ((bf16[64,4,2048]{2,1,0:T(4,128)(2,1)}), bf16[64,4,2048]{2,1,0:T(4,128)(2,1)}, u32[]{:S(2)}, u32[]{:S(2)}) async-start(bf16[64,4,2048]{2,1,0:T(4,128)(2,1)} %copy.125), calls=%async_computation.8 | async-start | bytes 2097152 | tf_op jit(solution)/shard_map/all_to_all | solution.py:39
  478.9 28.5 %all-to-all-done.8 = bf16[64,4,2048]{2,1,0:T(4,128)(2,1)} async-done(((bf16[64,4,2048]{2,1,0:T(4,128)(2,1)}), bf16[64,4,2048]{2,1,0:T(4,128)(2,1)}, u32[]{:S(2)}, u32[]{:S(2)}) %all-to-all-start.8) | async-done | bytes 1048608 | tf_op jit(solution)/shard_map/all_to_all | solution.py:39
  507.3 5.3 bitcast_dynamic-update-slice_fusion.7
  515.5 5.9 all-to-all-start.9
  539.0 11.0 %all-to-all-done.9 = bf16[64,4,2048]{2,1,0:T(4,128)(2,1)} async-done(((bf16[64,4,2048]{2,1,0:T(4,128)(2,1)}), bf16[64,4,2048]{2,1,0:T(4,128)(2,1)}, u32[]{:S(2)}, u32[]{:S(2)}) %all-to-all-start.9) | async-done | bytes 1048608 | tf_op jit(solution)/shard_map/all_to_all | solution.py:39
  565.6 6.6 %all-to-all-start.10 = ((bf16[64,4,2048]{2,1,0:T(4,128)(2,1)}), bf16[64,4,2048]{2,1,0:T(4,128)(2,1)}, u32[]{:S(2)}, u32[]{:S(2)}) async-start(bf16[64,4,2048]{2,1,0:T(4,128)(2,1)} %copy.131), calls=%async_computation.10 | async-start | bytes 2097152 | tf_op jit(solution)/shard_map/all_to_all | solution.py:39
  609.0 7.5 %all-to-all-start.11 = ((bf16[64,4,2048]{2,1,0:T(4,128)(2,1)}), bf16[64,4,2048]{2,1,0:T(4,128)(2,1)}, u32[]{:S(2)}, u32[]{:S(2)}) async-start(bf16[64,4,2048]{2,1,0:T(4,128)(2,1)} %copy.133), calls=%async_computation.11 | async-start | bytes 2097152 | tf_op jit(solution)/shard_map/all_to_all | solution.py:39
  619.3 6.7 %convolution_bitcast_fusion.1 = bf16[2048,768]{1,0:T(8,128)(2,1)} fusion(bf16[1,64,4,2048]{3,1,2,0:T(8,128)(2,1)} %fusion.119, bf16[1,64,4,2048]{3,1,2,0:T(8,128)(2,1)} %fusion.118, bf16[1,64,4,2048]{3,1,2,0:T(8,128)(2,1)} %bitcast.331, bf16[4,64,4,768]{3,1,2,0:T(8,128)(2,1)} %get-tuple-element.49), kind=kOutput, calls=%fused_computation.1 | convolution fusion | flops 2419064832 | bytes 7471104 | tf_op jit(solution)/shard_map/mpqd,mpqf->df/dot_general | solution.py:154
  626.0 5.9 convolution_bitcast_fusion
  631.9 13.1 %all-to-all-done.11 = bf16[64,4,2048]{2,1,0:T(4,128)(2,1)} async-done(((bf16[64,4,2048]{2,1,0:T(4,128)(2,1)}), bf16[64,4,2048]{2,1,0:T(4,128)(2,1)}, u32[]{:S(2)}, u32[]{:S(2)}) %all-to-all-start.11) | async-done | bytes 1048608 | tf_op jit(solution)/shard_map/all_to_all | solution.py:39
  (219 shorter events, 211.9 us)
Async XLA Ops:
  0.6 31.7 %collective-permute-start.1 = (bf16[3,64,512]{2,1,0:T(8,128)(2,1)}, bf16[3,64,512]{2,1,0:T(8,128)(2,1)}, u32[]{:S(2)}, u32[]{:S(2)}) collective-permute-start(bf16[3,64,512]{2,1,0:T(8,128)(2,1)} %param.11), channel_id=1, source_target_pairs={{64,192},{65,193},{66,194},{67,195},{68,196},{69,197},{70,198},{71... | collective-permute-start | bytes 589832 | tf_op jit(solution)/shard_map/ppermute | solution.py:68
  2.1 29.3 %collective-permute-start = (bf16[3,64,512]{2,1,0:T(8,128)(2,1)}, bf16[3,64,512]{2,1,0:T(8,128)(2,1)}, u32[]{:S(2)}, u32[]{:S(2)}) collective-permute-start(bf16[3,64,512]{2,1,0:T(8,128)(2,1)} %param.11), channel_id=1, source_target_pairs={{0,192},{1,193},{2,194},{3,195},{4,196},{5,197},{6,198},{7,199},{8... | collective-permute-start | bytes 589832 | tf_op jit(solution)/shard_map/ppermute | solution.py:68
  7.5 25.8 %collective-permute-start.2 = (bf16[3,64,512]{2,1,0:T(8,128)(2,1)}, bf16[3,64,512]{2,1,0:T(8,128)(2,1)}, u32[]{:S(2)}, u32[]{:S(2)}) collective-permute-start(bf16[3,64,512]{2,1,0:T(8,128)(2,1)} %param.11), channel_id=1, source_target_pairs={{128,192},{129,193},{130,194},{131,195},{132,196},{133,197},{134,1... | collective-permute-start | bytes 589832 | tf_op jit(solution)/shard_map/ppermute | solution.py:68
  10.3 12.2 %collective-permute-start.3 = (s32[3,64,4]{2,1,0:T(8,128)}, s32[3,64,4]{2,1,0:T(8,128)}, u32[]{:S(2)}, u32[]{:S(2)}) collective-permute-start(s32[3,64,4]{2,1,0:T(8,128)} %bitcast.4), channel_id=1, source_target_pairs={{64,0},{128,64},{192,128},{65,1},{129,65},{193,129},{66,2},{130,66... | collective-permute-start | bytes 9224 | tf_op jit(solution)/shard_map/ppermute | solution.py:10
  11.6 22.7 %collective-permute-start.4 = (bf16[3,64,2048]{2,1,0:T(8,128)(2,1)}, bf16[3,64,2048]{2,1,0:T(8,128)(2,1)}, u32[]{:S(2)}, u32[]{:S(2)}) collective-permute-start(bf16[3,64,2048]{2,1,0:T(8,128)(2,1)} %bitcast.335), channel_id=1, source_target_pairs={{64,0},{128,64},{192,128},{65,1},{129,65},{193,129},{66,2},{130,66... | collective-permute-start | bytes 2359304 | tf_op jit(solution)/shard_map/ppermute | solution.py:10
  39.8 63.7 %all-to-all-start = ((bf16[64,8,2048]{2,1,0:T(8,128)(2,1)}), bf16[64,8,2048]{2,1,0:T(8,128)(2,1)}, u32[]{:S(2)}, u32[]{:S(2)}) async-start(bf16[64,8,2048]{2,1,0:T(8,128)(2,1)} %copy.92), calls=%async_computation | async-start | bytes 4194304 | tf_op jit(solution)/shard_map/all_to_all | solution.py:39
  115.6 34.3 %all-to-all-start.1 = ((bf16[64,4,2048]{2,1,0:T(4,128)(2,1)}), bf16[64,4,2048]{2,1,0:T(4,128)(2,1)}, u32[]{:S(2)}, u32[]{:S(2)}) async-start(bf16[64,4,2048]{2,1,0:T(4,128)(2,1)} %copy.97), calls=%async_computation.1 | async-start | bytes 2097152 | tf_op jit(solution)/shard_map/all_to_all | solution.py:39
  152.4 10.4 %collective-permute-start.5 = (bf16[64,2048]{1,0:T(8,128)(2,1)S(1)}, bf16[64,2048]{1,0:T(8,128)(2,1)S(1)}, u32[]{:S(2)}, u32[]{:S(2)}) collective-permute-start(bf16[64,2048]{1,0:T(8,128)(2,1)S(1)} %fusion.57), channel_id=1, source_target_pairs={{64,0},{128,64},{192,128},{65,1},{129,65},{193,129},{66,2},{130,66... | collective-permute-start | bytes 786440 | tf_op jit(solution)/shard_map/ppermute | solution.py:10
  166.7 36.3 %all-to-all-start.2 = ((bf16[64,4,2048]{2,1,0:T(4,128)(2,1)}), bf16[64,4,2048]{2,1,0:T(4,128)(2,1)}, u32[]{:S(2)}, u32[]{:S(2)}) async-start(bf16[64,4,2048]{2,1,0:T(4,128)(2,1)} %copy.104), calls=%async_computation.2 | async-start | bytes 2097152 | tf_op jit(solution)/shard_map/all_to_all | solution.py:39
  176.1 26.9 %collective-permute-start.6 = (bf16[64,4,2048]{2,0,1:T(8,128)(2,1)}, bf16[64,4,2048]{2,0,1:T(8,128)(2,1)}, u32[]{:S(2)}, u32[]{:S(2)}) collective-permute-start(bf16[64,4,2048]{2,0,1:T(8,128)(2,1)} %copy.142), channel_id=1, source_target_pairs={{0,64},{64,128},{128,192},{1,65},{65,129},{129,193},{2,66},{66,130... | collective-permute-start | bytes 3145736 | tf_op jit(solution)/shard_map/ppermute | solution.py:10
  216.1 39.2 %all-to-all-start.3 = ((bf16[64,4,2048]{2,1,0:T(4,128)(2,1)}), bf16[64,4,2048]{2,1,0:T(4,128)(2,1)}, u32[]{:S(2)}, u32[]{:S(2)}) async-start(bf16[64,4,2048]{2,1,0:T(4,128)(2,1)} %copy.107), calls=%async_computation.3 | async-start | bytes 2097152 | tf_op jit(solution)/shard_map/all_to_all | solution.py:39
  257.8 10.0 %collective-permute-start.7 = (bf16[64,2048]{1,0:T(8,128)(2,1)S(1)}, bf16[64,2048]{1,0:T(8,128)(2,1)S(1)}, u32[]{:S(2)}, u32[]{:S(2)}) collective-permute-start(bf16[64,2048]{1,0:T(8,128)(2,1)S(1)} %add_convert_fusion.4), channel_id=1, source_target_pairs={{64,0},{128,64},{192,128},{65,1},{129,65},{193,129},{66,2},{130,66... | collective-permute-start | bytes 786440 | tf_op jit(solution)/shard_map/ppermute | solution.py:10
  272.2 41.1 %all-to-all-start.4 = ((bf16[64,4,2048]{2,1,0:T(4,128)(2,1)}), bf16[64,4,2048]{2,1,0:T(4,128)(2,1)}, u32[]{:S(2)}, u32[]{:S(2)}) async-start(bf16[64,4,2048]{2,1,0:T(4,128)(2,1)} %copy.111), calls=%async_computation.4 | async-start | bytes 2097152 | tf_op jit(solution)/shard_map/all_to_all | solution.py:39
  281.6 26.6 %collective-permute-start.8 = (bf16[64,4,2048]{2,0,1:T(8,128)(2,1)}, bf16[64,4,2048]{2,0,1:T(8,128)(2,1)}, u32[]{:S(2)}, u32[]{:S(2)}) collective-permute-start(bf16[64,4,2048]{2,0,1:T(8,128)(2,1)} %copy.98), channel_id=1, source_target_pairs={{0,64},{64,128},{128,192},{1,65},{65,129},{129,193},{2,66},{66,130... | collective-permute-start | bytes 3145736 | tf_op jit(solution)/shard_map/ppermute | solution.py:10
  321.5 39.2 %all-to-all-start.5 = ((bf16[64,4,2048]{2,1,0:T(4,128)(2,1)}), bf16[64,4,2048]{2,1,0:T(4,128)(2,1)}, u32[]{:S(2)}, u32[]{:S(2)}) async-start(bf16[64,4,2048]{2,1,0:T(4,128)(2,1)} %copy.115), calls=%async_computation.5 | async-start | bytes 2097152 | tf_op jit(solution)/shard_map/all_to_all | solution.py:39
  363.2 10.0 %collective-permute-start.9 = (bf16[64,2048]{1,0:T(8,128)(2,1)S(1)}, bf16[64,2048]{1,0:T(8,128)(2,1)S(1)}, u32[]{:S(2)}, u32[]{:S(2)}) collective-permute-start(bf16[64,2048]{1,0:T(8,128)(2,1)S(1)} %add_convert_fusion.3), channel_id=1, source_target_pairs={{64,0},{128,64},{192,128},{65,1},{129,65},{193,129},{66,2},{130,66... | collective-permute-start | bytes 786440 | tf_op jit(solution)/shard_map/ppermute | solution.py:10
  377.7 35.5 %all-to-all-start.6 = ((bf16[64,4,2048]{2,1,0:T(4,128)(2,1)}), bf16[64,4,2048]{2,1,0:T(4,128)(2,1)}, u32[]{:S(2)}, u32[]{:S(2)}) async-start(bf16[64,4,2048]{2,1,0:T(4,128)(2,1)} %copy.119), calls=%async_computation.6 | async-start | bytes 2097152 | tf_op jit(solution)/shard_map/all_to_all | solution.py:39
  421.3 34.6 %all-to-all-start.7 = ((bf16[64,4,2048]{2,1,0:T(4,128)(2,1)}), bf16[64,4,2048]{2,1,0:T(4,128)(2,1)}, u32[]{:S(2)}, u32[]{:S(2)}) async-start(bf16[64,4,2048]{2,1,0:T(4,128)(2,1)} %copy.121), calls=%async_computation.7 | async-start | bytes 2097152 | tf_op jit(solution)/shard_map/all_to_all | solution.py:39
  458.5 9.0 %collective-permute-start.13 = (bf16[64,2048]{1,0:T(8,128)(2,1)S(1)}, bf16[64,2048]{1,0:T(8,128)(2,1)S(1)}, u32[]{:S(2)}, u32[]{:S(2)}) collective-permute-start(bf16[64,2048]{1,0:T(8,128)(2,1)S(1)} %add_convert_fusion.2), channel_id=1, source_target_pairs={{64,0},{128,64},{192,128},{65,1},{129,65},{193,129},{66,2},{130,66... | collective-permute-start | bytes 786440 | tf_op jit(solution)/shard_map/ppermute | solution.py:10
  471.8 35.5 %all-to-all-start.8 = ((bf16[64,4,2048]{2,1,0:T(4,128)(2,1)}), bf16[64,4,2048]{2,1,0:T(4,128)(2,1)}, u32[]{:S(2)}, u32[]{:S(2)}) async-start(bf16[64,4,2048]{2,1,0:T(4,128)(2,1)} %copy.125), calls=%async_computation.8 | async-start | bytes 2097152 | tf_op jit(solution)/shard_map/all_to_all | solution.py:39
  515.5 34.6 %all-to-all-start.9 = ((bf16[64,4,2048]{2,1,0:T(4,128)(2,1)}), bf16[64,4,2048]{2,1,0:T(4,128)(2,1)}, u32[]{:S(2)}, u32[]{:S(2)}) async-start(bf16[64,4,2048]{2,1,0:T(4,128)(2,1)} %copy.127), calls=%async_computation.9 | async-start | bytes 2097152 | tf_op jit(solution)/shard_map/all_to_all | solution.py:39
  552.8 9.0 %collective-permute-start.17 = (bf16[64,2048]{1,0:T(8,128)(2,1)S(1)}, bf16[64,2048]{1,0:T(8,128)(2,1)S(1)}, u32[]{:S(2)}, u32[]{:S(2)}) collective-permute-start(bf16[64,2048]{1,0:T(8,128)(2,1)S(1)} %add_convert_fusion.1), channel_id=1, source_target_pairs={{64,0},{128,64},{192,128},{65,1},{129,65},{193,129},{66,2},{130,66... | collective-permute-start | bytes 786440 | tf_op jit(solution)/shard_map/ppermute | solution.py:10
  565.6 35.3 %all-to-all-start.10 = ((bf16[64,4,2048]{2,1,0:T(4,128)(2,1)}), bf16[64,4,2048]{2,1,0:T(4,128)(2,1)}, u32[]{:S(2)}, u32[]{:S(2)}) async-start(bf16[64,4,2048]{2,1,0:T(4,128)(2,1)} %copy.131), calls=%async_computation.10 | async-start | bytes 2097152 | tf_op jit(solution)/shard_map/all_to_all | solution.py:39
  575.9 10.2 %collective-permute-start.12 = (bf16[64,512]{1,0:T(8,128)(2,1)S(1)}, bf16[64,512]{1,0:T(8,128)(2,1)S(1)}, u32[]{:S(2)}, u32[]{:S(2)}) collective-permute-start(bf16[64,512]{1,0:T(8,128)(2,1)S(1)} %get-tuple-element.19), channel_id=1, source_target_pairs={{0,64},{1,65},{2,66},{3,67},{4,68},{5,69},{6,70},{7,71},{8,72},{9,... | collective-permute-start | bytes 196616 | tf_op jit(solution)/shard_map/ppermute | solution.py:176
  579.5 6.5 collective-permute-start.11
  582.0 4.1 collective-permute-start.10
  590.4 62.1 %collective-permute-start.16 = (bf16[64,512]{1,0:T(8,128)(2,1)}, bf16[64,512]{1,0:T(8,128)(2,1)S(1)}, u32[]{:S(2)}, u32[]{:S(2)}) collective-permute-start(bf16[64,512]{1,0:T(8,128)(2,1)} %get-tuple-element.22), channel_id=1, source_target_pairs={{0,64},{1,65},{2,66},{3,67},{4,68},{5,69},{6,70},{7,71},{8,72},{9,... | collective-permute-start | bytes 196616 | tf_op jit(solution)/shard_map/ppermute | solution.py:176
  591.7 62.2 %collective-permute-start.15 = (bf16[64,512]{1,0:T(8,128)(2,1)}, bf16[64,512]{1,0:T(8,128)(2,1)}, u32[]{:S(2)}, u32[]{:S(2)}) collective-permute-start(bf16[64,512]{1,0:T(8,128)(2,1)} %get-tuple-element.23), channel_id=1, source_target_pairs={{0,128},{1,129},{2,130},{3,131},{4,132},{5,133},{6,134},{7,135},{8... | collective-permute-start | bytes 196616 | tf_op jit(solution)/shard_map/ppermute | solution.py:176
  595.2 58.6 %collective-permute-start.14 = (bf16[64,512]{1,0:T(8,128)(2,1)}, bf16[64,512]{1,0:T(8,128)(2,1)}, u32[]{:S(2)}, u32[]{:S(2)}) collective-permute-start(bf16[64,512]{1,0:T(8,128)(2,1)} %get-tuple-element.24), channel_id=1, source_target_pairs={{0,192},{1,193},{2,194},{3,195},{4,196},{5,197},{6,198},{7,199},{8... | collective-permute-start | bytes 196616 | tf_op jit(solution)/shard_map/ppermute | solution.py:176
  609.0 36.0 %all-to-all-start.11 = ((bf16[64,4,2048]{2,1,0:T(4,128)(2,1)}), bf16[64,4,2048]{2,1,0:T(4,128)(2,1)}, u32[]{:S(2)}, u32[]{:S(2)}) async-start(bf16[64,4,2048]{2,1,0:T(4,128)(2,1)} %copy.133), calls=%async_computation.11 | async-start | bytes 2097152 | tf_op jit(solution)/shard_map/all_to_all | solution.py:39
  647.7 6.2 collective-permute-start.20
  650.0 4.3 collective-permute-start.19
  (41 other events, 477.8 us)
